TPU v7x, 128 devices: a whole 4x4x4 slice. The times are simulated.
128 devices in a mesh: gx: 16 (over x_hi, z, core), gy: 8 (over x_lo, y).
Axes of the slice: x: 4 (x_hi: 2, x_lo: 2; x = x_hi * 2 + x_lo), y: 4, z: 4, core: 2. Of those that a mesh axis runs over, the one named last changes fastest.
Arguments:
- wavefunctions: float32 [192, 36864], P('gx', 'gy'), may hold values from -6 to 6
- potential: float32 [192, 576], P('gx', 'gy'), may hold values from -1 to 1
- cell_matrix: float32 [343, 343], replicated, may hold values from -0.08639188 to 1.4863919, as said below
- pair_cell: int32 [128, 256], P(('gx', 'gy')), may hold values from 0 to 3, as said below
- pair_tile: float32 [128, 256, 18, 343], P(('gx', 'gy')), may hold values from -0.2159797 to 0.2159797, as said below
- slot_atom: int32 [128, 256], P(('gx', 'gy')), may hold values from 0 to 63, as said below
- coupling: float32 [8192, 18, 18], P(('gx', 'gy')), may hold values from -0.28 to 0.28, as said below
- bounds: float32 [2, 3], replicated, may hold values from -2.5 to 15, as said below
Outputs:
- filtered: float32 [192, 36864], P('gx', 'gy')
Inputs may be any that keep to these rules, and one draw needn't show every extreme that they name: `pair_cell`: slots d * 2 to d * 2 + 1 of a device go to owner d; each slot is live or padded, and a padded slot has cell 0. Some owner receives 2 live slots from every device in every draw. `slot_atom`: entry [d, s * 2 + k] names the atom on owner d of slot d * 2 + k of device s; padded slots name 0. `pair_tile`: padded slots hold all-zero tiles. `coupling`: each matrix is symmetric. `cell_matrix`: Symmetric. `bounds`: each row rises: lowest estimate, then lower end, then upper end.
All inputs are finite; a program needn't handle non-finite values.
Results may differ from a plain program's by a relative error of at most 0.0001.
Values sent between devices are 32-bit elements; how exact they have to be, the bound alone decides.
No kernel may reach another device: no remote copies, remote signals or barrier semaphores. Data moves between devices by JAX's collectives and lax.ppermute only.
A program may use at most 128 MiB of HBM per device.

v0:
```python
import jax
import jax.numpy as jnp
from jax import lax
from jax.sharding import PartitionSpec as P

DEG = 6
W = 64
CX = 2
CY = 1
CZ = 2
FILTERS = 2
ZN = 12


PRECISE = lax.Precision.HIGHEST


def shifted(value, axis, steps):
    count = lax.axis_size(axis)
    pairs = [(source, (source + steps) % count) for source in range(count)]
    return lax.ppermute(value, axis, pairs)


def split_lead(values, number):
    trailing = values.shape[1:]
    leading_part = values[: number * DEG].reshape((number, DEG) + trailing)
    upper_part = values[DEG::DEG][:, None]
    return jnp.concatenate([leading_part, upper_part], axis=1)


def join_lead(values):
    number = values.shape[0]
    trailing = values.shape[2:]
    leading_part = values[:, :DEG].reshape((number * DEG,) + trailing)
    leading_part = jnp.concatenate([leading_part, jnp.zeros((1,) + trailing, jnp.float32)], axis=0)
    upper_part = jnp.zeros((number + 1, DEG) + trailing, jnp.float32).at[1:, 0].set(values[:, DEG])
    upper_part = upper_part.reshape(((number + 1) * DEG,) + trailing)[: number * DEG + 1]
    return leading_part + upper_part


def gather_cells(extended, cells_x, cells_y, cells_z):
    closed = jnp.concatenate([extended, extended[:, :, :1]], axis=2)
    layered = split_lead(closed, cells_x)
    layered = split_lead(jnp.moveaxis(layered, 2, 0), cells_y)
    layered = split_lead(jnp.moveaxis(layered, 4, 0), cells_z)
    layered = layered.transpose(5, 3, 1, 4, 2, 0, 6)
    return layered.reshape((DEG + 1) ** 3, cells_x * cells_y * cells_z, layered.shape[-1])


def scatter_cells(cell_out, cells_x, cells_y, cells_z):
    columns = cell_out.shape[-1]
    layered = cell_out.reshape(DEG + 1, DEG + 1, DEG + 1, cells_x, cells_y, cells_z, columns)
    layered = layered.transpose(5, 2, 4, 1, 3, 0, 6)
    layered = join_lead(layered)
    layered = layered[:-1].at[0].add(layered[-1])
    layered = join_lead(jnp.moveaxis(layered, 0, 4))
    layered = join_lead(jnp.moveaxis(layered, 0, 3))
    return layered.transpose(0, 2, 1, 3)


def body(wavefunctions, potential, cell_matrix, pair_cell, pair_tile, slot_atom, coupling, bounds):
    rows_x = wavefunctions.shape[0]
    rows_y = potential.shape[1] // ZN
    local_pot = potential.reshape(rows_x, rows_y, ZN, 1)
    cell_index = pair_cell[0]
    tile_set = pair_tile[0]
    atom_index = slot_atom[0]
    one_hot = (
        atom_index[:, None] == jnp.arange(coupling.shape[0], dtype=jnp.int32)[None, :]
    ).astype(jnp.float32)

    def owner_work(received):
        atom_sums = jnp.einsum("pws,sa->pwa", received, one_hot, precision=PRECISE)
        applied = jnp.einsum("apq,qwa->pwa", coupling, atom_sums, precision=PRECISE)
        return jnp.einsum("pwa,sa->pws", applied, one_hot, precision=PRECISE)

    def owner_reply(received):
        return lax.all_to_all(
            owner_work(received), ("gx", "gy"), split_axis=2, concat_axis=2, tiled=True
        )

    def apply_operator(current):
        flattened = current.reshape(rows_x, rows_y * ZN * W)
        face_in = shifted(flattened[:1], "gx", -1)
        extended = jnp.concatenate([current, face_in.reshape(1, rows_y, ZN, W)], axis=0)
        side_plane = extended[:, :1].reshape(rows_x + 1, ZN * W)
        side_in = shifted(side_plane, "gy", -1)
        extended = jnp.concatenate([extended, side_in.reshape(rows_x + 1, 1, ZN, W)], axis=1)
        cell_in = gather_cells(extended, CX, CY, CZ)
        kinetic = jnp.dot(
            cell_matrix, cell_in.reshape(cell_in.shape[0], -1), precision=PRECISE
        ).reshape(cell_in.shape)
        picked = jnp.take(cell_in, cell_index, axis=1)
        projected = jnp.einsum("spn,nsw->pws", tile_set, picked, precision=PRECISE)
        returned = owner_reply(
            lax.all_to_all(projected, ("gx", "gy"), split_axis=2, concat_axis=2, tiled=True)
        )
        spread = jnp.einsum("spn,pws->nsw", tile_set, returned, precision=PRECISE)
        cell_out = kinetic.at[:, cell_index].add(spread)
        summed = scatter_cells(cell_out, CX, CY, CZ)
        upper_plane = summed[:, rows_y].reshape(rows_x + 1, ZN * W)
        arrived = shifted(upper_plane, "gy", 1)
        summed = summed[:, :rows_y].at[:, 0].add(arrived.reshape(rows_x + 1, ZN, W))
        edge_plane = summed[rows_x].reshape(1, rows_y * ZN * W)
        arrived_x = shifted(edge_plane, "gx", 1)
        summed = summed[:rows_x].at[0].add(arrived_x.reshape(rows_y, ZN, W))
        return summed + local_pot * current

    previous = wavefunctions.reshape(rows_x, rows_y, ZN, W)
    for filter_index in range(FILTERS):
        lower_bound = bounds[filter_index, 0]
        low_end = bounds[filter_index, 1]
        high_end = bounds[filter_index, 2]
        half_width = (high_end - low_end) / 2.0
        centre = (high_end + low_end) / 2.0
        sigma_now = half_width / (lower_bound - centre)
        gamma_term = 2.0 / sigma_now
        current = sigma_now / half_width * (apply_operator(previous) - centre * previous)
        sigma_next = 1.0 / (gamma_term - sigma_now)
        following = (
            2.0 * sigma_next / half_width * (apply_operator(current) - centre * current)
            - sigma_now * sigma_next * previous
        )
        current = following
        sigma_now = sigma_next
        previous = current
    return previous.reshape(rows_x, rows_y * ZN * W)


def solution(mesh):
    placed = (
        P("gx", "gy"),
        P("gx", "gy"),
        P(),
        P(("gx", "gy"), None),
        P(("gx", "gy"), None, None, None),
        P(("gx", "gy"), None),
        P(("gx", "gy"), None, None),
        P(),
    )
    return jax.shard_map(body, mesh=mesh, in_specs=placed, out_specs=P("gx", "gy"), check_vma=False)
```

profile of v0, /device:TPU:0, one launch (start us, length us, event | category | flops | bytes accessed | tf_op | source)
XLA Modules:
  0.0 958.3 jit_solution(16720854148485877923)
XLA Ops:
  1.0 6.1 collective-permute-start
  13.0 14.1 %copy.333 = f32[1,256,18,343]{3,2,1,0:T(8,128)} copy(f32[1,256,18,343]{1,0,3,2:T(1,128)} %param.62) | data formatting | bytes 12644352 | tf_op jit(solution)/shard_map/squeeze | solution.py:66
  29.8 10.5 %gather_fusion = f32[256,343,64]{1,2,0:T(8,128)} fusion(f32[343,4,64]{0,2,1:T(8,128)S(1)} %copy.226, s32[1024]{0:T(1024)S(1)} %pad_clamp_fusion), kind=kCustom, calls=%fused_computation.clone | custom fusion | bytes 44958720 | tf_op jit(solution)/shard_map/jit(_take)/gather | solution.py:93
  40.2 33.3 %fusion.145 = f32[256,18,64]{2,1,0:T(8,128)} fusion(f32[1,256,18,343]{3,2,1,0:T(8,128)} %copy.333, f32[256,343,64]{1,2,0:T(8,128)} %gather_fusion, pred[256]{0:T(512)(128)(4,1)S(1)} %compare_and_fusion), kind=kOutput, calls=%fused_computation.194 | convolution fusion | flops 1219477504 | bytes 29980928 | tf_op jit(solution)/shard_map/spn,nsw->pws/dot_general | solution.py:94
  77.5 7.0 all-to-all-start
  84.9 19.6 %all-to-all-done = f32[128,1,2304]{2,1,0:T(1,128)} async-done(((f32[128,1,2304]{2,1,0:T(1,128)}), f32[128,1,2304]{2,1,0:T(1,128)}, u32[]{:S(2)}, u32[]{:S(2)}) %all-to-all-start) | async-done | bytes 1179680 | tf_op jit(solution)/shard_map/all_to_all | solution.py:96
  132.3 6.1 all-to-all-start.1
  139.9 18.6 %all-to-all-done.1 = f32[128,1,2304]{2,1,0:T(1,128)} async-done(((f32[128,1,2304]{2,1,0:T(1,128)}), f32[128,1,2304]{2,1,0:T(1,128)}, u32[]{:S(2)}, u32[]{:S(2)}) %all-to-all-start.1) | async-done | bytes 1179680 | tf_op jit(solution)/shard_map/all_to_all | solution.py:78
  165.4 25.4 %fusion.32 = f32[256,343,64]{1,2,0:T(8,128)} fusion(f32[1,256,18,343]{3,2,1,0:T(8,128)} %copy.333, f32[256,18,64]{2,1,0:T(8,128)} %reshape.1424), kind=kOutput, calls=%fused_computation.40 | convolution fusion | flops 1213857792 | bytes 29980672 | tf_op jit(solution)/shard_map/spn,pws->nsw/dot_general | solution.py:98
  190.8 40.4 %scatter_fusion = f32[343,4,64]{0,2,1:T(8,128)S(1)} fusion(f32[343,4,64]{0,2,1:T(8,128)S(1)} %bitcast.343, s32[256]{0:T(256)S(1)} %bitcast.414, f32[256,343,64]{1,2,0:T(8,128)} %fusion.32), kind=kCustom, calls=%fused_computation.4 | custom fusion | flops 5619712 | bytes 67437568 | tf_op jit(solution)/shard_map/scatter-add | solution.py:99
  264.4 10.5 %gather_fusion.1 = f32[256,343,64]{1,2,0:T(8,128)} fusion(f32[343,4,64]{0,2,1:T(8,128)S(1)} %copy.253, s32[1024]{0:T(1024)S(1)} %pad_clamp_fusion), kind=kCustom, calls=%fused_computation.1.clone | custom fusion | bytes 44958720 | tf_op jit(solution)/shard_map/jit(_take)/gather | solution.py:93
  274.9 33.5 %fusion.140 = f32[256,18,64]{2,1,0:T(8,128)} fusion(f32[1,256,18,343]{3,2,1,0:T(8,128)} %copy.333, f32[256,343,64]{1,2,0:T(8,128)} %gather_fusion.1, pred[256]{0:T(512)(128)(4,1)S(1)} %compare_and_fusion), kind=kOutput, calls=%fused_computation.193 | convolution fusion | flops 1219477504 | bytes 29980928 | tf_op jit(solution)/shard_map/spn,nsw->pws/dot_general | solution.py:94
  312.4 28.5 %all_to_all.40 = f32[128,1,2304]{2,1,0:T(1,128)} all-to-all(f32[128,1,2304]{2,1,0:T(1,128)} %reshape.1425), channel_id=1, replica_groups=mesh['gx'=16,'gy'=8] {'gx','gy'}, dimensions={0} | all-to-all | bytes 2359296 | tf_op jit(solution)/shard_map/all_to_all | solution.py:96
  374.6 17.5 %all-to-all-done.3 = f32[128,1,2304]{2,1,0:T(1,128)} async-done(((f32[128,1,2304]{2,1,0:T(1,128)}), f32[128,1,2304]{2,1,0:T(1,128)}, u32[]{:S(2)}, u32[]{:S(2)}) %all-to-all-start.3) | async-done | bytes 1179680 | tf_op jit(solution)/shard_map/all_to_all | solution.py:78
  401.2 25.4 %fusion.35 = f32[256,343,64]{1,2,0:T(8,128)} fusion(f32[1,256,18,343]{3,2,1,0:T(8,128)} %copy.333, f32[256,18,64]{2,1,0:T(8,128)} %reshape.1428), kind=kOutput, calls=%fused_computation.41 | convolution fusion | flops 1213857792 | bytes 29980672 | tf_op jit(solution)/shard_map/spn,pws->nsw/dot_general | solution.py:98
  426.6 40.5 %scatter_fusion.1 = f32[343,4,64]{0,2,1:T(8,128)S(1)} fusion(f32[343,4,64]{0,2,1:T(8,128)S(1)} %bitcast.344, s32[256]{0:T(256)S(1)} %bitcast.415, f32[256,343,64]{1,2,0:T(8,128)} %fusion.35), kind=kCustom, calls=%fused_computation.5 | custom fusion | flops 5619712 | bytes 67437568 | tf_op jit(solution)/shard_map/scatter-add | solution.py:99
  501.6 10.5 %gather_fusion.2 = f32[256,343,64]{1,2,0:T(8,128)} fusion(f32[343,4,64]{0,2,1:T(8,128)S(1)} %copy.280, s32[1024]{0:T(1024)S(1)} %pad_clamp_fusion), kind=kCustom, calls=%fused_computation.2.clone | custom fusion | bytes 44958720 | tf_op jit(solution)/shard_map/jit(_take)/gather | solution.py:93
  512.1 33.7 %fusion.135 = f32[256,18,64]{2,1,0:T(8,128)} fusion(f32[1,256,18,343]{3,2,1,0:T(8,128)} %copy.333, f32[256,343,64]{1,2,0:T(8,128)} %gather_fusion.2, pred[256]{0:T(512)(128)(4,1)S(1)} %compare_and_fusion), kind=kOutput, calls=%fused_computation.192 | convolution fusion | flops 1219477504 | bytes 29980928 | tf_op jit(solution)/shard_map/spn,nsw->pws/dot_general | solution.py:94
  549.7 28.3 %all_to_all.41 = f32[128,1,2304]{2,1,0:T(1,128)} all-to-all(f32[128,1,2304]{2,1,0:T(1,128)} %reshape.1429), channel_id=1, replica_groups=mesh['gx'=16,'gy'=8] {'gx','gy'}, dimensions={0} | all-to-all | bytes 2359296 | tf_op jit(solution)/shard_map/all_to_all | solution.py:96
  605.2 5.9 all-to-all-start.5
  612.6 18.6 %all-to-all-done.5 = f32[128,1,2304]{2,1,0:T(1,128)} async-done(((f32[128,1,2304]{2,1,0:T(1,128)}), f32[128,1,2304]{2,1,0:T(1,128)}, u32[]{:S(2)}, u32[]{:S(2)}) %all-to-all-start.5) | async-done | bytes 1179680 | tf_op jit(solution)/shard_map/all_to_all | solution.py:78
  638.1 25.4 %fusion.38 = f32[256,343,64]{1,2,0:T(8,128)} fusion(f32[1,256,18,343]{3,2,1,0:T(8,128)} %copy.333, f32[256,18,64]{2,1,0:T(8,128)} %reshape.1432), kind=kOutput, calls=%fused_computation.42 | convolution fusion | flops 1213857792 | bytes 29980672 | tf_op jit(solution)/shard_map/spn,pws->nsw/dot_general | solution.py:98
  663.5 40.7 %scatter_fusion.2 = f32[343,4,64]{0,2,1:T(8,128)S(1)} fusion(f32[343,4,64]{0,2,1:T(8,128)S(1)} %bitcast.345, s32[256]{0:T(256)S(1)} %bitcast.416, f32[256,343,64]{1,2,0:T(8,128)} %fusion.38), kind=kCustom, calls=%fused_computation.6 | custom fusion | flops 5619712 | bytes 67437568 | tf_op jit(solution)/shard_map/scatter-add | solution.py:99
  736.8 10.5 %gather_fusion.3 = f32[256,343,64]{1,2,0:T(8,128)} fusion(f32[343,4,64]{0,2,1:T(8,128)S(1)} %copy.307, s32[1024]{0:T(1024)S(1)} %pad_clamp_fusion), kind=kCustom, calls=%fused_computation.3.clone | custom fusion | bytes 44958720 | tf_op jit(solution)/shard_map/jit(_take)/gather | solution.py:93
  747.2 33.5 %fusion.130 = f32[256,18,64]{2,1,0:T(8,128)} fusion(f32[1,256,18,343]{3,2,1,0:T(8,128)} %copy.333, f32[256,343,64]{1,2,0:T(8,128)} %gather_fusion.3, pred[256]{0:T(512)(128)(4,1)S(1)} %compare_and_fusion), kind=kOutput, calls=%fused_computation.191 | convolution fusion | flops 1219477504 | bytes 29980928 | tf_op jit(solution)/shard_map/spn,nsw->pws/dot_general | solution.py:94
  784.6 28.4 %all_to_all.42 = f32[128,1,2304]{2,1,0:T(1,128)} all-to-all(f32[128,1,2304]{2,1,0:T(1,128)} %reshape.1433), channel_id=1, replica_groups=mesh['gx'=16,'gy'=8] {'gx','gy'}, dimensions={0} | all-to-all | bytes 2359296 | tf_op jit(solution)/shard_map/all_to_all | solution.py:96
  838.3 5.9 all-to-all-start.7
  845.7 18.6 %all-to-all-done.7 = f32[128,1,2304]{2,1,0:T(1,128)} async-done(((f32[128,1,2304]{2,1,0:T(1,128)}), f32[128,1,2304]{2,1,0:T(1,128)}, u32[]{:S(2)}, u32[]{:S(2)}) %all-to-all-start.7) | async-done | bytes 1179680 | tf_op jit(solution)/shard_map/all_to_all | solution.py:78
  873.3 25.4 %fusion.41 = f32[256,343,64]{1,2,0:T(8,128)} fusion(f32[1,256,18,343]{3,2,1,0:T(8,128)} %copy.333, f32[256,18,64]{2,1,0:T(8,128)} %reshape.1436), kind=kOutput, calls=%fused_computation.43 | convolution fusion | flops 1213857792 | bytes 29980672 | tf_op jit(solution)/shard_map/spn,pws->nsw/dot_general | solution.py:98
  898.7 40.6 %scatter_fusion.3 = f32[343,4,64]{0,2,1:T(8,128)S(1)} fusion(f32[343,4,64]{0,2,1:T(8,128)S(1)} %bitcast.342, s32[256]{0:T(256)S(1)} %bitcast.417, f32[256,343,64]{1,2,0:T(8,128)} %fusion.41), kind=kCustom, calls=%fused_computation.7 | custom fusion | flops 5619712 | bytes 67437568 | tf_op jit(solution)/shard_map/scatter-add | solution.py:99
  942.5 6.1 collective-permute-done.14
  949.1 6.6 collective-permute-done.15
  (335 shorter events, 273.5 us)
Async XLA Ops:
  0.0 138.9 %copy-start = (f32[343,343]{1,0:T(8,128)S(1)}, f32[343,343]{1,0:T(8,128)}, u32[]{:S(2)}) copy-start(f32[343,343]{1,0:T(8,128)} %param.60) | copy-start | bytes 1411792
  1.0 8.7 collective-permute-start
  9.9 17.3 %collective-permute-start.1 = (f32[13,768]{1,0:T(8,128)S(1)}, f32[13,768]{1,0:T(8,128)S(1)}, u32[]{:S(2)}, u32[]{:S(2)}) collective-permute-start(f32[13,768]{1,0:T(8,128)S(1)} %reshape.1268), channel_id=1, source_target_pairs={{0,7},{1,0},{2,1},{3,2},{4,3},{5,4},{6,5},{7,6},{8,15},{9,8},{10,9... | collective-permute-start | bytes 119816 | tf_op jit(solution)/shard_map/ppermute | solution.py:21
  73.6 10.9 %copy-start.4 = (f32[64,18,18]{0,2,1:T(8,128)S(1)}, f32[64,18,18]{0,2,1:T(8,128)}, u32[]{:S(2)}) copy-start(f32[64,18,18]{0,2,1:T(8,128)} %param.64) | copy-start | bytes 248836
  73.6 40.4 %copy-start.5 = (s32[1,256]{1,0:T(1,128)S(1)}, s32[1,256]{1,0:T(1,128)}, u32[]{:S(2)}) copy-start(s32[1,256]{1,0:T(1,128)} %param.63) | copy-start | bytes 3076
  77.5 27.0 %all-to-all-start = ((f32[128,1,2304]{2,1,0:T(1,128)}), f32[128,1,2304]{2,1,0:T(1,128)}, u32[]{:S(2)}, u32[]{:S(2)}) async-start(f32[128,1,2304]{2,1,0:T(1,128)} %reshape.1421), calls=%async_computation | async-start | bytes 2359296 | tf_op jit(solution)/shard_map/all_to_all | solution.py:96
  123.5 14.9 %copy-start.8 = (s32[1,256]{1,0:T(1,128)S(1)}, s32[1,256]{1,0:T(1,128)}, u32[]{:S(2)}) copy-start(s32[1,256]{1,0:T(1,128)} %param.61) | copy-start | bytes 3076
  132.3 26.2 %all-to-all-start.1 = ((f32[128,1,2304]{2,1,0:T(1,128)}), f32[128,1,2304]{2,1,0:T(1,128)}, u32[]{:S(2)}, u32[]{:S(2)}) async-start(f32[128,1,2304]{2,1,0:T(1,128)} %reshape.1423), calls=%async_computation.1 | async-start | bytes 2359296 | tf_op jit(solution)/shard_map/all_to_all | solution.py:78
  232.9 9.4 copy-start.6
  233.0 12.5 %copy-start.7 = (f32[12,72]{1,0:T(8,128)S(1)}, f32[12,72]{1,0:T(8,128)}, u32[]{:S(2)}) copy-start(f32[12,72]{1,0:T(8,128)} %param.59) | copy-start | bytes 10372
  234.3 6.3 collective-permute-start.2
  242.3 6.9 collective-permute-start.3
  245.5 477.5 %copy-start.3 = (f32[12,6,12]{2,1,0:T(8,128)}, f32[12,6,12]{2,1,0:T(8,128)S(1)}, u32[]{:S(2)}) copy-start(f32[12,6,12]{2,1,0:T(8,128)S(1)} %mul.102) | copy-start | bytes 10372
  250.4 5.1 collective-permute-start.4
  255.7 4.2 collective-permute-start.5
  366.2 25.9 %all-to-all-start.3 = ((f32[128,1,2304]{2,1,0:T(1,128)}), f32[128,1,2304]{2,1,0:T(1,128)}, u32[]{:S(2)}, u32[]{:S(2)}) async-start(f32[128,1,2304]{2,1,0:T(1,128)} %reshape.1427), calls=%async_computation.3 | async-start | bytes 2359296 | tf_op jit(solution)/shard_map/all_to_all | solution.py:78
  472.8 0.9 copy-start.2
  473.7 6.3 collective-permute-start.6
  482.6 6.9 collective-permute-start.7
  492.4 2.2 collective-permute-start.8
  494.9 4.2 collective-permute-start.9
  605.2 26.0 %all-to-all-start.5 = ((f32[128,1,2304]{2,1,0:T(1,128)}), f32[128,1,2304]{2,1,0:T(1,128)}, u32[]{:S(2)}, u32[]{:S(2)}) async-start(f32[128,1,2304]{2,1,0:T(1,128)} %reshape.1431), calls=%async_computation.5 | async-start | bytes 2359296 | tf_op jit(solution)/shard_map/all_to_all | solution.py:78
  707.3 6.3 collective-permute-start.10
  715.2 6.9 collective-permute-start.11
  723.3 4.5 collective-permute-start.12
  728.0 4.2 collective-permute-start.13
  829.5 14.8 %copy-start.1 = (f32[7,7,7,2,1,2,64]{6,5,3,2,1,0,4:T(2,128)S(1)}, f32[7,7,7,2,1,2,64]{6,5,3,2,1,0,4:T(2,128)}, u32[]{:S(2)}) copy-start(f32[7,7,7,2,1,2,64]{6,5,3,2,1,0,4:T(2,128)} %copy.304) | copy-start | bytes 1053700
  838.3 26.0 %all-to-all-start.7 = ((f32[128,1,2304]{2,1,0:T(1,128)}), f32[128,1,2304]{2,1,0:T(1,128)}, u32[]{:S(2)}, u32[]{:S(2)}) async-start(f32[128,1,2304]{2,1,0:T(1,128)} %reshape.1435), calls=%async_computation.7 | async-start | bytes 2359296 | tf_op jit(solution)/shard_map/all_to_all | solution.py:78
  942.4 6.3 collective-permute-start.14
  948.8 6.9 collective-permute-start.15
where the time goes:
time: 973 us; the launch traced here: 958 us
  matrix products  273 us (28%)
  other arithmetic  223 us (23%)
  local copies, waits for them, and re-layouts  174 us (18%)
  waiting for transfers between devices  146 us (15%)
  blocking collectives  85.2 us (9%)
  starting transfers between devices  48.2 us (5%)
    scatter-add x4, other arithmetic, apply_operator(): cell_out = kinetic.at[:, cell_index].add(spread)  162 us
    dot_general x4, matrix products, apply_operator(): projected = jnp.einsum('spn,nsw->pws', tile_set, picked, precision=PRECISE)  134 us
    dot_general x4, matrix products, apply_operator(): spread = jnp.einsum('spn,pws->nsw', tile_set, returned, precision=PRECISE)  102 us
    all_to_all x3, blocking collectives, apply_operator(): lax.all_to_all(projected, ('gx', 'gy'), split_axis=2, concat_axis=2, tile...  85.2 us
    all_to_all x4, waiting for transfers between devices, owner_reply(): lax.all_to_all(owner_work(received), ('gx', 'gy'), split_axis=2, concat_a...  73.2 us
    unnamed x48, local copies, waits for them, and re-layouts  56.6 us
    ppermute x16, waiting for transfers between devices, shifted(): return lax.ppermute(value, axis, pairs)  53.1 us
    gather x4, local copies, waits for them, and re-layouts, apply_operator(): picked = jnp.take(cell_in, cell_index, axis=1)  41.9 us
  transfers between devices with their start and end apart: 21, of which 19 were waited for; matrix products, arithmetic and copies ran while one was open for 3% of the time, Pallas kernels for 0%

commit v1 on v0

v1 whole, which is shorter than its diff:
```python
import jax
import jax.numpy as jnp
from jax import lax
from jax.sharding import PartitionSpec as P

DEG = 6
W = 64
CX = 2
CY = 1
CZ = 2
FILTERS = 2
ZN = 12


PRECISE = lax.Precision.HIGHEST


def shifted(value, axis, steps):
    count = lax.axis_size(axis)
    pairs = [(source, (source + steps) % count) for source in range(count)]
    return lax.ppermute(value, axis, pairs)


def cell_ranges():
    for p in range(CX):
        for q in range(CY):
            for r in range(CZ):
                yield p * DEG, q * DEG, r * DEG


def gather_cells(extended):
    closed = jnp.concatenate([extended, extended[:, :, :1]], axis=2)
    blocks = [
        closed[x0 : x0 + DEG + 1, y0 : y0 + DEG + 1, z0 : z0 + DEG + 1]
        for x0, y0, z0 in cell_ranges()
    ]
    stacked = jnp.stack(blocks, axis=3)
    return stacked.reshape((DEG + 1) ** 3, len(blocks) * stacked.shape[-1])


def scatter_cells(cell_out, columns):
    cells = cell_out.shape[1] // columns
    blocks = cell_out.reshape(DEG + 1, DEG + 1, DEG + 1, cells, columns)
    nx, ny, nz = CX * DEG + 1, CY * DEG + 1, CZ * DEG + 1
    total = None
    for index, (x0, y0, z0) in enumerate(cell_ranges()):
        padded = jnp.pad(
            blocks[:, :, :, index],
            ((x0, nx - x0 - DEG - 1), (y0, ny - y0 - DEG - 1), (z0, nz - z0 - DEG - 1), (0, 0)),
        )
        total = padded if total is None else total + padded
    return total[:, :, :ZN].at[:, :, 0].add(total[:, :, ZN])


def body(wavefunctions, potential, cell_matrix, pair_cell, pair_tile, slot_atom, coupling, bounds):
    rows_x = wavefunctions.shape[0]
    rows_y = potential.shape[1] // ZN
    slots, nproj, npc = pair_tile.shape[1:]
    atoms = coupling.shape[0]
    cells = CX * CY * CZ
    owners = lax.axis_size(("gx", "gy"))
    local_pot = potential.reshape(rows_x, rows_y, ZN, 1)
    tile_flat = pair_tile[0].reshape(slots * nproj, npc)
    cell_mask = (pair_cell[0][:, None] == jnp.arange(cells, dtype=jnp.int32)[None, :]).astype(jnp.float32)
    row_mask = jnp.repeat(cell_mask, nproj, axis=0)[:, :, None]
    one_hot = (
        slot_atom[0][:, None] == jnp.arange(atoms, dtype=jnp.int32)[None, :]
    ).astype(jnp.float32)

    def exchange(values):
        return lax.all_to_all(values, ("gx", "gy"), split_axis=0, concat_axis=0, tiled=True)

    def owner_work(received):
        atom_sums = lax.dot_general(
            one_hot, received, (((0,), (0,)), ((), ())), precision=PRECISE
        ).reshape(atoms, nproj, W)
        applied = jnp.einsum("apq,aqw->apw", coupling, atom_sums, precision=PRECISE)
        return jnp.dot(one_hot, applied.reshape(atoms, nproj * W), precision=PRECISE)

    def apply_operator(current):
        face_in = shifted(current[:1], "gx", -1)
        extended = jnp.concatenate([current, face_in], axis=0)
        side_in = shifted(extended[:, :1], "gy", -1)
        extended = jnp.concatenate([extended, side_in], axis=1)
        cell_in = gather_cells(extended)
        every_cell = jnp.dot(tile_flat, cell_in, precision=PRECISE)
        projected = (every_cell.reshape(slots * nproj, cells, W) * row_mask).sum(axis=1)
        received = exchange(projected.reshape(owners, -1)).reshape(slots, nproj * W)
        returned = exchange(owner_work(received).reshape(owners, -1))
        spread_in = (returned.reshape(slots * nproj, 1, W) * row_mask).reshape(slots * nproj, cells * W)
        kinetic = jnp.dot(cell_matrix, cell_in, precision=PRECISE)
        spread = lax.dot_general(
            tile_flat, spread_in, (((0,), (0,)), ((), ())), precision=PRECISE
        )
        summed = scatter_cells(kinetic + spread, W)
        arrived = shifted(summed[:, rows_y], "gy", 1)
        summed = summed[:, :rows_y].at[:, 0].add(arrived)
        arrived_x = shifted(summed[rows_x], "gx", 1)
        summed = summed[:rows_x].at[0].add(arrived_x)
        return summed + local_pot * current

    previous = wavefunctions.reshape(rows_x, rows_y, ZN, W)
    for filter_index in range(FILTERS):
        lower_bound = bounds[filter_index, 0]
        low_end = bounds[filter_index, 1]
        high_end = bounds[filter_index, 2]
        half_width = (high_end - low_end) / 2.0
        centre = (high_end + low_end) / 2.0
        sigma_now = half_width / (lower_bound - centre)
        gamma_term = 2.0 / sigma_now
        current = sigma_now / half_width * (apply_operator(previous) - centre * previous)
        sigma_next = 1.0 / (gamma_term - sigma_now)
        following = (
            2.0 * sigma_next / half_width * (apply_operator(current) - centre * current)
            - sigma_now * sigma_next * previous
        )
        current = following
        sigma_now = sigma_next
        previous = current
    return previous.reshape(rows_x, rows_y * ZN * W)


def solution(mesh):
    placed = (
        P("gx", "gy"),
        P("gx", "gy"),
        P(),
        P(("gx", "gy"), None),
        P(("gx", "gy"), None, None, None),
        P(("gx", "gy"), None),
        P(("gx", "gy"), None, None),
        P(),
    )
    return jax.shard_map(body, mesh=mesh, in_specs=placed, out_specs=P("gx", "gy"), check_vma=False)
```

time: 973 us -> 664 us (0.68)
  other arithmetic: 223 us -> 60.5 us
  matrix products: 273 us -> 139 us
  blocking collectives: 85.2 us -> 191 us
  waiting for transfers between devices: 146 us -> 81.3 us
  starting transfers between devices: 48.2 us -> 23.6 us
  local copies, waits for them, and re-layouts: 174 us -> 150 us
    scatter-add x16 -> x8, other arithmetic: 168 us -> 4.3 us  [the longest x4 2.43 us: apply_operator(): summed = summed[:rows_x].at[0].add(arrived_x)]
    dot_general x24, matrix products: 273 us -> 139 us  [the longest x4 56.1 us: apply_operator(): every_cell = jnp.dot(tile_flat, cell_in, precision=PRECISE)]
    all_to_all x3 -> x7, blocking collectives: 85.2 us -> 191 us  [exchange(): lax.all_to_all(values, ('gx', 'gy'), split_axis=0, concat_axis=0, tiled=T...]
    all_to_all x5 -> x1, waiting for transfers between devices: 92.9 us -> 19.1 us  [exchange(): lax.all_to_all(values, ('gx', 'gy'), split_axis=0, concat_axis=0, tiled=T...]
    gather x4 -> x0, local copies, waits for them, and re-layouts: 41.9 us -> none  [apply_operator(): picked = jnp.take(cell_in, cell_index, axis=1)]
    unnamed x48 -> x37, local copies, waits for them, and re-layouts: 56.6 us -> 18 us
    all_to_all x1 -> x8, local copies, waits for them, and re-layouts: 0.58 us -> 26.6 us  [exchange(): lax.all_to_all(values, ('gx', 'gy'), split_axis=0, concat_axis=0, tiled=T...]
    all_to_all x5 -> x1, starting transfers between devices: 30.8 us -> 7.85 us  [exchange(): lax.all_to_all(values, ('gx', 'gy'), split_axis=0, concat_axis=0, tiled=T...]
  transfers between devices with their start and end apart: 21 -> 17, of which waited for: 19 -> 16; matrix products, arithmetic and copies ran while one was open for 3% -> 5% of each run, Pallas kernels for 0% -> 0%
where the time goes in v1:
time: 664 us; the launch traced here: 653 us
  blocking collectives  191 us (29%)
  local copies, waits for them, and re-layouts  150 us (23%)
  matrix products  139 us (21%)
  waiting for transfers between devices  81.3 us (12%)
  other arithmetic  60.5 us (9%)
  starting transfers between devices  23.6 us (4%)
  between operations  7.94 us (1%)
    all_to_all x7, blocking collectives, exchange(): lax.all_to_all(values, ('gx', 'gy'), split_axis=0, concat_axis=0, tiled=T...  191 us
    ppermute x16, waiting for transfers between devices, shifted(): return lax.ppermute(value, axis, pairs)  62.2 us
    dot_general x4, matrix products, apply_operator(): every_cell = jnp.dot(tile_flat, cell_in, precision=PRECISE)  56.1 us
    dot_general x4, matrix products, apply_operator(): lax.dot_general(tile_flat, spread_in, (((0,), (0,)), ((), ())), precision...  53.5 us
    all_to_all x8, other arithmetic, exchange(): lax.all_to_all(values, ('gx', 'gy'), split_axis=0, concat_axis=0, tiled=T...  38.9 us
    all_to_all x8, local copies, waits for them, and re-layouts, exchange(): lax.all_to_all(values, ('gx', 'gy'), split_axis=0, concat_axis=0, tiled=T...  26.6 us
    mul x8, local copies, waits for them, and re-layouts, apply_operator(): returned.reshape(slots * nproj, 1, W) * row_mask  21 us
    all_to_all x1, waiting for transfers between devices, exchange(): lax.all_to_all(values, ('gx', 'gy'), split_axis=0, concat_axis=0, tiled=T...  19.1 us
  transfers between devices with their start and end apart: 17, of which 16 were waited for; matrix products, arithmetic and copies ran while one was open for 5% of the time, Pallas kernels for 0%

profile of v1, /device:TPU:0, one launch (start us, length us, event | category | flops | bytes accessed | tf_op | source)
XLA Modules:
  0.0 652.6 jit_solution(6363149003020926955)
XLA Ops:
  1.1 6.1 collective-permute-start
  12.1 14.0 %copy.139 = f32[1,256,18,343]{3,2,1,0:T(8,128)} copy(f32[1,256,18,343]{1,0,3,2:T(1,128)} %param.36) | data formatting | bytes 12644352 | tf_op args[4]
  26.0 9.2 %reshape_squeeze.3 = f32[4608,343]{1,0:T(8,128)} reshape(f32[1,256,18,343]{3,2,1,0:T(8,128)} %copy.139) | data formatting | bytes 12644352 | tf_op jit(solution)/shard_map/reshape;squeeze | solution.py:63
  36.7 14.0 %fusion.58 = f32[256,4608]{1,0:T(8,128)S(1)} fusion(f32[343,256]{1,0:T(8,128)S(1)} %reshape.599, f32[4608,343]{1,0:T(8,128)} %reshape_squeeze.3), kind=kOutput, calls=%fused_computation.155 | convolution fusion | flops 4855431168 | bytes 11392000 | tf_op jit(solution)/shard_map/dot_general | solution.py:86
  56.8 7.9 %all-to-all-start = ((f32[128,1,2304]{2,1,0:T(1,128)}), f32[128,1,2304]{2,1,0:T(1,128)S(1)}, u32[]{:S(2)}, u32[]{:S(2)}) async-start(f32[128,1,2304]{2,1,0:T(1,128)} %all_to_all.64), calls=%async_computation | async-start | bytes 2359296 | tf_op jit(solution)/shard_map/all_to_all | solution.py:71
  65.9 19.1 %all-to-all-done = f32[128,1,2304]{2,1,0:T(1,128)S(1)} async-done(((f32[128,1,2304]{2,1,0:T(1,128)}), f32[128,1,2304]{2,1,0:T(1,128)S(1)}, u32[]{:S(2)}, u32[]{:S(2)}) %all-to-all-start) | async-done | bytes 1179680 | tf_op jit(solution)/shard_map/all_to_all | solution.py:71
  102.7 26.4 %all_to_all.80 = f32[128,1,2304]{2,1,0:T(1,128)} all-to-all(f32[128,1,2304]{2,1,0:T(1,128)} %all_to_all.65), channel_id=1, replica_groups=mesh['gx'=16,'gy'=8] {'gx','gy'}, dimensions={0} | all-to-all | bytes 2359296 | tf_op jit(solution)/shard_map/all_to_all | solution.py:71
  137.7 13.4 %fusion.59 = f32[256,343]{0,1:T(8,128)S(1)} fusion(f32[4608,256]{0,1:T(8,128)S(1)} %bitcast.227, f32[4608,343]{1,0:T(8,128)} %reshape_squeeze.3), kind=kOutput, calls=%fused_computation.156 | convolution fusion | flops 4855431168 | bytes 11392000 | tf_op jit(solution)/shard_map/dot_general | solution.py:92
  155.9 6.7 %collective-permute-done.2 = f32[13,12,64]{2,1,0:T(8,128)S(1)} collective-permute-done((f32[13,12,64]{2,1,0:T(8,128)S(1)}, f32[13,12,64]{2,1,0:T(8,128)S(1)}, u32[]{:S(2)}, u32[]{:S(2)}) %collective-permute-start.2) | collective-permute-done | bytes 39968 | tf_op jit(solution)/shard_map/ppermute | solution.py:21
  184.4 14.0 %fusion.60 = f32[256,4608]{1,0:T(8,128)S(1)} fusion(f32[343,256]{1,0:T(8,128)S(1)} %reshape.606, f32[4608,343]{1,0:T(8,128)} %reshape_squeeze.3), kind=kOutput, calls=%fused_computation.157 | convolution fusion | flops 4855431168 | bytes 11392000 | tf_op jit(solution)/shard_map/dot_general | solution.py:86
  206.5 28.4 %all_to_all.81 = f32[128,1,2304]{2,1,0:T(1,128)} all-to-all(f32[128,1,2304]{2,1,0:T(1,128)} %all_to_all.66), channel_id=1, replica_groups=mesh['gx'=16,'gy'=8] {'gx','gy'}, dimensions={0} | all-to-all | bytes 2359296 | tf_op jit(solution)/shard_map/all_to_all | solution.py:71
  234.9 5.1 reduce.27
  256.4 26.4 %all_to_all.82 = f32[128,1,2304]{2,1,0:T(1,128)} all-to-all(f32[128,1,2304]{2,1,0:T(1,128)} %all_to_all.67), channel_id=1, replica_groups=mesh['gx'=16,'gy'=8] {'gx','gy'}, dimensions={0} | all-to-all | bytes 2359296 | tf_op jit(solution)/shard_map/all_to_all | solution.py:71
  282.7 5.1 reduce.28
  295.4 13.4 %fusion.61 = f32[256,343]{0,1:T(8,128)S(1)} fusion(f32[4608,256]{0,1:T(8,128)S(1)} %bitcast.228, f32[4608,343]{1,0:T(8,128)} %reshape_squeeze.3), kind=kOutput, calls=%fused_computation.158 | convolution fusion | flops 4855431168 | bytes 11392000 | tf_op jit(solution)/shard_map/dot_general | solution.py:92
  319.5 5.6 collective-permute-done.6
  328.2 5.8 collective-permute-done.7
  344.5 14.0 %fusion.62 = f32[256,4608]{1,0:T(8,128)S(1)} fusion(f32[343,256]{1,0:T(8,128)S(1)} %reshape.613, f32[4608,343]{1,0:T(8,128)} %reshape_squeeze.3), kind=kOutput, calls=%fused_computation.159 | convolution fusion | flops 4855431168 | bytes 11392000 | tf_op jit(solution)/shard_map/dot_general | solution.py:86
  366.6 28.4 %all_to_all.83 = f32[128,1,2304]{2,1,0:T(1,128)} all-to-all(f32[128,1,2304]{2,1,0:T(1,128)} %all_to_all.68), channel_id=1, replica_groups=mesh['gx'=16,'gy'=8] {'gx','gy'}, dimensions={0} | all-to-all | bytes 2359296 | tf_op jit(solution)/shard_map/all_to_all | solution.py:71
  395.0 5.1 reduce.29
  416.5 26.4 %all_to_all.84 = f32[128,1,2304]{2,1,0:T(1,128)} all-to-all(f32[128,1,2304]{2,1,0:T(1,128)} %all_to_all.69), channel_id=1, replica_groups=mesh['gx'=16,'gy'=8] {'gx','gy'}, dimensions={0} | all-to-all | bytes 2359296 | tf_op jit(solution)/shard_map/all_to_all | solution.py:71
  442.9 5.1 reduce.30
  455.5 13.4 %fusion.63 = f32[256,343]{0,1:T(8,128)S(1)} fusion(f32[4608,256]{0,1:T(8,128)S(1)} %bitcast.229, f32[4608,343]{1,0:T(8,128)} %reshape_squeeze.3), kind=kOutput, calls=%fused_computation.160 | convolution fusion | flops 4855431168 | bytes 11392000 | tf_op jit(solution)/shard_map/dot_general | solution.py:92
  479.7 5.6 collective-permute-done.10
  508.2 14.0 %fusion.64 = f32[256,4608]{1,0:T(8,128)S(1)} fusion(f32[343,256]{1,0:T(8,128)S(1)} %reshape.620, f32[4608,343]{1,0:T(8,128)} %reshape_squeeze.3), kind=kOutput, calls=%fused_computation.161 | convolution fusion | flops 4855431168 | bytes 11392000 | tf_op jit(solution)/shard_map/dot_general | solution.py:86
  530.4 28.4 %all_to_all.85 = f32[128,1,2304]{2,1,0:T(1,128)} all-to-all(f32[128,1,2304]{2,1,0:T(1,128)} %all_to_all.70), channel_id=1, replica_groups=mesh['gx'=16,'gy'=8] {'gx','gy'}, dimensions={0} | all-to-all | bytes 2359296 | tf_op jit(solution)/shard_map/all_to_all | solution.py:71
  558.8 5.1 reduce.31
  580.2 26.2 %all_to_all.86 = f32[128,1,2304]{2,1,0:T(1,128)} all-to-all(f32[128,1,2304]{2,1,0:T(1,128)} %all_to_all.71), channel_id=1, replica_groups=mesh['gx'=16,'gy'=8] {'gx','gy'}, dimensions={0} | all-to-all | bytes 2359296 | tf_op jit(solution)/shard_map/all_to_all | solution.py:71
  606.5 5.1 reduce.32
  619.1 13.4 %fusion.65 = f32[256,343]{0,1:T(8,128)S(1)} fusion(f32[4608,256]{0,1:T(8,128)S(1)} %bitcast.226, f32[4608,343]{1,0:T(8,128)} %reshape_squeeze.3), kind=kOutput, calls=%fused_computation.162 | convolution fusion | flops 4855431168 | bytes 11392000 | tf_op jit(solution)/shard_map/dot_general | solution.py:92
  637.1 6.7 %collective-permute-done.14 = f32[13,12,64]{2,1,0:T(8,128)S(1)} collective-permute-done((f32[13,12,64]{2,1,0:T(8,128)S(1)}, f32[13,12,64]{2,1,0:T(8,128)S(1)}, u32[]{:S(2)}, u32[]{:S(2)}) %collective-permute-start.14) | collective-permute-done | bytes 39968 | tf_op jit(solution)/shard_map/ppermute | solution.py:21
  644.1 6.9 %collective-permute-done.15 = f32[6,12,64]{2,1,0:T(8,128)S(1)} collective-permute-done((f32[6,12,64]{2,1,0:T(8,128)S(1)}, f32[6,12,64]{2,1,0:T(8,128)S(1)}, u32[]{:S(2)}, u32[]{:S(2)}) %collective-permute-start.15) | collective-permute-done | bytes 18464 | tf_op jit(solution)/shard_map/ppermute | solution.py:21
  (209 shorter events, 220.3 us)
Async XLA Ops:
  0.0 151.1 %copy-start = (f32[343,343]{1,0:T(8,128)S(1)}, f32[343,343]{1,0:T(8,128)}, u32[]{:S(2)}) copy-start(f32[343,343]{1,0:T(8,128)} %param.34) | copy-start | bytes 1411792
  0.0 12.1 %copy-start.10 = (s32[1,256]{1,0:T(1,128)S(1)}, s32[1,256]{1,0:T(1,128)}, u32[]{:S(2)}) copy-start(s32[1,256]{1,0:T(1,128)} %param.35) | copy-start | bytes 3076
  1.1 7.8 %collective-permute-start = (f32[1,6,12,64]{3,2,1,0:T(8,128)S(1)}, f32[1,6,12,64]{3,2,1,0:T(8,128)S(1)}, u32[]{:S(2)}, u32[]{:S(2)}) collective-permute-start(f32[1,6,12,64]{3,2,1,0:T(8,128)S(1)} %slice.568), channel_id=1, source_target_pairs={{0,120},{8,0},{16,8},{24,16},{32,24},{40,32},{48,40},{56,48},{64,5... | collective-permute-start | bytes 55304 | tf_op jit(solution)/shard_map/ppermute | solution.py:21
  8.9 26.9 %collective-permute-start.1 = (f32[13,1,12,64]{3,2,1,0:T(8,128)S(1)}, f32[13,1,12,64]{3,2,1,0:T(8,128)S(1)}, u32[]{:S(2)}, u32[]{:S(2)}) collective-permute-start(f32[13,1,12,64]{3,2,1,0:T(8,128)S(1)} %slice.648), channel_id=1, source_target_pairs={{0,7},{1,0},{2,1},{3,2},{4,3},{5,4},{6,5},{7,6},{8,15},{9,8},{10,9... | collective-permute-start | bytes 119816 | tf_op jit(solution)/shard_map/ppermute | solution.py:21
  56.8 28.3 %all-to-all-start = ((f32[128,1,2304]{2,1,0:T(1,128)}), f32[128,1,2304]{2,1,0:T(1,128)S(1)}, u32[]{:S(2)}, u32[]{:S(2)}) async-start(f32[128,1,2304]{2,1,0:T(1,128)} %all_to_all.64), calls=%async_computation | async-start | bytes 2359296 | tf_op jit(solution)/shard_map/all_to_all | solution.py:71
  89.2 2.9 copy-start.7
  152.9 10.6 %copy-start.8 = (f32[2,3]{1,0:T(2,128)S(1)}, f32[2,3]{1,0:T(2,128)}, u32[]{:S(2)}) copy-start(f32[2,3]{1,0:T(2,128)} %param.39) | copy-start | bytes 76
  152.9 14.5 %copy-start.9 = (f32[12,72]{1,0:T(8,128)S(1)}, f32[12,72]{1,0:T(8,128)}, u32[]{:S(2)}) copy-start(f32[12,72]{1,0:T(8,128)} %param.33) | copy-start | bytes 10372
  155.6 7.1 %collective-permute-start.2 = (f32[13,12,64]{2,1,0:T(8,128)S(1)}, f32[13,12,64]{2,1,0:T(8,128)S(1)}, u32[]{:S(2)}, u32[]{:S(2)}) collective-permute-start(f32[13,12,64]{2,1,0:T(8,128)S(1)} %slice_bitcast_fusion.6), channel_id=1, source_target_pairs={{0,1},{1,2},{2,3},{3,4},{4,5},{5,6},{6,7},{7,0},{8,9},{9,10},{10,1... | collective-permute-start | bytes 119816 | tf_op jit(solution)/shard_map/ppermute | solution.py:21
  162.6 0.8 copy-start.1
  163.5 7.1 %collective-permute-start.3 = (f32[6,12,64]{2,1,0:T(8,128)S(1)}, f32[6,12,64]{2,1,0:T(8,128)S(1)}, u32[]{:S(2)}, u32[]{:S(2)}) collective-permute-start(f32[6,12,64]{2,1,0:T(8,128)S(1)} %slice_bitcast_fusion.11), channel_id=1, source_target_pairs={{0,8},{8,16},{16,24},{24,32},{32,40},{40,48},{48,56},{56,64},{64,7... | collective-permute-start | bytes 55304 | tf_op jit(solution)/shard_map/ppermute | solution.py:21
  167.4 14.3 %copy-start.4 = (f32[12,6,12]{2,1,0:T(8,128)}, f32[12,6,12]{2,1,0:T(8,128)S(1)}, u32[]{:S(2)}) copy-start(f32[12,6,12]{2,1,0:T(8,128)S(1)} %mul.229) | copy-start | bytes 10372
  171.7 5.1 collective-permute-start.4
  176.8 4.8 collective-permute-start.5
  314.6 20.3 %copy-start.5 = (f32[12,6,12]{2,1,0:T(8,128)S(1)}, f32[12,6,12]{2,1,0:T(8,128)}, u32[]{:S(2)}) copy-start(f32[12,6,12]{2,1,0:T(8,128)} %copy-done.4) | copy-start | bytes 10372
  318.3 6.8 %collective-permute-start.6 = (f32[13,12,64]{2,1,0:T(8,128)S(1)}, f32[13,12,64]{2,1,0:T(8,128)S(1)}, u32[]{:S(2)}, u32[]{:S(2)}) collective-permute-start(f32[13,12,64]{2,1,0:T(8,128)S(1)} %slice_bitcast_fusion.4), channel_id=1, source_target_pairs={{0,1},{1,2},{2,3},{3,4},{4,5},{5,6},{6,7},{7,0},{8,9},{9,10},{10,1... | collective-permute-start | bytes 119816 | tf_op jit(solution)/shard_map/ppermute | solution.py:21
  326.1 0.8 copy-start.2
  326.9 7.1 %collective-permute-start.7 = (f32[6,12,64]{2,1,0:T(8,128)S(1)}, f32[6,12,64]{2,1,0:T(8,128)S(1)}, u32[]{:S(2)}, u32[]{:S(2)}) collective-permute-start(f32[6,12,64]{2,1,0:T(8,128)S(1)} %slice_bitcast_fusion.10), channel_id=1, source_target_pairs={{0,8},{8,16},{16,24},{24,32},{32,40},{40,48},{48,56},{56,64},{64,7... | collective-permute-start | bytes 55304 | tf_op jit(solution)/shard_map/ppermute | solution.py:21
  335.1 1.8 collective-permute-start.8
  336.9 4.8 collective-permute-start.9
  478.5 6.8 %collective-permute-start.10 = (f32[13,12,64]{2,1,0:T(8,128)S(1)}, f32[13,12,64]{2,1,0:T(8,128)S(1)}, u32[]{:S(2)}, u32[]{:S(2)}) collective-permute-start(f32[13,12,64]{2,1,0:T(8,128)S(1)} %slice_bitcast_fusion.2), channel_id=1, source_target_pairs={{0,1},{1,2},{2,3},{3,4},{4,5},{5,6},{6,7},{7,0},{8,9},{9,10},{10,1... | collective-permute-start | bytes 119816 | tf_op jit(solution)/shard_map/ppermute | solution.py:21
  486.2 0.8 copy-start.3
  487.0 7.1 %collective-permute-start.11 = (f32[6,12,64]{2,1,0:T(8,128)S(1)}, f32[6,12,64]{2,1,0:T(8,128)S(1)}, u32[]{:S(2)}, u32[]{:S(2)}) collective-permute-start(f32[6,12,64]{2,1,0:T(8,128)S(1)} %slice_bitcast_fusion.9), channel_id=1, source_target_pairs={{0,8},{8,16},{16,24},{24,32},{32,40},{40,48},{48,56},{56,64},{64,7... | collective-permute-start | bytes 55304 | tf_op jit(solution)/shard_map/ppermute | solution.py:21
  495.2 4.3 collective-permute-start.12
  499.5 4.8 collective-permute-start.13
  634.4 16.7 %copy-start.6 = (f32[12,6,12]{2,1,0:T(8,128)S(1)}, f32[12,6,12]{2,1,0:T(8,128)}, u32[]{:S(2)}) copy-start(f32[12,6,12]{2,1,0:T(8,128)} %copy-done.4) | copy-start | bytes 10372
  636.9 6.9 %collective-permute-start.14 = (f32[13,12,64]{2,1,0:T(8,128)S(1)}, f32[13,12,64]{2,1,0:T(8,128)S(1)}, u32[]{:S(2)}, u32[]{:S(2)}) collective-permute-start(f32[13,12,64]{2,1,0:T(8,128)S(1)} %slice_bitcast_fusion), channel_id=1, source_target_pairs={{0,1},{1,2},{2,3},{3,4},{4,5},{5,6},{6,7},{7,0},{8,9},{9,10},{10,1... | collective-permute-start | bytes 119816 | tf_op jit(solution)/shard_map/ppermute | solution.py:21
  643.8 7.2 %collective-permute-start.15 = (f32[6,12,64]{2,1,0:T(8,128)S(1)}, f32[6,12,64]{2,1,0:T(8,128)S(1)}, u32[]{:S(2)}, u32[]{:S(2)}) collective-permute-start(f32[6,12,64]{2,1,0:T(8,128)S(1)} %slice_bitcast_fusion.8), channel_id=1, source_target_pairs={{0,8},{8,16},{16,24},{24,32},{32,40},{40,48},{48,56},{56,64},{64,7... | collective-permute-start | bytes 55304 | tf_op jit(solution)/shard_map/ppermute | solution.py:21

commit v2 on v1

--- a/solution.py
+++ b/solution.py
@@ -13,12 +13,24 @@
 
 
 PRECISE = lax.Precision.HIGHEST
+DENSE = lax.Precision.HIGH
 
 
 def shifted(value, axis, steps):
     count = lax.axis_size(axis)
     pairs = [(source, (source + steps) % count) for source in range(count)]
     return lax.ppermute(value, axis, pairs)
+
+
+def diagonal(value, steps):
+    count_x = lax.axis_size("gx")
+    count_y = lax.axis_size("gy")
+    pairs = [
+        (u * count_y + v, ((u + steps) % count_x) * count_y + (v + steps) % count_y)
+        for u in range(count_x)
+        for v in range(count_y)
+    ]
+    return lax.ppermute(value, ("gx", "gy"), pairs)
 
 
 def cell_ranges():
@@ -78,25 +90,32 @@
         return jnp.dot(one_hot, applied.reshape(atoms, nproj * W), precision=PRECISE)
 
     def apply_operator(current):
-        face_in = shifted(current[:1], "gx", -1)
-        extended = jnp.concatenate([current, face_in], axis=0)
-        side_in = shifted(extended[:, :1], "gy", -1)
-        extended = jnp.concatenate([extended, side_in], axis=1)
+        face_x = shifted(current[:1], "gx", -1)
+        face_y = shifted(current[:, :1], "gy", -1)
+        corner = diagonal(current[:1, :1], -1)
+        extended = jnp.concatenate(
+            [
+                jnp.concatenate([current, face_y], axis=1),
+                jnp.concatenate([face_x, corner], axis=1),
+            ],
+            axis=0,
+        )
         cell_in = gather_cells(extended)
-        every_cell = jnp.dot(tile_flat, cell_in, precision=PRECISE)
+        every_cell = jnp.dot(tile_flat, cell_in, precision=DENSE)
         projected = (every_cell.reshape(slots * nproj, cells, W) * row_mask).sum(axis=1)
         received = exchange(projected.reshape(owners, -1)).reshape(slots, nproj * W)
         returned = exchange(owner_work(received).reshape(owners, -1))
         spread_in = (returned.reshape(slots * nproj, 1, W) * row_mask).reshape(slots * nproj, cells * W)
-        kinetic = jnp.dot(cell_matrix, cell_in, precision=PRECISE)
+        kinetic = jnp.dot(cell_matrix, cell_in, precision=DENSE)
         spread = lax.dot_general(
-            tile_flat, spread_in, (((0,), (0,)), ((), ())), precision=PRECISE
+            tile_flat, spread_in, (((0,), (0,)), ((), ())), precision=DENSE
         )
         summed = scatter_cells(kinetic + spread, W)
-        arrived = shifted(summed[:, rows_y], "gy", 1)
-        summed = summed[:, :rows_y].at[:, 0].add(arrived)
-        arrived_x = shifted(summed[rows_x], "gx", 1)
-        summed = summed[:rows_x].at[0].add(arrived_x)
+        from_y = shifted(summed[:rows_x, rows_y], "gy", 1)
+        from_x = shifted(summed[rows_x, :rows_y], "gx", 1)
+        from_corner = diagonal(summed[rows_x, rows_y], 1)
+        summed = summed[:rows_x, :rows_y].at[:, 0].add(from_y)
+        summed = summed.at[0].add(from_x).at[0, 0].add(from_corner)
         return summed + local_pot * current
 
     previous = wavefunctions.reshape(rows_x, rows_y, ZN, W)

time: 664 us -> 593 us (0.89)
  blocking collectives: 191 us -> 85.9 us
  waiting for transfers between devices: 81.3 us -> 135 us
  matrix products: 139 us -> 96.1 us
  starting transfers between devices: 23.6 us -> 53.5 us
    all_to_all x7 -> x3, blocking collectives: 191 us -> 85.9 us  [exchange(): lax.all_to_all(values, ('gx', 'gy'), split_axis=0, concat_axis=0, tiled=T...]
    all_to_all x1 -> x5, waiting for transfers between devices: 19.1 us -> 91.3 us  [exchange(): lax.all_to_all(values, ('gx', 'gy'), split_axis=0, concat_axis=0, tiled=T...]
    ppermute x16, waiting for transfers between devices: 62.2 us -> 23 us  [shifted(): return lax.ppermute(value, axis, pairs)]
    dot_general x8, matrix products: 59 us -> 34.9 us  [the longest x4 33.2 us: apply_operator(): every_cell = jnp.dot(tile_flat, cell_in, precision=DENSE)]
    all_to_all x1 -> x5, starting transfers between devices: 7.85 us -> 29.1 us  [exchange(): lax.all_to_all(values, ('gx', 'gy'), split_axis=0, concat_axis=0, tiled=T...]
    ppermute x0 -> x8, waiting for transfers between devices: none -> 20.4 us  [diagonal(): return lax.ppermute(value, ('gx', 'gy'), pairs)]
    dot_general x4, matrix products: 53.5 us -> 35 us  [apply_operator(): lax.dot_general(tile_flat, spread_in, (((0,), (0,)), ((), ())), precision...]
    ppermute x0 -> x8, starting transfers between devices: none -> 8.29 us  [diagonal(): return lax.ppermute(value, ('gx', 'gy'), pairs)]
  transfers between devices with their start and end apart: 17 -> 29, of which waited for: 16 -> 20; matrix products, arithmetic and copies ran while one was open for 5% -> 6% of each run, Pallas kernels for 0% -> 0%
where the time goes in v2:
time: 593 us; the launch traced here: 584 us
  local copies, waits for them, and re-layouts  148 us (25%)
  waiting for transfers between devices  135 us (23%)
  matrix products  96.1 us (16%)
  blocking collectives  85.9 us (14%)
  other arithmetic  57.3 us (10%)
  starting transfers between devices  53.5 us (9%)
  between operations  7.94 us (1%)
    all_to_all x5, waiting for transfers between devices, exchange(): lax.all_to_all(values, ('gx', 'gy'), split_axis=0, concat_axis=0, tiled=T...  91.3 us
    all_to_all x3, blocking collectives, exchange(): lax.all_to_all(values, ('gx', 'gy'), split_axis=0, concat_axis=0, tiled=T...  85.9 us
    all_to_all x8, other arithmetic, exchange(): lax.all_to_all(values, ('gx', 'gy'), split_axis=0, concat_axis=0, tiled=T...  38.9 us
    dot_general x4, matrix products, apply_operator(): lax.dot_general(tile_flat, spread_in, (((0,), (0,)), ((), ())), precision...  35 us
    dot_general x4, matrix products, apply_operator(): every_cell = jnp.dot(tile_flat, cell_in, precision=DENSE)  33.2 us
    all_to_all x5, starting transfers between devices, exchange(): lax.all_to_all(values, ('gx', 'gy'), split_axis=0, concat_axis=0, tiled=T...  29.1 us
    all_to_all x8, local copies, waits for them, and re-layouts, exchange(): lax.all_to_all(values, ('gx', 'gy'), split_axis=0, concat_axis=0, tiled=T...  26.7 us
    ppermute x16, waiting for transfers between devices, shifted(): return lax.ppermute(value, axis, pairs)  23 us
  transfers between devices with their start and end apart: 29, of which 20 were waited for; matrix products, arithmetic and copies ran while one was open for 6% of the time, Pallas kernels for 0%

profile of v2, /device:TPU:0, one launch (start us, length us, event | category | flops | bytes accessed | tf_op | source)
XLA Modules:
  0.0 583.5 jit_solution(1540313327667864114)
XLA Ops:
  5.3 4.6 collective-permute-start.2
  13.8 14.0 %copy.123 = f32[1,256,18,343]{3,2,1,0:T(8,128)} copy(f32[1,256,18,343]{1,0,3,2:T(1,128)} %param.44) | data formatting | bytes 12644352 | tf_op args[4]
  27.8 9.2 %reshape_squeeze.3 = f32[4608,343]{1,0:T(8,128)} reshape(f32[1,256,18,343]{3,2,1,0:T(8,128)} %copy.123) | data formatting | bytes 12644352 | tf_op jit(solution)/shard_map/reshape;squeeze | solution.py:75
  38.4 8.3 %fusion.67 = f32[256,4608]{1,0:T(8,128)S(1)} fusion(f32[343,256]{1,0:T(8,128)S(1)} %reshape.743, f32[4608,343]{1,0:T(8,128)} %reshape_squeeze.3), kind=kOutput, calls=%fused_computation.176 | convolution fusion | flops 2427715584 | bytes 11392000 | tf_op jit(solution)/shard_map/dot_general | solution.py:104
  52.9 4.8 all-to-all-start
  59.0 19.1 %all-to-all-done = f32[128,1,2304]{2,1,0:T(1,128)S(1)} async-done(((f32[128,1,2304]{2,1,0:T(1,128)}), f32[128,1,2304]{2,1,0:T(1,128)S(1)}, u32[]{:S(2)}, u32[]{:S(2)}) %all-to-all-start) | async-done | bytes 1179680 | tf_op jit(solution)/shard_map/all_to_all | solution.py:83
  95.9 6.1 %all-to-all-start.1 = ((f32[128,1,2304]{2,1,0:T(1,128)}), f32[128,1,2304]{2,1,0:T(1,128)}, u32[]{:S(2)}, u32[]{:S(2)}) async-start(f32[128,1,2304]{2,1,0:T(1,128)} %all_to_all.65), calls=%async_computation.1 | async-start | bytes 2359296 | tf_op jit(solution)/shard_map/all_to_all | solution.py:83
  106.6 15.5 %all-to-all-done.1 = f32[128,1,2304]{2,1,0:T(1,128)} async-done(((f32[128,1,2304]{2,1,0:T(1,128)}), f32[128,1,2304]{2,1,0:T(1,128)}, u32[]{:S(2)}, u32[]{:S(2)}) %all-to-all-start.1) | async-done | bytes 1179680 | tf_op jit(solution)/shard_map/all_to_all | solution.py:83
  130.7 8.7 %fusion.68 = f32[256,343]{0,1:T(8,128)S(1)} fusion(f32[4608,256]{0,1:T(8,128)S(1)} %bitcast.233, f32[4608,343]{1,0:T(8,128)} %reshape_squeeze.3), kind=kOutput, calls=%fused_computation.177 | convolution fusion | flops 2427715584 | bytes 11392000 | tf_op jit(solution)/shard_map/dot_general | solution.py:110
  144.9 5.6 collective-permute-done.3
  163.1 8.3 %fusion.69 = f32[256,4608]{1,0:T(8,128)S(1)} fusion(f32[343,256]{1,0:T(8,128)S(1)} %reshape.751, f32[4608,343]{1,0:T(8,128)} %reshape_squeeze.3), kind=kOutput, calls=%fused_computation.178 | convolution fusion | flops 2427715584 | bytes 11392000 | tf_op jit(solution)/shard_map/dot_general | solution.py:104
  179.5 28.6 %all_to_all.80 = f32[128,1,2304]{2,1,0:T(1,128)} all-to-all(f32[128,1,2304]{2,1,0:T(1,128)} %all_to_all.66), channel_id=1, replica_groups=mesh['gx'=16,'gy'=8] {'gx','gy'}, dimensions={0} | all-to-all | bytes 2359296 | tf_op jit(solution)/shard_map/all_to_all | solution.py:83
  208.2 5.1 reduce.35
  229.6 6.1 %all-to-all-start.3 = ((f32[128,1,2304]{2,1,0:T(1,128)}), f32[128,1,2304]{2,1,0:T(1,128)}, u32[]{:S(2)}, u32[]{:S(2)}) async-start(f32[128,1,2304]{2,1,0:T(1,128)} %all_to_all.67), calls=%async_computation.3 | async-start | bytes 2359296 | tf_op jit(solution)/shard_map/all_to_all | solution.py:83
  235.9 19.9 %all-to-all-done.3 = f32[128,1,2304]{2,1,0:T(1,128)} async-done(((f32[128,1,2304]{2,1,0:T(1,128)}), f32[128,1,2304]{2,1,0:T(1,128)}, u32[]{:S(2)}, u32[]{:S(2)}) %all-to-all-start.3) | async-done | bytes 1179680 | tf_op jit(solution)/shard_map/all_to_all | solution.py:83
  255.8 5.1 reduce.36
  268.4 8.7 %fusion.70 = f32[256,343]{0,1:T(8,128)S(1)} fusion(f32[4608,256]{0,1:T(8,128)S(1)} %bitcast.234, f32[4608,343]{1,0:T(8,128)} %reshape_squeeze.3), kind=kOutput, calls=%fused_computation.179 | convolution fusion | flops 2427715584 | bytes 11392000 | tf_op jit(solution)/shard_map/dot_general | solution.py:110
  308.4 8.3 %fusion.71 = f32[256,4608]{1,0:T(8,128)S(1)} fusion(f32[343,256]{1,0:T(8,128)S(1)} %reshape.759, f32[4608,343]{1,0:T(8,128)} %reshape_squeeze.3), kind=kOutput, calls=%fused_computation.180 | convolution fusion | flops 2427715584 | bytes 11392000 | tf_op jit(solution)/shard_map/dot_general | solution.py:104
  324.8 28.6 %all_to_all.81 = f32[128,1,2304]{2,1,0:T(1,128)} all-to-all(f32[128,1,2304]{2,1,0:T(1,128)} %all_to_all.68), channel_id=1, replica_groups=mesh['gx'=16,'gy'=8] {'gx','gy'}, dimensions={0} | all-to-all | bytes 2359296 | tf_op jit(solution)/shard_map/all_to_all | solution.py:83
  353.4 5.1 reduce.37
  374.9 6.1 %all-to-all-start.5 = ((f32[128,1,2304]{2,1,0:T(1,128)}), f32[128,1,2304]{2,1,0:T(1,128)}, u32[]{:S(2)}, u32[]{:S(2)}) async-start(f32[128,1,2304]{2,1,0:T(1,128)} %all_to_all.69), calls=%async_computation.5 | async-start | bytes 2359296 | tf_op jit(solution)/shard_map/all_to_all | solution.py:83
  384.1 16.9 %all-to-all-done.5 = f32[128,1,2304]{2,1,0:T(1,128)} async-done(((f32[128,1,2304]{2,1,0:T(1,128)}), f32[128,1,2304]{2,1,0:T(1,128)}, u32[]{:S(2)}, u32[]{:S(2)}) %all-to-all-start.5) | async-done | bytes 1179680 | tf_op jit(solution)/shard_map/all_to_all | solution.py:83
  401.1 5.1 reduce.38
  413.7 8.7 %fusion.72 = f32[256,343]{0,1:T(8,128)S(1)} fusion(f32[4608,256]{0,1:T(8,128)S(1)} %bitcast.235, f32[4608,343]{1,0:T(8,128)} %reshape_squeeze.3), kind=kOutput, calls=%fused_computation.181 | convolution fusion | flops 2427715584 | bytes 11392000 | tf_op jit(solution)/shard_map/dot_general | solution.py:110
  453.7 8.3 %fusion.73 = f32[256,4608]{1,0:T(8,128)S(1)} fusion(f32[343,256]{1,0:T(8,128)S(1)} %reshape.767, f32[4608,343]{1,0:T(8,128)} %reshape_squeeze.3), kind=kOutput, calls=%fused_computation.182 | convolution fusion | flops 2427715584 | bytes 11392000 | tf_op jit(solution)/shard_map/dot_general | solution.py:104
  470.1 28.6 %all_to_all.82 = f32[128,1,2304]{2,1,0:T(1,128)} all-to-all(f32[128,1,2304]{2,1,0:T(1,128)} %all_to_all.70), channel_id=1, replica_groups=mesh['gx'=16,'gy'=8] {'gx','gy'}, dimensions={0} | all-to-all | bytes 2359296 | tf_op jit(solution)/shard_map/all_to_all | solution.py:83
  498.7 5.1 reduce.39
  520.2 6.0 %all-to-all-start.7 = ((f32[128,1,2304]{2,1,0:T(1,128)}), f32[128,1,2304]{2,1,0:T(1,128)}, u32[]{:S(2)}, u32[]{:S(2)}) async-start(f32[128,1,2304]{2,1,0:T(1,128)} %all_to_all.71), calls=%async_computation.7 | async-start | bytes 2359296 | tf_op jit(solution)/shard_map/all_to_all | solution.py:83
  526.3 19.9 %all-to-all-done.7 = f32[128,1,2304]{2,1,0:T(1,128)} async-done(((f32[128,1,2304]{2,1,0:T(1,128)}), f32[128,1,2304]{2,1,0:T(1,128)}, u32[]{:S(2)}, u32[]{:S(2)}) %all-to-all-start.7) | async-done | bytes 1179680 | tf_op jit(solution)/shard_map/all_to_all | solution.py:83
  546.2 5.1 reduce.40
  558.8 8.7 %fusion.74 = f32[256,343]{0,1:T(8,128)S(1)} fusion(f32[4608,256]{0,1:T(8,128)S(1)} %bitcast.232, f32[4608,343]{1,0:T(8,128)} %reshape_squeeze.3), kind=kOutput, calls=%fused_computation.183 | convolution fusion | flops 2427715584 | bytes 11392000 | tf_op jit(solution)/shard_map/dot_general | solution.py:110
  572.9 5.7 collective-permute-done.21
  (225 shorter events, 231.3 us)
Async XLA Ops:
  0.0 139.4 %copy-start = (f32[343,343]{1,0:T(8,128)S(1)}, f32[343,343]{1,0:T(8,128)}, u32[]{:S(2)}) copy-start(f32[343,343]{1,0:T(8,128)} %param.42) | copy-start | bytes 1411792
  1.2 36.4 %collective-permute-start = (f32[12,1,12,64]{3,2,1,0:T(8,128)S(1)}, f32[12,1,12,64]{3,2,1,0:T(8,128)S(1)}, u32[]{:S(2)}, u32[]{:S(2)}) collective-permute-start(f32[12,1,12,64]{3,2,1,0:T(8,128)S(1)} %slice.784), channel_id=1, source_target_pairs={{0,7},{1,0},{2,1},{3,2},{4,3},{5,4},{6,5},{7,6},{8,15},{9,8},{10,9... | collective-permute-start | bytes 110600 | tf_op jit(solution)/shard_map/ppermute | solution.py:22
  5.3 32.3 %collective-permute-start.2 = (f32[1,1,12,64]{3,2,1,0:T(8,128)S(1)}, f32[1,1,12,64]{3,2,1,0:T(8,128)S(1)}, u32[]{:S(2)}, u32[]{:S(2)}) collective-permute-start(f32[1,1,12,64]{3,2,1,0:T(8,128)S(1)} %slice.786), channel_id=1, source_target_pairs={{0,127},{1,120},{2,121},{3,122},{4,123},{5,124},{6,125},{7,126},{8... | collective-permute-start | bytes 9224 | tf_op jit(solution)/shard_map/ppermute | solution.py:33
  11.0 26.6 %collective-permute-start.1 = (f32[1,6,12,64]{3,2,1,0:T(8,128)S(1)}, f32[1,6,12,64]{3,2,1,0:T(8,128)S(1)}, u32[]{:S(2)}, u32[]{:S(2)}) collective-permute-start(f32[1,6,12,64]{3,2,1,0:T(8,128)S(1)} %slice.698), channel_id=1, source_target_pairs={{0,120},{8,0},{16,8},{24,16},{32,24},{40,32},{48,40},{56,48},{64,5... | collective-permute-start | bytes 55304 | tf_op jit(solution)/shard_map/ppermute | solution.py:22
  52.9 25.2 %all-to-all-start = ((f32[128,1,2304]{2,1,0:T(1,128)}), f32[128,1,2304]{2,1,0:T(1,128)S(1)}, u32[]{:S(2)}, u32[]{:S(2)}) async-start(f32[128,1,2304]{2,1,0:T(1,128)} %all_to_all.64), calls=%async_computation | async-start | bytes 2359296 | tf_op jit(solution)/shard_map/all_to_all | solution.py:83
  95.9 26.2 %all-to-all-start.1 = ((f32[128,1,2304]{2,1,0:T(1,128)}), f32[128,1,2304]{2,1,0:T(1,128)}, u32[]{:S(2)}, u32[]{:S(2)}) async-start(f32[128,1,2304]{2,1,0:T(1,128)} %all_to_all.65), calls=%async_computation.1 | async-start | bytes 2359296 | tf_op jit(solution)/shard_map/all_to_all | solution.py:83
  140.8 13.2 %copy-start.1 = (f32[12,6,12]{2,1,0:T(8,128)S(1)}, f32[12,6,12]{2,1,0:T(8,128)}, u32[]{:S(2)}) copy-start(f32[12,6,12]{2,1,0:T(8,128)} %mul.229) | copy-start | bytes 10372
  143.6 6.9 %collective-permute-start.3 = (f32[12,12,64]{2,1,0:T(8,128)S(1)}, f32[12,12,64]{2,1,0:T(8,128)S(1)}, u32[]{:S(2)}, u32[]{:S(2)}) collective-permute-start(f32[12,12,64]{2,1,0:T(8,128)S(1)} %slice_bitcast_fusion.4), channel_id=1, source_target_pairs={{0,1},{1,2},{2,3},{3,4},{4,5},{5,6},{6,7},{7,0},{8,9},{9,10},{10,1... | collective-permute-start | bytes 110600 | tf_op jit(solution)/shard_map/ppermute | solution.py:22
  143.8 7.4 %collective-permute-start.4 = (f32[6,12,64]{2,1,0:T(8,128)S(1)}, f32[6,12,64]{2,1,0:T(8,128)S(1)}, u32[]{:S(2)}, u32[]{:S(2)}) collective-permute-start(f32[6,12,64]{2,1,0:T(8,128)S(1)} %slice_bitcast_fusion.8), channel_id=1, source_target_pairs={{0,8},{8,16},{16,24},{24,32},{32,40},{40,48},{48,56},{56,64},{64,7... | collective-permute-start | bytes 55304 | tf_op jit(solution)/shard_map/ppermute | solution.py:22
  144.0 9.9 %collective-permute-start.5 = (f32[12,64]{1,0:T(8,128)S(1)}, f32[12,64]{1,0:T(8,128)S(1)}, u32[]{:S(2)}, u32[]{:S(2)}) collective-permute-start(f32[12,64]{1,0:T(8,128)S(1)} %slice_bitcast_fusion.12), channel_id=1, source_target_pairs={{0,9},{1,10},{2,11},{3,12},{4,13},{5,14},{6,15},{7,8},{8,17},{9,18... | collective-permute-start | bytes 9224 | tf_op jit(solution)/shard_map/ppermute | solution.py:33
  154.2 6.1 %collective-permute-start.6 = (f32[12,1,12,64]{3,2,1,0:T(8,128)S(1)}, f32[12,1,12,64]{3,2,1,0:T(8,128)S(1)}, u32[]{:S(2)}, u32[]{:S(2)}) collective-permute-start(f32[12,1,12,64]{3,2,1,0:T(8,128)S(1)} %slice.799), channel_id=1, source_target_pairs={{0,7},{1,0},{2,1},{3,2},{4,3},{5,4},{6,5},{7,6},{8,15},{9,8},{10,9... | collective-permute-start | bytes 110600 | tf_op jit(solution)/shard_map/ppermute | solution.py:22
  156.1 4.2 collective-permute-start.7
  157.2 3.1 collective-permute-start.8
  229.6 26.2 %all-to-all-start.3 = ((f32[128,1,2304]{2,1,0:T(1,128)}), f32[128,1,2304]{2,1,0:T(1,128)}, u32[]{:S(2)}, u32[]{:S(2)}) async-start(f32[128,1,2304]{2,1,0:T(1,128)} %all_to_all.67), calls=%async_computation.3 | async-start | bytes 2359296 | tf_op jit(solution)/shard_map/all_to_all | solution.py:83
  281.6 17.7 %copy-start.2 = (f32[12,6,12]{2,1,0:T(8,128)S(1)}, f32[12,6,12]{2,1,0:T(8,128)}, u32[]{:S(2)}) copy-start(f32[12,6,12]{2,1,0:T(8,128)} %mul.229) | copy-start | bytes 10372
  287.3 6.9 %collective-permute-start.9 = (f32[12,12,64]{2,1,0:T(8,128)S(1)}, f32[12,12,64]{2,1,0:T(8,128)S(1)}, u32[]{:S(2)}, u32[]{:S(2)}) collective-permute-start(f32[12,12,64]{2,1,0:T(8,128)S(1)} %slice_bitcast_fusion.3), channel_id=1, source_target_pairs={{0,1},{1,2},{2,3},{3,4},{4,5},{5,6},{6,7},{7,0},{8,9},{9,10},{10,1... | collective-permute-start | bytes 110600 | tf_op jit(solution)/shard_map/ppermute | solution.py:22
  289.2 7.2 %collective-permute-start.10 = (f32[6,12,64]{2,1,0:T(8,128)S(1)}, f32[6,12,64]{2,1,0:T(8,128)S(1)}, u32[]{:S(2)}, u32[]{:S(2)}) collective-permute-start(f32[6,12,64]{2,1,0:T(8,128)S(1)} %slice_bitcast_fusion.7), channel_id=1, source_target_pairs={{0,8},{8,16},{16,24},{24,32},{32,40},{40,48},{48,56},{56,64},{64,7... | collective-permute-start | bytes 55304 | tf_op jit(solution)/shard_map/ppermute | solution.py:22
  289.3 9.9 %collective-permute-start.11 = (f32[12,64]{1,0:T(8,128)S(1)}, f32[12,64]{1,0:T(8,128)S(1)}, u32[]{:S(2)}, u32[]{:S(2)}) collective-permute-start(f32[12,64]{1,0:T(8,128)S(1)} %slice_bitcast_fusion.11), channel_id=1, source_target_pairs={{0,9},{1,10},{2,11},{3,12},{4,13},{5,14},{6,15},{7,8},{8,17},{9,18... | collective-permute-start | bytes 9224 | tf_op jit(solution)/shard_map/ppermute | solution.py:33
  299.5 6.1 %collective-permute-start.12 = (f32[12,1,12,64]{3,2,1,0:T(8,128)S(1)}, f32[12,1,12,64]{3,2,1,0:T(8,128)S(1)}, u32[]{:S(2)}, u32[]{:S(2)}) collective-permute-start(f32[12,1,12,64]{3,2,1,0:T(8,128)S(1)} %slice.814), channel_id=1, source_target_pairs={{0,7},{1,0},{2,1},{3,2},{4,3},{5,4},{6,5},{7,6},{8,15},{9,8},{10,9... | collective-permute-start | bytes 110600 | tf_op jit(solution)/shard_map/ppermute | solution.py:22
  301.4 4.2 collective-permute-start.13
  302.5 3.1 collective-permute-start.14
  374.9 26.2 %all-to-all-start.5 = ((f32[128,1,2304]{2,1,0:T(1,128)}), f32[128,1,2304]{2,1,0:T(1,128)}, u32[]{:S(2)}, u32[]{:S(2)}) async-start(f32[128,1,2304]{2,1,0:T(1,128)} %all_to_all.69), calls=%async_computation.5 | async-start | bytes 2359296 | tf_op jit(solution)/shard_map/all_to_all | solution.py:83
  432.5 6.9 %collective-permute-start.15 = (f32[12,12,64]{2,1,0:T(8,128)S(1)}, f32[12,12,64]{2,1,0:T(8,128)S(1)}, u32[]{:S(2)}, u32[]{:S(2)}) collective-permute-start(f32[12,12,64]{2,1,0:T(8,128)S(1)} %slice_bitcast_fusion.2), channel_id=1, source_target_pairs={{0,1},{1,2},{2,3},{3,4},{4,5},{5,6},{6,7},{7,0},{8,9},{9,10},{10,1... | collective-permute-start | bytes 110600 | tf_op jit(solution)/shard_map/ppermute | solution.py:22
  434.5 7.2 %collective-permute-start.16 = (f32[6,12,64]{2,1,0:T(8,128)S(1)}, f32[6,12,64]{2,1,0:T(8,128)S(1)}, u32[]{:S(2)}, u32[]{:S(2)}) collective-permute-start(f32[6,12,64]{2,1,0:T(8,128)S(1)} %slice_bitcast_fusion.6), channel_id=1, source_target_pairs={{0,8},{8,16},{16,24},{24,32},{32,40},{40,48},{48,56},{56,64},{64,7... | collective-permute-start | bytes 55304 | tf_op jit(solution)/shard_map/ppermute | solution.py:22
  434.6 9.9 %collective-permute-start.17 = (f32[12,64]{1,0:T(8,128)S(1)}, f32[12,64]{1,0:T(8,128)S(1)}, u32[]{:S(2)}, u32[]{:S(2)}) collective-permute-start(f32[12,64]{1,0:T(8,128)S(1)} %slice_bitcast_fusion.10), channel_id=1, source_target_pairs={{0,9},{1,10},{2,11},{3,12},{4,13},{5,14},{6,15},{7,8},{8,17},{9,18... | collective-permute-start | bytes 9224 | tf_op jit(solution)/shard_map/ppermute | solution.py:33
  444.8 6.1 %collective-permute-start.18 = (f32[12,1,12,64]{3,2,1,0:T(8,128)S(1)}, f32[12,1,12,64]{3,2,1,0:T(8,128)S(1)}, u32[]{:S(2)}, u32[]{:S(2)}) collective-permute-start(f32[12,1,12,64]{3,2,1,0:T(8,128)S(1)} %slice.829), channel_id=1, source_target_pairs={{0,7},{1,0},{2,1},{3,2},{4,3},{5,4},{6,5},{7,6},{8,15},{9,8},{10,9... | collective-permute-start | bytes 110600 | tf_op jit(solution)/shard_map/ppermute | solution.py:22
  446.7 4.2 collective-permute-start.19
  447.8 3.1 collective-permute-start.20
  520.2 26.0 %all-to-all-start.7 = ((f32[128,1,2304]{2,1,0:T(1,128)}), f32[128,1,2304]{2,1,0:T(1,128)}, u32[]{:S(2)}, u32[]{:S(2)}) async-start(f32[128,1,2304]{2,1,0:T(1,128)} %all_to_all.71), calls=%async_computation.7 | async-start | bytes 2359296 | tf_op jit(solution)/shard_map/all_to_all | solution.py:83
  571.8 6.9 %collective-permute-start.21 = (f32[12,12,64]{2,1,0:T(8,128)S(1)}, f32[12,12,64]{2,1,0:T(8,128)S(1)}, u32[]{:S(2)}, u32[]{:S(2)}) collective-permute-start(f32[12,12,64]{2,1,0:T(8,128)S(1)} %slice_bitcast_fusion.1), channel_id=1, source_target_pairs={{0,1},{1,2},{2,3},{3,4},{4,5},{5,6},{6,7},{7,0},{8,9},{9,10},{10,1... | collective-permute-start | bytes 110600 | tf_op jit(solution)/shard_map/ppermute | solution.py:22
  572.0 7.2 %collective-permute-start.22 = (f32[6,12,64]{2,1,0:T(8,128)S(1)}, f32[6,12,64]{2,1,0:T(8,128)S(1)}, u32[]{:S(2)}, u32[]{:S(2)}) collective-permute-start(f32[6,12,64]{2,1,0:T(8,128)S(1)} %slice_bitcast_fusion.5), channel_id=1, source_target_pairs={{0,8},{8,16},{16,24},{24,32},{32,40},{40,48},{48,56},{56,64},{64,7... | collective-permute-start | bytes 55304 | tf_op jit(solution)/shard_map/ppermute | solution.py:22
  572.0 9.9 %collective-permute-start.23 = (f32[12,64]{1,0:T(8,128)S(1)}, f32[12,64]{1,0:T(8,128)S(1)}, u32[]{:S(2)}, u32[]{:S(2)}) collective-permute-start(f32[12,64]{1,0:T(8,128)S(1)} %slice_bitcast_fusion.9), channel_id=1, source_target_pairs={{0,9},{1,10},{2,11},{3,12},{4,13},{5,14},{6,15},{7,8},{8,17},{9,18... | collective-permute-start | bytes 9224 | tf_op jit(solution)/shard_map/ppermute | solution.py:33
  (4 other events, 36.4 us)

commit v3 on v2

--- a/solution.py
+++ b/solution.py
@@ -10,6 +10,7 @@
 CZ = 2
 FILTERS = 2
 ZN = 12
+CAP = 2
 
 
 PRECISE = lax.Precision.HIGHEST
@@ -72,22 +73,34 @@
     cells = CX * CY * CZ
     owners = lax.axis_size(("gx", "gy"))
     local_pot = potential.reshape(rows_x, rows_y, ZN, 1)
-    tile_flat = pair_tile[0].reshape(slots * nproj, npc)
     cell_mask = (pair_cell[0][:, None] == jnp.arange(cells, dtype=jnp.int32)[None, :]).astype(jnp.float32)
-    row_mask = jnp.repeat(cell_mask, nproj, axis=0)[:, :, None]
     one_hot = (
         slot_atom[0][:, None] == jnp.arange(atoms, dtype=jnp.int32)[None, :]
     ).astype(jnp.float32)
+    rows = -(-nproj // 8) * 8
+    tiles = pair_tile[0].reshape(owners, CAP, nproj, npc)
+    tiles = jnp.pad(tiles, ((0, 0), (0, 0), (0, rows - nproj), (0, 0)))
+    tile_k = [tiles[:, k].reshape(owners * rows, npc) for k in range(CAP)]
+    slot_cells = cell_mask.reshape(owners, CAP, cells)
+    mask_k = [slot_cells[:, k][:, None, :, None] for k in range(CAP)]
+    incoming = one_hot.reshape(owners, CAP, atoms)
+    hot_k = [incoming[:, k] for k in range(CAP)]
+    coupling_pad = jnp.pad(coupling, ((0, 0), (0, rows - nproj), (0, rows - nproj)))
 
     def exchange(values):
         return lax.all_to_all(values, ("gx", "gy"), split_axis=0, concat_axis=0, tiled=True)
 
     def owner_work(received):
-        atom_sums = lax.dot_general(
-            one_hot, received, (((0,), (0,)), ((), ())), precision=PRECISE
-        ).reshape(atoms, nproj, W)
-        applied = jnp.einsum("apq,aqw->apw", coupling, atom_sums, precision=PRECISE)
-        return jnp.dot(one_hot, applied.reshape(atoms, nproj * W), precision=PRECISE)
+        atom_sums = None
+        for k in range(CAP):
+            full = jnp.einsum("sa,spx->apx", hot_k[k], received, precision=PRECISE)
+            part = full[:, :, k * W : (k + 1) * W]
+            atom_sums = part if atom_sums is None else atom_sums + part
+        applied = jnp.einsum("apq,aqw->apw", coupling_pad, atom_sums, precision=PRECISE)
+        return jnp.concatenate(
+            [jnp.einsum("sa,apw->spw", hot_k[k], applied, precision=PRECISE) for k in range(CAP)],
+            axis=-1,
+        )
 
     def apply_operator(current):
         face_x = shifted(current[:1], "gx", -1)
@@ -101,16 +114,19 @@
             axis=0,
         )
         cell_in = gather_cells(extended)
-        every_cell = jnp.dot(tile_flat, cell_in, precision=DENSE)
-        projected = (every_cell.reshape(slots * nproj, cells, W) * row_mask).sum(axis=1)
-        received = exchange(projected.reshape(owners, -1)).reshape(slots, nproj * W)
-        returned = exchange(owner_work(received).reshape(owners, -1))
-        spread_in = (returned.reshape(slots * nproj, 1, W) * row_mask).reshape(slots * nproj, cells * W)
-        kinetic = jnp.dot(cell_matrix, cell_in, precision=DENSE)
-        spread = lax.dot_general(
-            tile_flat, spread_in, (((0,), (0,)), ((), ())), precision=DENSE
-        )
-        summed = scatter_cells(kinetic + spread, W)
+        parts = []
+        for k in range(CAP):
+            every_cell = jnp.dot(tile_k[k], cell_in, precision=DENSE)
+            parts.append((every_cell.reshape(owners, rows, cells, W) * mask_k[k]).sum(axis=2))
+        returned = exchange(owner_work(exchange(jnp.concatenate(parts, axis=-1))))
+        spread = jnp.dot(cell_matrix, cell_in, precision=DENSE)
+        for k in range(CAP):
+            part = returned[:, :, k * W : (k + 1) * W]
+            spread_in = (part[:, :, None, :] * mask_k[k]).reshape(owners * rows, cells * W)
+            spread = spread + lax.dot_general(
+                tile_k[k], spread_in, (((0,), (0,)), ((), ())), precision=DENSE
+            )
+        summed = scatter_cells(spread, W)
         from_y = shifted(summed[:rows_x, rows_y], "gy", 1)
         from_x = shifted(summed[rows_x, :rows_y], "gx", 1)
         from_corner = diagonal(summed[rows_x, rows_y], 1)

time: 593 us -> 682 us (1.15)
  local copies, waits for them, and re-layouts: 148 us -> 233 us
  other arithmetic: 57.3 us -> 28 us
  matrix products: 96.1 us -> 114 us
  blocking collectives: 85.9 us -> 97.5 us
    mul x9 -> x17, local copies, waits for them, and re-layouts: 21.4 us -> 112 us  [the longest x16 112 us: apply_operator(): part[:, :, None, :] * mask_k[k]]
    slice x0 -> x19, local copies, waits for them, and re-layouts: none -> 42.6 us  [the longest x12 21.9 us: apply_operator(): part = returned[:, :, k * W:(k + 1) * W]]
    all_to_all x8 -> x0, other arithmetic: 38.9 us -> none  [exchange(): lax.all_to_all(values, ('gx', 'gy'), split_axis=0, concat_axis=0, tiled=T...]
    all_to_all x8 -> x0, local copies, waits for them, and re-layouts: 26.7 us -> none  [exchange(): lax.all_to_all(values, ('gx', 'gy'), split_axis=0, concat_axis=0, tiled=T...]
    reshape x8 -> x0, local copies, waits for them, and re-layouts: 14.9 us -> none  [the longest x4 8.94 us: apply_operator(): received = exchange(projected.reshape(owners, -1)).reshape(slots, nproj * W)]
    mul x4 -> x7, other arithmetic: 5.99 us -> 20.5 us  [apply_operator(): part[:, :, None, :] * mask_k[k]]
    dot_general x24 -> x32, matrix products: 96.1 us -> 110 us  [the longest x8 58.2 us: apply_operator(): lax.dot_general(tile_k[k], spread_in, (((0,), (0,)), ((), ())), precision...]
    concatenate x0 -> x8, local copies, waits for them, and re-layouts: none -> 13.2 us  [the longest x4 6.61 us: apply_operator(): returned = exchange(owner_work(exchange(jnp.concatenate(parts, axis=-1))))]
  transfers between devices with their start and end apart: 29 -> 29, of which waited for: 20 -> 20; matrix products, arithmetic and copies ran while one was open for 6% -> 10% of each run, Pallas kernels for 0% -> 0%
where the time goes in v3:
time: 682 us; the launch traced here: 670 us
  local copies, waits for them, and re-layouts  233 us (34%)
  waiting for transfers between devices  139 us (20%)
  matrix products  114 us (17%)
  blocking collectives  97.5 us (14%)
  starting transfers between devices  49.8 us (7%)
  other arithmetic  28 us (4%)
  between operations  8.73 us (1%)
    mul x16, local copies, waits for them, and re-layouts, apply_operator(): part[:, :, None, :] * mask_k[k]  112 us
    all_to_all x3, blocking collectives, exchange(): lax.all_to_all(values, ('gx', 'gy'), split_axis=0, concat_axis=0, tiled=T...  97.5 us
    all_to_all x5, waiting for transfers between devices, exchange(): lax.all_to_all(values, ('gx', 'gy'), split_axis=0, concat_axis=0, tiled=T...  95.6 us
    dot_general x8, matrix products, apply_operator(): lax.dot_general(tile_k[k], spread_in, (((0,), (0,)), ((), ())), precision...  58.2 us
    dot_general x8, matrix products, apply_operator(): every_cell = jnp.dot(tile_k[k], cell_in, precision=DENSE)  36.2 us
    all_to_all x5, starting transfers between devices, exchange(): lax.all_to_all(values, ('gx', 'gy'), split_axis=0, concat_axis=0, tiled=T...  24.2 us
    ppermute x16, waiting for transfers between devices, shifted(): return lax.ppermute(value, axis, pairs)  22.6 us
    slice x12, local copies, waits for them, and re-layouts, apply_operator(): part = returned[:, :, k * W:(k + 1) * W]  21.9 us
  transfers between devices with their start and end apart: 29, of which 20 were waited for; matrix products, arithmetic and copies ran while one was open for 10% of the time, Pallas kernels for 0%

profile of v3, /device:TPU:0, one launch (start us, length us, event | category | flops | bytes accessed | tf_op | source)
XLA Modules:
  0.0 669.8 jit_solution(13716009974558265208)
XLA Ops:
  15.2 16.6 %copy.166 = f32[1,256,18,343]{3,1,2,0:T(8,128)} copy(f32[1,256,18,343]{1,0,3,2:T(1,128)} %param.44) | data formatting | bytes 12644352 | tf_op args[4]
  31.8 9.4 %reshape_squeeze.9 = f32[128,2,18,343]{3,1,0,2:T(2,128)} reshape(f32[1,256,18,343]{3,1,2,0:T(8,128)} %copy.166) | data formatting | bytes 12644352 | tf_op jit(solution)/shard_map/reshape;squeeze | solution.py:81
  41.1 12.1 %copy.167 = f32[128,2,18,343]{0,3,2,1:T(8,128)} copy(f32[128,2,18,343]{3,1,0,2:T(2,128)} %reshape_squeeze.9) | data formatting | bytes 12644352 | tf_op jit(solution)/shard_map/reshape;squeeze | solution.py:81
  69.9 23.3 %all-to-all-done = f32[128,24,128]{2,1,0:T(8,128)S(1)} async-done(((f32[128,24,128]{2,1,0:T(8,128)}), f32[128,24,128]{2,1,0:T(8,128)S(1)}, u32[]{:S(2)}, u32[]{:S(2)}) %all-to-all-start) | async-done | bytes 1572896 | tf_op jit(solution)/shard_map/all_to_all | solution.py:91
  135.7 6.9 %copy.181 = f32[128,24,4,64]{3,2,1,0:T(4,128)} copy(f32[128,24,4,64]{0,3,2,1:T(8,128)} %broadcast_multiply_fusion.7) | data formatting | bytes 6291456 | tf_op jit(solution)/shard_map/mul | solution.py:125
  142.6 7.0 %mul.334 = f32[3072,256]{1,0:T(8,128)} reshape(f32[128,24,4,64]{3,2,1,0:T(4,128)} %copy.181) | data formatting | bytes 6291456 | tf_op jit(solution)/shard_map/mul | solution.py:125
  154.2 6.9 %copy.184 = f32[128,24,4,64]{3,2,1,0:T(4,128)} copy(f32[128,24,4,64]{0,3,2,1:T(8,128)} %broadcast_multiply_fusion.6) | data formatting | bytes 6291456 | tf_op jit(solution)/shard_map/mul | solution.py:125
  161.2 7.3 %mul.337 = f32[3072,256]{1,0:T(8,128)} reshape(f32[128,24,4,64]{3,2,1,0:T(4,128)} %copy.184) | data formatting | bytes 6291456 | tf_op jit(solution)/shard_map/mul | solution.py:125
  168.5 7.3 %fusion.170 = f32[343,256]{1,0:T(8,128)S(1)} fusion(f32[3072,343]{1,0:T(8,128)} %bitcast.336, f32[3072,256]{1,0:T(8,128)} %mul.334), kind=kOutput, calls=%fused_computation.275 | convolution fusion | flops 1618477056 | bytes 7711744 | tf_op jit(solution)/shard_map/dot_general | solution.py:126
  215.3 32.5 %all_to_all.40 = f32[128,24,128]{2,1,0:T(8,128)S(1)} all-to-all(f32[128,24,128]{2,1,0:T(8,128)} %copy.192), channel_id=1, replica_groups=mesh['gx'=16,'gy'=8] {'gx','gy'}, dimensions={0} | all-to-all | bytes 3145728 | tf_op jit(solution)/shard_map/all_to_all | solution.py:91
  260.0 24.5 %all-to-all-done.3 = f32[128,24,128]{2,1,0:T(8,128)S(1)} async-done(((f32[128,24,128]{2,1,0:T(8,128)}), f32[128,24,128]{2,1,0:T(8,128)S(1)}, u32[]{:S(2)}, u32[]{:S(2)}) %all-to-all-start.3) | async-done | bytes 1572896 | tf_op jit(solution)/shard_map/all_to_all | solution.py:91
  290.5 6.9 %copy.200 = f32[128,24,4,64]{3,2,1,0:T(4,128)} copy(f32[128,24,4,64]{0,3,2,1:T(8,128)} %broadcast_multiply_fusion.5) | data formatting | bytes 6291456 | tf_op jit(solution)/shard_map/mul | solution.py:125
  297.4 6.9 %mul.348 = f32[3072,256]{1,0:T(8,128)} reshape(f32[128,24,4,64]{3,2,1,0:T(4,128)} %copy.200) | data formatting | bytes 6291456 | tf_op jit(solution)/shard_map/mul | solution.py:125
  304.3 8.0 %fusion.172 = f32[343,256]{1,0:T(8,128)} fusion(f32[3072,343]{1,0:T(8,128)} %bitcast.337, f32[3072,256]{1,0:T(8,128)} %mul.348), kind=kOutput, calls=%fused_computation.277 | convolution fusion | flops 1618477056 | bytes 7711744 | tf_op jit(solution)/shard_map/dot_general | solution.py:126
  323.8 7.3 %mul.351 = f32[3072,256]{1,0:T(8,128)} reshape(f32[128,24,4,64]{3,2,1,0:T(4,128)} %copy.202) | data formatting | bytes 6291456 | tf_op jit(solution)/shard_map/mul | solution.py:125
  331.1 7.2 %fusion.173 = f32[343,256]{1,0:T(8,128)S(1)} fusion(f32[3072,343]{1,0:T(8,128)} %bitcast.333, f32[3072,256]{1,0:T(8,128)} %mul.351), kind=kOutput, calls=%fused_computation.278 | convolution fusion | flops 1618477056 | bytes 7711744 | tf_op jit(solution)/shard_map/dot_general | solution.py:126
  376.0 32.5 %all_to_all.41 = f32[128,24,128]{2,1,0:T(8,128)S(1)} all-to-all(f32[128,24,128]{2,1,0:T(8,128)} %copy.210), channel_id=1, replica_groups=mesh['gx'=16,'gy'=8] {'gx','gy'}, dimensions={0} | all-to-all | bytes 3145728 | tf_op jit(solution)/shard_map/all_to_all | solution.py:91
  423.5 21.5 %all-to-all-done.5 = f32[128,24,128]{2,1,0:T(8,128)S(1)} async-done(((f32[128,24,128]{2,1,0:T(8,128)}), f32[128,24,128]{2,1,0:T(8,128)S(1)}, u32[]{:S(2)}, u32[]{:S(2)}) %all-to-all-start.5) | async-done | bytes 1572896 | tf_op jit(solution)/shard_map/all_to_all | solution.py:91
  451.2 6.9 %copy.218 = f32[128,24,4,64]{3,2,1,0:T(4,128)} copy(f32[128,24,4,64]{0,3,2,1:T(8,128)} %broadcast_multiply_fusion.3) | data formatting | bytes 6291456 | tf_op jit(solution)/shard_map/mul | solution.py:125
  458.1 6.9 %mul.362 = f32[3072,256]{1,0:T(8,128)} reshape(f32[128,24,4,64]{3,2,1,0:T(4,128)} %copy.218) | data formatting | bytes 6291456 | tf_op jit(solution)/shard_map/mul | solution.py:125
  465.0 8.0 %fusion.174 = f32[343,256]{1,0:T(8,128)} fusion(f32[3072,343]{1,0:T(8,128)} %bitcast.338, f32[3072,256]{1,0:T(8,128)} %mul.362), kind=kOutput, calls=%fused_computation.279 | convolution fusion | flops 1618477056 | bytes 7711744 | tf_op jit(solution)/shard_map/dot_general | solution.py:126
  477.6 6.9 %copy.220 = f32[128,24,4,64]{3,2,1,0:T(4,128)} copy(f32[128,24,4,64]{0,3,2,1:T(8,128)} %broadcast_multiply_fusion.2) | data formatting | bytes 6291456 | tf_op jit(solution)/shard_map/mul | solution.py:125
  484.5 7.3 %mul.365 = f32[3072,256]{1,0:T(8,128)} reshape(f32[128,24,4,64]{3,2,1,0:T(4,128)} %copy.220) | data formatting | bytes 6291456 | tf_op jit(solution)/shard_map/mul | solution.py:125
  491.8 7.2 %fusion.175 = f32[343,256]{1,0:T(8,128)S(1)} fusion(f32[3072,343]{1,0:T(8,128)} %bitcast.334, f32[3072,256]{1,0:T(8,128)} %mul.365), kind=kOutput, calls=%fused_computation.280 | convolution fusion | flops 1618477056 | bytes 7711744 | tf_op jit(solution)/shard_map/dot_general | solution.py:126
  532.3 32.5 %all_to_all.42 = f32[128,24,128]{2,1,0:T(8,128)S(1)} all-to-all(f32[128,24,128]{2,1,0:T(8,128)} %copy.228), channel_id=1, replica_groups=mesh['gx'=16,'gy'=8] {'gx','gy'}, dimensions={0} | all-to-all | bytes 3145728 | tf_op jit(solution)/shard_map/all_to_all | solution.py:91
  576.9 24.5 %all-to-all-done.7 = f32[128,24,128]{2,1,0:T(8,128)S(1)} async-done(((f32[128,24,128]{2,1,0:T(8,128)}), f32[128,24,128]{2,1,0:T(8,128)S(1)}, u32[]{:S(2)}, u32[]{:S(2)}) %all-to-all-start.7) | async-done | bytes 1572896 | tf_op jit(solution)/shard_map/all_to_all | solution.py:91
  611.5 6.9 %copy.236 = f32[128,24,4,64]{3,2,1,0:T(4,128)} copy(f32[128,24,4,64]{0,3,2,1:T(8,128)} %get-tuple-element.261) | data formatting | bytes 6291456 | tf_op jit(solution)/shard_map/mul | solution.py:125
  618.4 6.9 %mul.374 = f32[3072,256]{1,0:T(8,128)} reshape(f32[128,24,4,64]{3,2,1,0:T(4,128)} %copy.236) | data formatting | bytes 6291456 | tf_op jit(solution)/shard_map/mul | solution.py:125
  625.3 7.1 %fusion.176 = f32[343,256]{1,0:T(8,128)S(1)} fusion(f32[3072,343]{1,0:T(8,128)} %bitcast.339, f32[3072,256]{1,0:T(8,128)} %mul.374), kind=kOutput, calls=%fused_computation.281 | convolution fusion | flops 1618477056 | bytes 7711744 | tf_op jit(solution)/shard_map/dot_general | solution.py:126
  632.4 6.9 %copy.238 = f32[128,24,4,64]{3,2,1,0:T(4,128)} copy(f32[128,24,4,64]{0,3,2,1:T(8,128)} %get-tuple-element.260) | data formatting | bytes 6291456 | tf_op jit(solution)/shard_map/mul | solution.py:125
  639.3 7.2 %mul.377 = f32[3072,256]{1,0:T(8,128)} reshape(f32[128,24,4,64]{3,2,1,0:T(4,128)} %copy.238) | data formatting | bytes 6291456 | tf_op jit(solution)/shard_map/mul | solution.py:125
  646.5 7.2 %fusion.177 = f32[343,256]{1,0:T(8,128)S(1)} fusion(f32[3072,343]{1,0:T(8,128)} %bitcast.335, f32[3072,256]{1,0:T(8,128)} %mul.377), kind=kOutput, calls=%fused_computation.282 | convolution fusion | flops 1618477056 | bytes 7711744 | tf_op jit(solution)/shard_map/dot_general | solution.py:126
  (303 shorter events, 274.6 us)
Async XLA Ops:
  0.0 182.1 %copy-start = (f32[343,343]{1,0:T(8,128)S(1)}, f32[343,343]{1,0:T(8,128)}, u32[]{:S(2)}) copy-start(f32[343,343]{1,0:T(8,128)} %param.42) | copy-start | bytes 1411792
  1.2 30.6 %copy-start.5 = (f32[12,6,12,64]{3,2,1,0:T(8,128)}, f32[12,6,12,64]{3,2,1,0:T(8,128)S(1)}, u32[]{:S(2)}) copy-start(f32[12,6,12,64]{3,2,1,0:T(8,128)S(1)} %reshape.761) | copy-start | bytes 663556
  1.2 52.0 %collective-permute-start = (f32[12,1,12,64]{3,2,1,0:T(8,128)S(1)}, f32[12,1,12,64]{3,2,1,0:T(8,128)S(1)}, u32[]{:S(2)}, u32[]{:S(2)}) collective-permute-start(f32[12,1,12,64]{3,2,1,0:T(8,128)S(1)} %slice.880), channel_id=1, source_target_pairs={{0,7},{1,0},{2,1},{3,2},{4,3},{5,4},{6,5},{7,6},{8,15},{9,8},{10,9... | collective-permute-start | bytes 110600 | tf_op jit(solution)/shard_map/ppermute | solution.py:23
  5.3 47.9 %collective-permute-start.2 = (f32[1,1,12,64]{3,2,1,0:T(8,128)S(1)}, f32[1,1,12,64]{3,2,1,0:T(8,128)S(1)}, u32[]{:S(2)}, u32[]{:S(2)}) collective-permute-start(f32[1,1,12,64]{3,2,1,0:T(8,128)S(1)} %slice.882), channel_id=1, source_target_pairs={{0,127},{1,120},{2,121},{3,122},{4,123},{5,124},{6,125},{7,126},{8... | collective-permute-start | bytes 9224 | tf_op jit(solution)/shard_map/ppermute | solution.py:34
  11.0 42.2 %collective-permute-start.1 = (f32[1,6,12,64]{3,2,1,0:T(8,128)S(1)}, f32[1,6,12,64]{3,2,1,0:T(8,128)S(1)}, u32[]{:S(2)}, u32[]{:S(2)}) collective-permute-start(f32[1,6,12,64]{3,2,1,0:T(8,128)S(1)} %slice.764), channel_id=1, source_target_pairs={{0,120},{8,0},{16,8},{24,16},{32,24},{40,32},{48,40},{56,48},{64,5... | collective-permute-start | bytes 55304 | tf_op jit(solution)/shard_map/ppermute | solution.py:23
  63.8 29.5 %all-to-all-start = ((f32[128,24,128]{2,1,0:T(8,128)}), f32[128,24,128]{2,1,0:T(8,128)S(1)}, u32[]{:S(2)}, u32[]{:S(2)}) async-start(f32[128,24,128]{2,1,0:T(8,128)} %copy.173), calls=%async_computation | async-start | bytes 3145728 | tf_op jit(solution)/shard_map/all_to_all | solution.py:91
  100.3 29.3 %all-to-all-start.1 = ((f32[128,24,128]{2,1,0:T(8,128)}), f32[128,24,128]{2,1,0:T(8,128)S(1)}, u32[]{:S(2)}, u32[]{:S(2)}) async-start(f32[128,24,128]{2,1,0:T(8,128)} %copy.179), calls=%async_computation.1 | async-start | bytes 3145728 | tf_op jit(solution)/shard_map/all_to_all | solution.py:91
  186.3 6.9 %collective-permute-start.3 = (f32[12,12,64]{2,1,0:T(8,128)S(1)}, f32[12,12,64]{2,1,0:T(8,128)S(1)}, u32[]{:S(2)}, u32[]{:S(2)}) collective-permute-start(f32[12,12,64]{2,1,0:T(8,128)S(1)} %slice_bitcast_fusion.4), channel_id=1, source_target_pairs={{0,1},{1,2},{2,3},{3,4},{4,5},{5,6},{6,7},{7,0},{8,9},{9,10},{10,1... | collective-permute-start | bytes 110600 | tf_op jit(solution)/shard_map/ppermute | solution.py:23
  186.5 7.2 %collective-permute-start.4 = (f32[6,12,64]{2,1,0:T(8,128)S(1)}, f32[6,12,64]{2,1,0:T(8,128)S(1)}, u32[]{:S(2)}, u32[]{:S(2)}) collective-permute-start(f32[6,12,64]{2,1,0:T(8,128)S(1)} %slice_bitcast_fusion.8), channel_id=1, source_target_pairs={{0,8},{8,16},{16,24},{24,32},{32,40},{40,48},{48,56},{56,64},{64,7... | collective-permute-start | bytes 55304 | tf_op jit(solution)/shard_map/ppermute | solution.py:23
  186.6 10.0 %collective-permute-start.5 = (f32[12,64]{1,0:T(8,128)S(1)}, f32[12,64]{1,0:T(8,128)S(1)}, u32[]{:S(2)}, u32[]{:S(2)}) collective-permute-start(f32[12,64]{1,0:T(8,128)S(1)} %slice_bitcast_fusion.12), channel_id=1, source_target_pairs={{0,9},{1,10},{2,11},{3,12},{4,13},{5,14},{6,15},{7,8},{8,17},{9,18... | collective-permute-start | bytes 9224 | tf_op jit(solution)/shard_map/ppermute | solution.py:34
  196.8 6.2 collective-permute-start.6
  198.7 4.3 collective-permute-start.7
  199.8 3.2 collective-permute-start.8
  254.9 29.5 %all-to-all-start.3 = ((f32[128,24,128]{2,1,0:T(8,128)}), f32[128,24,128]{2,1,0:T(8,128)S(1)}, u32[]{:S(2)}, u32[]{:S(2)}) async-start(f32[128,24,128]{2,1,0:T(8,128)} %copy.198), calls=%async_computation.3 | async-start | bytes 3145728 | tf_op jit(solution)/shard_map/all_to_all | solution.py:91
  339.7 17.5 %copy-start.7 = (f32[12,6,12,64]{3,2,1,0:T(8,128)S(1)}, f32[12,6,12,64]{3,2,1,0:T(8,128)}, u32[]{:S(2)}) copy-start(f32[12,6,12,64]{3,2,1,0:T(8,128)} %copy-done.5) | copy-start | bytes 663556
  345.3 6.7 %collective-permute-start.9 = (f32[12,12,64]{2,1,0:T(8,128)S(1)}, f32[12,12,64]{2,1,0:T(8,128)S(1)}, u32[]{:S(2)}, u32[]{:S(2)}) collective-permute-start(f32[12,12,64]{2,1,0:T(8,128)S(1)} %slice_bitcast_fusion.3), channel_id=1, source_target_pairs={{0,1},{1,2},{2,3},{3,4},{4,5},{5,6},{6,7},{7,0},{8,9},{9,10},{10,1... | collective-permute-start | bytes 110600 | tf_op jit(solution)/shard_map/ppermute | solution.py:23
  347.1 7.2 %collective-permute-start.10 = (f32[6,12,64]{2,1,0:T(8,128)S(1)}, f32[6,12,64]{2,1,0:T(8,128)S(1)}, u32[]{:S(2)}, u32[]{:S(2)}) collective-permute-start(f32[6,12,64]{2,1,0:T(8,128)S(1)} %slice_bitcast_fusion.7), channel_id=1, source_target_pairs={{0,8},{8,16},{16,24},{24,32},{32,40},{40,48},{48,56},{56,64},{64,7... | collective-permute-start | bytes 55304 | tf_op jit(solution)/shard_map/ppermute | solution.py:23
  347.2 10.0 %collective-permute-start.11 = (f32[12,64]{1,0:T(8,128)S(1)}, f32[12,64]{1,0:T(8,128)S(1)}, u32[]{:S(2)}, u32[]{:S(2)}) collective-permute-start(f32[12,64]{1,0:T(8,128)S(1)} %slice_bitcast_fusion.11), channel_id=1, source_target_pairs={{0,9},{1,10},{2,11},{3,12},{4,13},{5,14},{6,15},{7,8},{8,17},{9,18... | collective-permute-start | bytes 9224 | tf_op jit(solution)/shard_map/ppermute | solution.py:34
  357.4 6.2 collective-permute-start.12
  359.3 4.3 collective-permute-start.13
  360.4 3.2 collective-permute-start.14
  415.5 29.5 %all-to-all-start.5 = ((f32[128,24,128]{2,1,0:T(8,128)}), f32[128,24,128]{2,1,0:T(8,128)S(1)}, u32[]{:S(2)}, u32[]{:S(2)}) async-start(f32[128,24,128]{2,1,0:T(8,128)} %copy.216), calls=%async_computation.5 | async-start | bytes 3145728 | tf_op jit(solution)/shard_map/all_to_all | solution.py:91
  503.3 6.9 %collective-permute-start.15 = (f32[12,12,64]{2,1,0:T(8,128)S(1)}, f32[12,12,64]{2,1,0:T(8,128)S(1)}, u32[]{:S(2)}, u32[]{:S(2)}) collective-permute-start(f32[12,12,64]{2,1,0:T(8,128)S(1)} %slice_bitcast_fusion.2), channel_id=1, source_target_pairs={{0,1},{1,2},{2,3},{3,4},{4,5},{5,6},{6,7},{7,0},{8,9},{9,10},{10,1... | collective-permute-start | bytes 110600 | tf_op jit(solution)/shard_map/ppermute | solution.py:23
  503.4 7.2 %collective-permute-start.16 = (f32[6,12,64]{2,1,0:T(8,128)S(1)}, f32[6,12,64]{2,1,0:T(8,128)S(1)}, u32[]{:S(2)}, u32[]{:S(2)}) collective-permute-start(f32[6,12,64]{2,1,0:T(8,128)S(1)} %slice_bitcast_fusion.6), channel_id=1, source_target_pairs={{0,8},{8,16},{16,24},{24,32},{32,40},{40,48},{48,56},{56,64},{64,7... | collective-permute-start | bytes 55304 | tf_op jit(solution)/shard_map/ppermute | solution.py:23
  503.5 9.9 %collective-permute-start.17 = (f32[12,64]{1,0:T(8,128)S(1)}, f32[12,64]{1,0:T(8,128)S(1)}, u32[]{:S(2)}, u32[]{:S(2)}) collective-permute-start(f32[12,64]{1,0:T(8,128)S(1)} %slice_bitcast_fusion.10), channel_id=1, source_target_pairs={{0,9},{1,10},{2,11},{3,12},{4,13},{5,14},{6,15},{7,8},{8,17},{9,18... | collective-permute-start | bytes 9224 | tf_op jit(solution)/shard_map/ppermute | solution.py:34
  513.7 6.2 collective-permute-start.18
  515.6 4.3 collective-permute-start.19
  516.7 3.2 collective-permute-start.20
  571.8 29.5 %all-to-all-start.7 = ((f32[128,24,128]{2,1,0:T(8,128)}), f32[128,24,128]{2,1,0:T(8,128)S(1)}, u32[]{:S(2)}, u32[]{:S(2)}) async-start(f32[128,24,128]{2,1,0:T(8,128)} %copy.234), calls=%async_computation.7 | async-start | bytes 3145728 | tf_op jit(solution)/shard_map/all_to_all | solution.py:91
  658.0 6.9 %collective-permute-start.21 = (f32[12,12,64]{2,1,0:T(8,128)S(1)}, f32[12,12,64]{2,1,0:T(8,128)S(1)}, u32[]{:S(2)}, u32[]{:S(2)}) collective-permute-start(f32[12,12,64]{2,1,0:T(8,128)S(1)} %slice_bitcast_fusion.1), channel_id=1, source_target_pairs={{0,1},{1,2},{2,3},{3,4},{4,5},{5,6},{6,7},{7,0},{8,9},{9,10},{10,1... | collective-permute-start | bytes 110600 | tf_op jit(solution)/shard_map/ppermute | solution.py:23
  658.1 7.2 %collective-permute-start.22 = (f32[6,12,64]{2,1,0:T(8,128)S(1)}, f32[6,12,64]{2,1,0:T(8,128)S(1)}, u32[]{:S(2)}, u32[]{:S(2)}) collective-permute-start(f32[6,12,64]{2,1,0:T(8,128)S(1)} %slice_bitcast_fusion.5), channel_id=1, source_target_pairs={{0,8},{8,16},{16,24},{24,32},{32,40},{40,48},{48,56},{56,64},{64,7... | collective-permute-start | bytes 55304 | tf_op jit(solution)/shard_map/ppermute | solution.py:23
  658.2 9.9 %collective-permute-start.23 = (f32[12,64]{1,0:T(8,128)S(1)}, f32[12,64]{1,0:T(8,128)S(1)}, u32[]{:S(2)}, u32[]{:S(2)}) collective-permute-start(f32[12,64]{1,0:T(8,128)S(1)} %slice_bitcast_fusion.9), channel_id=1, source_target_pairs={{0,9},{1,10},{2,11},{3,12},{4,13},{5,14},{6,15},{7,8},{8,17},{9,18... | collective-permute-start | bytes 9224 | tf_op jit(solution)/shard_map/ppermute | solution.py:34
  (21 other events, 147.7 us)

commit v4 on v3

--- a/solution.py
+++ b/solution.py
@@ -78,11 +78,14 @@
         slot_atom[0][:, None] == jnp.arange(atoms, dtype=jnp.int32)[None, :]
     ).astype(jnp.float32)
     rows = -(-nproj // 8) * 8
-    tiles = pair_tile[0].reshape(owners, CAP, nproj, npc)
-    tiles = jnp.pad(tiles, ((0, 0), (0, 0), (0, rows - nproj), (0, 0)))
-    tile_k = [tiles[:, k].reshape(owners * rows, npc) for k in range(CAP)]
+    tile_set = pair_tile[0]
+    tile_k = [
+        jnp.pad(tile_set[k::CAP], ((0, 0), (0, rows - nproj), (0, 0))).reshape(owners * rows, npc)
+        for k in range(CAP)
+    ]
+    tile_t = [tile.T for tile in tile_k]
     slot_cells = cell_mask.reshape(owners, CAP, cells)
-    mask_k = [slot_cells[:, k][:, None, :, None] for k in range(CAP)]
+    mask_k = [jnp.repeat(slot_cells[:, k], rows, axis=0) for k in range(CAP)]
     incoming = one_hot.reshape(owners, CAP, atoms)
     hot_k = [incoming[:, k] for k in range(CAP)]
     coupling_pad = jnp.pad(coupling, ((0, 0), (0, rows - nproj), (0, rows - nproj)))
@@ -117,15 +120,19 @@
         parts = []
         for k in range(CAP):
             every_cell = jnp.dot(tile_k[k], cell_in, precision=DENSE)
-            parts.append((every_cell.reshape(owners, rows, cells, W) * mask_k[k]).sum(axis=2))
+            picked = None
+            for c in range(cells):
+                term = every_cell[:, c * W : (c + 1) * W] * mask_k[k][:, c : c + 1]
+                picked = term if picked is None else picked + term
+            parts.append(picked.reshape(owners, rows, W))
         returned = exchange(owner_work(exchange(jnp.concatenate(parts, axis=-1))))
         spread = jnp.dot(cell_matrix, cell_in, precision=DENSE)
         for k in range(CAP):
-            part = returned[:, :, k * W : (k + 1) * W]
-            spread_in = (part[:, :, None, :] * mask_k[k]).reshape(owners * rows, cells * W)
-            spread = spread + lax.dot_general(
-                tile_k[k], spread_in, (((0,), (0,)), ((), ())), precision=DENSE
+            part = returned[:, :, k * W : (k + 1) * W].reshape(owners * rows, W)
+            spread_in = jnp.concatenate(
+                [part * mask_k[k][:, c : c + 1] for c in range(cells)], axis=1
             )
+            spread = spread + jnp.dot(tile_t[k], spread_in, precision=DENSE)
         summed = scatter_cells(spread, W)
         from_y = shifted(summed[:rows_x, rows_y], "gy", 1)
         from_x = shifted(summed[rows_x, :rows_y], "gx", 1)

time: 682 us -> 795 us (1.17); the launches traced: 670 us -> 791 us
  local copies, waits for them, and re-layouts: 233 us -> 331 us
  waiting for transfers between devices: 139 us -> 158 us
  other arithmetic: 28 us -> 43.3 us
  matrix products: 114 us -> 102 us
    slice x15 -> x8, local copies, waits for them, and re-layouts: 40.6 us -> 232 us  [the longest x2 219 us: body(): tile_set[k::CAP]]
    mul x17 -> x0, local copies, waits for them, and re-layouts: 112 us -> none  [the longest x16 112 us: apply_operator(): part[:, :, None, :] * mask_k[k]]
    another operation x2 -> x0, local copies, waits for them, and re-layouts: 21.4 us -> none  [body(): tiles = pair_tile[0].reshape(owners, CAP, nproj, npc)]
    all_to_all x5, waiting for transfers between devices: 95.6 us -> 113 us  [exchange(): lax.all_to_all(values, ('gx', 'gy'), split_axis=0, concat_axis=0, tiled=T...]
    reshape x0 -> x10, local copies, waits for them, and re-layouts: none -> 16.3 us  [the longest x8 15.9 us: apply_operator(): part = returned[:, :, k * W:(k + 1) * W].reshape(owners * rows, W)]
    add x0 -> x8, local copies, waits for them, and re-layouts: none -> 15.4 us  [apply_operator(): picked = term if picked is None else picked + term]
    dot_general x8, matrix products: 58.2 us -> 43.4 us  [apply_operator(): spread = spread + jnp.dot(tile_t[k], spread_in, precision=DENSE)]
    add x0 -> x8, other arithmetic: none -> 11 us  [apply_operator(): picked = term if picked is None else picked + term]
  transfers between devices with their start and end apart: 29 -> 29, of which waited for: 20 -> 20; matrix products, arithmetic and copies ran while one was open for 10% -> 32% of each run, Pallas kernels for 0% -> 0%
where the time goes in v4:
time: 795 us; the launch traced here: 791 us
  local copies, waits for them, and re-layouts  331 us (42%)
  waiting for transfers between devices  158 us (20%)
  matrix products  102 us (13%)
  blocking collectives  97 us (12%)
  starting transfers between devices  51.5 us (6%)
  other arithmetic  43.3 us (5%)
  between operations  8.81 us (1%)
    slice x2, local copies, waits for them, and re-layouts, body(): tile_set[k::CAP]  219 us
    all_to_all x5, waiting for transfers between devices, exchange(): lax.all_to_all(values, ('gx', 'gy'), split_axis=0, concat_axis=0, tiled=T...  113 us
    all_to_all x3, blocking collectives, exchange(): lax.all_to_all(values, ('gx', 'gy'), split_axis=0, concat_axis=0, tiled=T...  97 us
    dot_general x8, matrix products, apply_operator(): spread = spread + jnp.dot(tile_t[k], spread_in, precision=DENSE)  43.4 us
    dot_general x8, matrix products, apply_operator(): every_cell = jnp.dot(tile_k[k], cell_in, precision=DENSE)  36.9 us
    all_to_all x5, starting transfers between devices, exchange(): lax.all_to_all(values, ('gx', 'gy'), split_axis=0, concat_axis=0, tiled=T...  26.1 us
    ppermute x16, waiting for transfers between devices, shifted(): return lax.ppermute(value, axis, pairs)  23.4 us
    ppermute x8, waiting for transfers between devices, diagonal(): return lax.ppermute(value, ('gx', 'gy'), pairs)  21.7 us
  transfers between devices with their start and end apart: 29, of which 20 were waited for; matrix products, arithmetic and copies ran while one was open for 32% of the time, Pallas kernels for 0%

profile of v4, /device:TPU:0, one launch (start us, length us, event | category | flops | bytes accessed | tf_op | source)
XLA Modules:
  0.0 790.8 jit_solution(16703805117779034336)
XLA Ops:
  5.3 4.6 collective-permute-start.2
  16.0 6.0 copy.401
  22.0 109.7 %slice.946 = f32[128,18,343]{0,2,1:T(8,128)} slice(f32[256,18,343]{0,2,1:T(8,128)} %bitcast.329), slice={[0:256:2], [0:18:1], [0:343:1]} | slice | bytes 6322176 | tf_op jit(solution)/shard_map/slice | solution.py:83
  131.7 109.2 %slice.957 = f32[128,18,343]{0,2,1:T(8,128)} slice(f32[256,18,343]{0,2,1:T(8,128)} %bitcast.330), slice={[1:256:2], [0:18:1], [0:343:1]} | slice | bytes 6322176 | tf_op jit(solution)/shard_map/slice | solution.py:83
  240.9 5.2 copy.342
  246.2 5.2 copy.343
  251.4 5.0 pad.103.clone
  259.7 4.8 fusion.236
  274.8 4.6 all-to-all-start
  281.7 22.4 %all-to-all-done = f32[128,24,128]{2,1,0:T(8,128)S(1)} async-done(((f32[128,24,128]{2,1,0:T(8,128)}), f32[128,24,128]{2,1,0:T(8,128)S(1)}, u32[]{:S(2)}, u32[]{:S(2)}) %all-to-all-start) | async-done | bytes 1572896 | tf_op jit(solution)/shard_map/all_to_all | solution.py:94
  311.1 4.9 all-to-all-start.1
  319.9 20.7 %all-to-all-done.1 = f32[128,24,128]{2,1,0:T(8,128)S(1)} async-done(((f32[128,24,128]{2,1,0:T(8,128)}), f32[128,24,128]{2,1,0:T(8,128)S(1)}, u32[]{:S(2)}, u32[]{:S(2)}) %all-to-all-start.1) | async-done | bytes 1572896 | tf_op jit(solution)/shard_map/all_to_all | solution.py:94
  351.6 7.1 fusion
  368.3 5.3 collective-permute-done.3
  386.5 4.8 fusion.238
  406.1 32.4 %all_to_all.40 = f32[128,24,128]{2,1,0:T(8,128)S(1)} all-to-all(f32[128,24,128]{2,1,0:T(8,128)S(1)} %pad_maximum_fusion.2), channel_id=1, replica_groups=mesh['gx'=16,'gy'=8] {'gx','gy'}, dimensions={0} | all-to-all | bytes 3145728 | tf_op jit(solution)/shard_map/all_to_all | solution.py:94
  445.6 4.9 all-to-all-start.3
  450.6 24.5 %all-to-all-done.3 = f32[128,24,128]{2,1,0:T(8,128)S(1)} async-done(((f32[128,24,128]{2,1,0:T(8,128)}), f32[128,24,128]{2,1,0:T(8,128)S(1)}, u32[]{:S(2)}, u32[]{:S(2)}) %all-to-all-start.3) | async-done | bytes 1572896 | tf_op jit(solution)/shard_map/all_to_all | solution.py:94
  486.1 7.1 fusion.16
  504.1 5.3 collective-permute-done.9
  521.4 4.8 fusion.240
  538.7 32.2 %all_to_all.41 = f32[128,24,128]{2,1,0:T(8,128)S(1)} all-to-all(f32[128,24,128]{2,1,0:T(8,128)S(1)} %pad_maximum_fusion.4), channel_id=1, replica_groups=mesh['gx'=16,'gy'=8] {'gx','gy'}, dimensions={0} | all-to-all | bytes 3145728 | tf_op jit(solution)/shard_map/all_to_all | solution.py:94
  582.6 5.9 all-to-all-start.5
  591.8 21.0 %all-to-all-done.5 = f32[128,24,128]{2,1,0:T(8,128)} async-done(((f32[128,24,128]{2,1,0:T(8,128)}), f32[128,24,128]{2,1,0:T(8,128)}, u32[]{:S(2)}, u32[]{:S(2)}) %all-to-all-start.5) | async-done | bytes 1572896 | tf_op jit(solution)/shard_map/all_to_all | solution.py:94
  622.7 7.2 fusion.32
  639.7 5.3 collective-permute-done.15
  657.9 4.7 fusion.242
  679.1 32.3 %all_to_all.42 = f32[128,24,128]{2,1,0:T(8,128)S(1)} all-to-all(f32[128,24,128]{2,1,0:T(8,128)S(1)} %pad_maximum_fusion.6), channel_id=1, replica_groups=mesh['gx'=16,'gy'=8] {'gx','gy'}, dimensions={0} | all-to-all | bytes 3145728 | tf_op jit(solution)/shard_map/all_to_all | solution.py:94
  723.0 5.9 all-to-all-start.7
  729.1 24.1 %all-to-all-done.7 = f32[128,24,128]{2,1,0:T(8,128)} async-done(((f32[128,24,128]{2,1,0:T(8,128)}), f32[128,24,128]{2,1,0:T(8,128)}, u32[]{:S(2)}, u32[]{:S(2)}) %all-to-all-start.7) | async-done | bytes 1572896 | tf_op jit(solution)/shard_map/all_to_all | solution.py:94
  764.7 6.3 fusion.48
  780.5 5.7 collective-permute-done.21
  (362 shorter events, 233.0 us)
Async XLA Ops:
  0.0 362.5 %copy-start = (f32[343,343]{1,0:T(8,128)S(1)}, f32[343,343]{1,0:T(8,128)}, u32[]{:S(2)}) copy-start(f32[343,343]{1,0:T(8,128)} %param.42) | copy-start | bytes 1411792
  1.2 257.7 %collective-permute-start = (f32[12,1,12,64]{3,2,1,0:T(8,128)S(1)}, f32[12,1,12,64]{3,2,1,0:T(8,128)S(1)}, u32[]{:S(2)}, u32[]{:S(2)}) collective-permute-start(f32[12,1,12,64]{3,2,1,0:T(8,128)S(1)} %slice.1096), channel_id=1, source_target_pairs={{0,7},{1,0},{2,1},{3,2},{4,3},{5,4},{6,5},{7,6},{8,15},{9,8},{10,9... | collective-permute-start | bytes 110600 | tf_op jit(solution)/shard_map/ppermute | solution.py:23
  5.3 253.5 %collective-permute-start.2 = (f32[1,1,12,64]{3,2,1,0:T(8,128)S(1)}, f32[1,1,12,64]{3,2,1,0:T(8,128)S(1)}, u32[]{:S(2)}, u32[]{:S(2)}) collective-permute-start(f32[1,1,12,64]{3,2,1,0:T(8,128)S(1)} %slice.1098), channel_id=1, source_target_pairs={{0,127},{1,120},{2,121},{3,122},{4,123},{5,124},{6,125},{7,126},{8... | collective-permute-start | bytes 9224 | tf_op jit(solution)/shard_map/ppermute | solution.py:34
  11.0 247.9 %collective-permute-start.1 = (f32[1,6,12,64]{3,2,1,0:T(8,128)S(1)}, f32[1,6,12,64]{3,2,1,0:T(8,128)S(1)}, u32[]{:S(2)}, u32[]{:S(2)}) collective-permute-start(f32[1,6,12,64]{3,2,1,0:T(8,128)S(1)} %slice.940), channel_id=1, source_target_pairs={{0,120},{8,0},{16,8},{24,16},{32,24},{40,32},{48,40},{56,48},{64,5... | collective-permute-start | bytes 55304 | tf_op jit(solution)/shard_map/ppermute | solution.py:23
  15.9 334.0 %copy-start.14 = (f32[3072,1]{0,1:T(1,128)}, f32[3072,1]{0,1:T(1,128)S(1)}, u32[]{:S(2)}) copy-start(f32[3072,1]{0,1:T(1,128)S(1)} %get-tuple-element.286) | copy-start | bytes 36868
  15.9 334.0 %copy-start.16 = (f32[3072,1]{0,1:T(1,128)}, f32[3072,1]{0,1:T(1,128)S(1)}, u32[]{:S(2)}) copy-start(f32[3072,1]{0,1:T(1,128)S(1)} %get-tuple-element.287) | copy-start | bytes 36868
  274.8 29.3 %all-to-all-start = ((f32[128,24,128]{2,1,0:T(8,128)}), f32[128,24,128]{2,1,0:T(8,128)S(1)}, u32[]{:S(2)}, u32[]{:S(2)}) async-start(f32[128,24,128]{2,1,0:T(8,128)} %pad_maximum_fusion), calls=%async_computation | async-start | bytes 3145728 | tf_op jit(solution)/shard_map/all_to_all | solution.py:94
  311.1 29.5 %all-to-all-start.1 = ((f32[128,24,128]{2,1,0:T(8,128)}), f32[128,24,128]{2,1,0:T(8,128)S(1)}, u32[]{:S(2)}, u32[]{:S(2)}) async-start(f32[128,24,128]{2,1,0:T(8,128)} %copy.241), calls=%async_computation.1 | async-start | bytes 3145728 | tf_op jit(solution)/shard_map/all_to_all | solution.py:94
  366.8 6.9 collective-permute-start.3
  366.9 7.2 collective-permute-start.4
  367.0 10.3 %collective-permute-start.5 = (f32[12,64]{1,0:T(8,128)S(1)}, f32[12,64]{1,0:T(8,128)S(1)}, u32[]{:S(2)}, u32[]{:S(2)}) collective-permute-start(f32[12,64]{1,0:T(8,128)S(1)} %slice_bitcast_fusion.12), channel_id=1, source_target_pairs={{0,9},{1,10},{2,11},{3,12},{4,13},{5,14},{6,15},{7,8},{8,17},{9,18... | collective-permute-start | bytes 9224 | tf_op jit(solution)/shard_map/ppermute | solution.py:34
  377.6 6.1 collective-permute-start.6
  379.5 4.1 collective-permute-start.7
  380.6 3.1 collective-permute-start.8
  445.6 29.5 %all-to-all-start.3 = ((f32[128,24,128]{2,1,0:T(8,128)}), f32[128,24,128]{2,1,0:T(8,128)S(1)}, u32[]{:S(2)}, u32[]{:S(2)}) async-start(f32[128,24,128]{2,1,0:T(8,128)} %copy.263), calls=%async_computation.3 | async-start | bytes 3145728 | tf_op jit(solution)/shard_map/all_to_all | solution.py:94
  502.4 6.9 collective-permute-start.9
  502.6 7.2 collective-permute-start.10
  502.7 10.4 %collective-permute-start.11 = (f32[12,64]{1,0:T(8,128)S(1)}, f32[12,64]{1,0:T(8,128)S(1)}, u32[]{:S(2)}, u32[]{:S(2)}) collective-permute-start(f32[12,64]{1,0:T(8,128)S(1)} %slice_bitcast_fusion.11), channel_id=1, source_target_pairs={{0,9},{1,10},{2,11},{3,12},{4,13},{5,14},{6,15},{7,8},{8,17},{9,18... | collective-permute-start | bytes 9224 | tf_op jit(solution)/shard_map/ppermute | solution.py:34
  514.4 6.1 collective-permute-start.12
  516.4 4.1 collective-permute-start.13
  517.4 3.1 collective-permute-start.14
  582.6 30.2 %all-to-all-start.5 = ((f32[128,24,128]{2,1,0:T(8,128)}), f32[128,24,128]{2,1,0:T(8,128)}, u32[]{:S(2)}, u32[]{:S(2)}) async-start(f32[128,24,128]{2,1,0:T(8,128)} %copy.285), calls=%async_computation.5 | async-start | bytes 3145728 | tf_op jit(solution)/shard_map/all_to_all | solution.py:94
  638.1 6.9 collective-permute-start.15
  638.3 7.2 collective-permute-start.16
  638.4 10.3 %collective-permute-start.17 = (f32[12,64]{1,0:T(8,128)S(1)}, f32[12,64]{1,0:T(8,128)S(1)}, u32[]{:S(2)}, u32[]{:S(2)}) collective-permute-start(f32[12,64]{1,0:T(8,128)S(1)} %slice_bitcast_fusion.10), channel_id=1, source_target_pairs={{0,9},{1,10},{2,11},{3,12},{4,13},{5,14},{6,15},{7,8},{8,17},{9,18... | collective-permute-start | bytes 9224 | tf_op jit(solution)/shard_map/ppermute | solution.py:34
  648.9 6.1 collective-permute-start.18
  650.9 4.1 collective-permute-start.19
  651.9 3.1 collective-permute-start.20
  723.0 30.2 %all-to-all-start.7 = ((f32[128,24,128]{2,1,0:T(8,128)}), f32[128,24,128]{2,1,0:T(8,128)}, u32[]{:S(2)}, u32[]{:S(2)}) async-start(f32[128,24,128]{2,1,0:T(8,128)} %copy.307), calls=%async_computation.7 | async-start | bytes 3145728 | tf_op jit(solution)/shard_map/all_to_all | solution.py:94
  779.3 6.9 collective-permute-start.21
  779.5 7.2 collective-permute-start.22
  779.5 9.9 %collective-permute-start.23 = (f32[12,64]{1,0:T(8,128)S(1)}, f32[12,64]{1,0:T(8,128)S(1)}, u32[]{:S(2)}, u32[]{:S(2)}) collective-permute-start(f32[12,64]{1,0:T(8,128)S(1)} %slice_bitcast_fusion.9), channel_id=1, source_target_pairs={{0,9},{1,10},{2,11},{3,12},{4,13},{5,14},{6,15},{7,8},{8,17},{9,18... | collective-permute-start | bytes 9224 | tf_op jit(solution)/shard_map/ppermute | solution.py:34
  (48 other events, 2226.1 us)

commit v5 on v3

--- a/solution.py
+++ b/solution.py
@@ -78,11 +78,9 @@
         slot_atom[0][:, None] == jnp.arange(atoms, dtype=jnp.int32)[None, :]
     ).astype(jnp.float32)
     rows = -(-nproj // 8) * 8
-    tiles = pair_tile[0].reshape(owners, CAP, nproj, npc)
-    tiles = jnp.pad(tiles, ((0, 0), (0, 0), (0, rows - nproj), (0, 0)))
-    tile_k = [tiles[:, k].reshape(owners * rows, npc) for k in range(CAP)]
-    slot_cells = cell_mask.reshape(owners, CAP, cells)
-    mask_k = [slot_cells[:, k][:, None, :, None] for k in range(CAP)]
+    tile_all = jnp.pad(pair_tile[0], ((0, 0), (0, rows - nproj), (0, 0))).reshape(slots * rows, npc)
+    tile_t = tile_all.T
+    mask_all = jnp.repeat(cell_mask, rows, axis=0)
     incoming = one_hot.reshape(owners, CAP, atoms)
     hot_k = [incoming[:, k] for k in range(CAP)]
     coupling_pad = jnp.pad(coupling, ((0, 0), (0, rows - nproj), (0, rows - nproj)))
@@ -114,18 +112,21 @@
             axis=0,
         )
         cell_in = gather_cells(extended)
-        parts = []
-        for k in range(CAP):
-            every_cell = jnp.dot(tile_k[k], cell_in, precision=DENSE)
-            parts.append((every_cell.reshape(owners, rows, cells, W) * mask_k[k]).sum(axis=2))
-        returned = exchange(owner_work(exchange(jnp.concatenate(parts, axis=-1))))
-        spread = jnp.dot(cell_matrix, cell_in, precision=DENSE)
-        for k in range(CAP):
-            part = returned[:, :, k * W : (k + 1) * W]
-            spread_in = (part[:, :, None, :] * mask_k[k]).reshape(owners * rows, cells * W)
-            spread = spread + lax.dot_general(
-                tile_k[k], spread_in, (((0,), (0,)), ((), ())), precision=DENSE
-            )
+        every_cell = jnp.dot(tile_all, cell_in, precision=DENSE)
+        picked = None
+        for c in range(cells):
+            term = every_cell[:, c * W : (c + 1) * W] * mask_all[:, c : c + 1]
+            picked = term if picked is None else picked + term
+        picked = picked.reshape(owners, CAP, rows, W)
+        send = jnp.concatenate([picked[:, k] for k in range(CAP)], axis=-1)
+        returned = exchange(owner_work(exchange(send)))
+        by_slot = jnp.stack(
+            [returned[:, :, k * W : (k + 1) * W] for k in range(CAP)], axis=1
+        ).reshape(slots * rows, W)
+        spread_in = jnp.concatenate([by_slot * mask_all[:, c : c + 1] for c in range(cells)], axis=1)
+        spread = jnp.dot(cell_matrix, cell_in, precision=DENSE) + jnp.dot(
+            tile_t, spread_in, precision=DENSE
+        )
         summed = scatter_cells(spread, W)
         from_y = shifted(summed[:rows_x, rows_y], "gy", 1)
         from_x = shifted(summed[rows_x, :rows_y], "gx", 1)

time: 682 us -> 533 us (0.78)
  local copies, waits for them, and re-layouts: 233 us -> 99 us
  waiting for transfers between devices: 139 us -> 156 us
  matrix products: 114 us -> 97.2 us
  other arithmetic: 28 us -> 16.3 us
    mul x17 -> x0, local copies, waits for them, and re-layouts: 112 us -> none  [the longest x16 112 us: apply_operator(): part[:, :, None, :] * mask_k[k]]
    slice x15 -> x1, local copies, waits for them, and re-layouts: 40.6 us -> 0.07 us  [apply_operator(): term = every_cell[:, c * W:(c + 1) * W] * mask_all[:, c:c + 1]]
    dot_general x20 -> x12, matrix products: 96.2 us -> 78.7 us  [the longest x4 45.5 us: apply_operator(): jnp.dot(tile_t, spread_in, precision=DENSE)]
    mul x7 -> x4, other arithmetic: 20.5 us -> 3.57 us  [apply_operator(): by_slot * mask_all[:, c:c + 1]]
    all_to_all x5, waiting for transfers between devices: 95.6 us -> 112 us  [exchange(): lax.all_to_all(values, ('gx', 'gy'), split_axis=0, concat_axis=0, tiled=T...]
    another operation x2 -> x8, local copies, waits for them, and re-layouts: 21.4 us -> 10.1 us  [apply_operator(): jnp.stack([returned[:, :, k * W:(k + 1) * W] for k in range(CAP)], axis=1)]
    reshape x0 -> x5, local copies, waits for them, and re-layouts: none -> 9.73 us  [the longest x4 9.4 us: apply_operator(): by_slot = jnp.stack([returned[:, :, k * W:(k + 1) * W] for k in range(CAP...]
    add x0 -> x4, local copies, waits for them, and re-layouts: none -> 9.54 us  [apply_operator(): picked = term if picked is None else picked + term]
  transfers between devices with their start and end apart: 29 -> 29, of which waited for: 20 -> 20; matrix products, arithmetic and copies ran while one was open for 10% -> 6% of each run, Pallas kernels for 0% -> 0%
where the time goes in v5:
time: 533 us; the launch traced here: 525 us
  waiting for transfers between devices  156 us (29%)
  local copies, waits for them, and re-layouts  99 us (19%)
  blocking collectives  98 us (18%)
  matrix products  97.2 us (18%)
  starting transfers between devices  49.3 us (9%)
  other arithmetic  16.3 us (3%)
  between operations  8.53 us (2%)
    all_to_all x5, waiting for transfers between devices, exchange(): lax.all_to_all(values, ('gx', 'gy'), split_axis=0, concat_axis=0, tiled=T...  112 us
    all_to_all x3, blocking collectives, exchange(): lax.all_to_all(values, ('gx', 'gy'), split_axis=0, concat_axis=0, tiled=T...  98 us
    dot_general x4, matrix products, apply_operator(): jnp.dot(tile_t, spread_in, precision=DENSE)  45.5 us
    dot_general x4, matrix products, apply_operator(): every_cell = jnp.dot(tile_all, cell_in, precision=DENSE)  31.5 us
    all_to_all x5, starting transfers between devices, exchange(): lax.all_to_all(values, ('gx', 'gy'), split_axis=0, concat_axis=0, tiled=T...  24.6 us
    ppermute x16, waiting for transfers between devices, shifted(): return lax.ppermute(value, axis, pairs)  23.1 us
    ppermute x8, waiting for transfers between devices, diagonal(): return lax.ppermute(value, ('gx', 'gy'), pairs)  21 us
    unnamed x74, local copies, waits for them, and re-layouts  18.3 us
  transfers between devices with their start and end apart: 29, of which 20 were waited for; matrix products, arithmetic and copies ran while one was open for 6% of the time, Pallas kernels for 0%

profile of v5, /device:TPU:0, one launch (start us, length us, event | category | flops | bytes accessed | tf_op | source)
XLA Modules:
  0.0 524.5 jit_solution(4214186458145967450)
XLA Ops:
  1.2 4.1 collective-permute-start
  5.3 4.6 collective-permute-start.2
  14.4 14.0 %copy.285 = f32[1,256,18,343]{3,2,1,0:T(8,128)} copy(f32[1,256,18,343]{1,0,3,2:T(1,128)} %param.44) | data formatting | bytes 12644352
  28.4 8.0 %pad.100.clone = f32[256,24,343]{2,1,0:T(8,128)} pad(f32[256,18,343]{2,1,0:T(8,128)} %bitcast.308, f32[]{:T(128)} %constant.363.clone.1), padding=0_0x0_6x0_0 | pad | bytes 14751748 | tf_op jit(solution)/shard_map/jit(_pad)/pad | solution.py:81
  37.3 7.9 %fusion.179 = f32[6144,256]{0,1:T(8,128)S(1)} fusion(f32[6144,343]{1,0:T(8,128)} %bitcast.300, f32[343,256]{1,0:T(8,128)S(1)} %reshape.637), kind=kOutput, calls=%fused_computation.332 | convolution fusion | flops 3236954112 | bytes 15072256 | tf_op jit(solution)/shard_map/dot_general | solution.py:115
  51.7 5.2 all-to-all-start
  59.7 21.9 %all-to-all-done = f32[128,24,128]{2,1,0:T(8,128)S(1)} async-done(((f32[128,24,128]{2,1,0:T(8,128)}), f32[128,24,128]{2,1,0:T(8,128)S(1)}, u32[]{:S(2)}, u32[]{:S(2)}) %all-to-all-start) | async-done | bytes 1572896 | tf_op jit(solution)/shard_map/all_to_all | solution.py:89
  88.6 4.9 all-to-all-start.1
  98.4 19.8 %all-to-all-done.1 = f32[128,24,128]{2,1,0:T(8,128)S(1)} async-done(((f32[128,24,128]{2,1,0:T(8,128)}), f32[128,24,128]{2,1,0:T(8,128)S(1)}, u32[]{:S(2)}, u32[]{:S(2)}) %all-to-all-start.1) | async-done | bytes 1572896 | tf_op jit(solution)/shard_map/all_to_all | solution.py:89
  124.0 11.4 %fusion = f32[343,256]{1,0:T(8,128)S(1)} fusion(f32[6144,343]{1,0:T(8,128)} %bitcast.301, f32[6144,64]{0,1:T(8,128)S(1)} %get-tuple-element.238, f32[6144,64]{0,1:T(8,128)S(1)} %get-tuple-element.239, f32[6144,64]{0,1:T(8,128)S(1)} %get-tuple-element.240, f32[6144,64]{0,1:T(8,128)S(1)} %get-tuple-element.237), kind=kOutput, calls=%fused_computation | convolution fusion | flops 3241672704 | bytes 15072256 | tf_op jit(solution)/shard_map/dot_general | solution.py:127
  141.0 5.5 %collective-permute-done.3 = f32[12,12,64]{2,1,0:T(8,128)S(1)} collective-permute-done((f32[12,12,64]{2,1,0:T(8,128)S(1)}, f32[12,12,64]{2,1,0:T(8,128)S(1)}, u32[]{:S(2)}, u32[]{:S(2)}) %collective-permute-start.3) | collective-permute-done | bytes 36896 | tf_op jit(solution)/shard_map/ppermute | solution.py:23
  153.2 3.1 collective-permute-done.8
  157.2 7.9 %fusion.180 = f32[6144,256]{0,1:T(8,128)S(1)} fusion(f32[6144,343]{1,0:T(8,128)} %bitcast.302, f32[343,256]{1,0:T(8,128)S(1)} %reshape.646), kind=kOutput, calls=%fused_computation.333 | convolution fusion | flops 3236954112 | bytes 15072256 | tf_op jit(solution)/shard_map/dot_general | solution.py:115
  170.5 32.7 %all_to_all.40 = f32[128,24,128]{2,1,0:T(8,128)S(1)} all-to-all(f32[128,24,128]{2,1,0:T(8,128)S(1)} %pad_maximum_fusion.6), channel_id=1, replica_groups=mesh['gx'=16,'gy'=8] {'gx','gy'}, dimensions={0} | all-to-all | bytes 3145728 | tf_op jit(solution)/shard_map/all_to_all | solution.py:89
  210.4 4.8 all-to-all-start.3
  215.4 24.5 %all-to-all-done.3 = f32[128,24,128]{2,1,0:T(8,128)S(1)} async-done(((f32[128,24,128]{2,1,0:T(8,128)}), f32[128,24,128]{2,1,0:T(8,128)S(1)}, u32[]{:S(2)}, u32[]{:S(2)}) %all-to-all-start.3) | async-done | bytes 1572896 | tf_op jit(solution)/shard_map/all_to_all | solution.py:89
  245.6 11.4 %fusion.8 = f32[343,256]{1,0:T(8,128)S(1)} fusion(f32[6144,343]{1,0:T(8,128)} %bitcast.303, f32[6144,64]{0,1:T(8,128)S(1)} %get-tuple-element.230, f32[6144,64]{0,1:T(8,128)S(1)} %get-tuple-element.231, f32[6144,64]{0,1:T(8,128)S(1)} %get-tuple-element.232, f32[6144,64]{0,1:T(8,128)S(1)} %get-tuple-element.229), kind=kOutput, calls=%fused_computation.8 | convolution fusion | flops 3241672704 | bytes 15072256 | tf_op jit(solution)/shard_map/dot_general | solution.py:127
  267.1 3.7 collective-permute-done.9
  279.4 3.1 collective-permute-done.14
  284.0 7.9 %fusion.181 = f32[6144,256]{0,1:T(8,128)S(1)} fusion(f32[6144,343]{1,0:T(8,128)} %bitcast.304, f32[343,256]{1,0:T(8,128)S(1)} %reshape.653), kind=kOutput, calls=%fused_computation.334 | convolution fusion | flops 3236954112 | bytes 15072256 | tf_op jit(solution)/shard_map/dot_general | solution.py:115
  297.4 32.7 %all_to_all.41 = f32[128,24,128]{2,1,0:T(8,128)S(1)} all-to-all(f32[128,24,128]{2,1,0:T(8,128)S(1)} %pad_maximum_fusion.8), channel_id=1, replica_groups=mesh['gx'=16,'gy'=8] {'gx','gy'}, dimensions={0} | all-to-all | bytes 3145728 | tf_op jit(solution)/shard_map/all_to_all | solution.py:89
  338.0 4.8 all-to-all-start.5
  345.9 21.5 %all-to-all-done.5 = f32[128,24,128]{2,1,0:T(8,128)S(1)} async-done(((f32[128,24,128]{2,1,0:T(8,128)}), f32[128,24,128]{2,1,0:T(8,128)S(1)}, u32[]{:S(2)}, u32[]{:S(2)}) %all-to-all-start.5) | async-done | bytes 1572896 | tf_op jit(solution)/shard_map/all_to_all | solution.py:89
  374.0 11.4 %fusion.16 = f32[343,256]{1,0:T(8,128)S(1)} fusion(f32[6144,343]{1,0:T(8,128)} %bitcast.305, f32[6144,64]{0,1:T(8,128)S(1)} %get-tuple-element.222, f32[6144,64]{0,1:T(8,128)S(1)} %get-tuple-element.223, f32[6144,64]{0,1:T(8,128)S(1)} %get-tuple-element.224, f32[6144,64]{0,1:T(8,128)S(1)} %get-tuple-element.221), kind=kOutput, calls=%fused_computation.16 | convolution fusion | flops 3241672704 | bytes 15072256 | tf_op jit(solution)/shard_map/dot_general | solution.py:127
  392.0 5.5 %collective-permute-done.15 = f32[12,12,64]{2,1,0:T(8,128)S(1)} collective-permute-done((f32[12,12,64]{2,1,0:T(8,128)S(1)}, f32[12,12,64]{2,1,0:T(8,128)S(1)}, u32[]{:S(2)}, u32[]{:S(2)}) %collective-permute-start.15) | collective-permute-done | bytes 36896 | tf_op jit(solution)/shard_map/ppermute | solution.py:23
  404.2 3.1 collective-permute-done.20
  408.9 7.9 %fusion.182 = f32[6144,256]{0,1:T(8,128)S(1)} fusion(f32[6144,343]{1,0:T(8,128)} %bitcast.306, f32[343,256]{1,0:T(8,128)S(1)} %reshape.660), kind=kOutput, calls=%fused_computation.335 | convolution fusion | flops 3236954112 | bytes 15072256 | tf_op jit(solution)/shard_map/dot_general | solution.py:115
  422.2 32.7 %all_to_all.42 = f32[128,24,128]{2,1,0:T(8,128)S(1)} all-to-all(f32[128,24,128]{2,1,0:T(8,128)S(1)} %pad_maximum_fusion.10), channel_id=1, replica_groups=mesh['gx'=16,'gy'=8] {'gx','gy'}, dimensions={0} | all-to-all | bytes 3145728 | tf_op jit(solution)/shard_map/all_to_all | solution.py:89
  462.1 4.8 all-to-all-start.7
  467.1 24.5 %all-to-all-done.7 = f32[128,24,128]{2,1,0:T(8,128)S(1)} async-done(((f32[128,24,128]{2,1,0:T(8,128)}), f32[128,24,128]{2,1,0:T(8,128)S(1)}, u32[]{:S(2)}, u32[]{:S(2)}) %all-to-all-start.7) | async-done | bytes 1572896 | tf_op jit(solution)/shard_map/all_to_all | solution.py:89
  497.4 11.4 %fusion.24 = f32[343,256]{1,0:T(8,128)S(1)} fusion(f32[6144,343]{1,0:T(8,128)} %bitcast.307, f32[6144,64]{0,1:T(8,128)S(1)} %get-tuple-element.214, f32[6144,64]{0,1:T(8,128)S(1)} %get-tuple-element.215, f32[6144,64]{0,1:T(8,128)S(1)} %get-tuple-element.216, f32[6144,64]{0,1:T(8,128)S(1)} %get-tuple-element.213), kind=kOutput, calls=%fused_computation.24 | convolution fusion | flops 3241672704 | bytes 15072256 | tf_op jit(solution)/shard_map/dot_general | solution.py:127
  514.2 5.7 %collective-permute-done.21 = f32[12,12,64]{2,1,0:T(8,128)S(1)} collective-permute-done((f32[12,12,64]{2,1,0:T(8,128)S(1)}, f32[12,12,64]{2,1,0:T(8,128)S(1)}, u32[]{:S(2)}, u32[]{:S(2)}) %collective-permute-start.21) | collective-permute-done | bytes 36896 | tf_op jit(solution)/shard_map/ppermute | solution.py:23
  (287 shorter events, 143.9 us)
Async XLA Ops:
  0.0 135.4 %copy-start = (f32[343,343]{1,0:T(8,128)S(1)}, f32[343,343]{1,0:T(8,128)}, u32[]{:S(2)}) copy-start(f32[343,343]{1,0:T(8,128)} %param.42) | copy-start | bytes 1411792
  1.2 27.2 %copy-start.5 = (f32[12,6,12,64]{3,2,1,0:T(8,128)}, f32[12,6,12,64]{3,2,1,0:T(8,128)S(1)}, u32[]{:S(2)}) copy-start(f32[12,6,12,64]{3,2,1,0:T(8,128)S(1)} %reshape.636) | copy-start | bytes 663556
  1.2 35.2 %collective-permute-start = (f32[12,1,12,64]{3,2,1,0:T(8,128)S(1)}, f32[12,1,12,64]{3,2,1,0:T(8,128)S(1)}, u32[]{:S(2)}, u32[]{:S(2)}) collective-permute-start(f32[12,1,12,64]{3,2,1,0:T(8,128)S(1)} %slice.1004), channel_id=1, source_target_pairs={{0,7},{1,0},{2,1},{3,2},{4,3},{5,4},{6,5},{7,6},{8,15},{9,8},{10,9... | collective-permute-start | bytes 110600 | tf_op jit(solution)/shard_map/ppermute | solution.py:23
  5.3 31.1 %collective-permute-start.2 = (f32[1,1,12,64]{3,2,1,0:T(8,128)S(1)}, f32[1,1,12,64]{3,2,1,0:T(8,128)S(1)}, u32[]{:S(2)}, u32[]{:S(2)}) collective-permute-start(f32[1,1,12,64]{3,2,1,0:T(8,128)S(1)} %slice.1006), channel_id=1, source_target_pairs={{0,127},{1,120},{2,121},{3,122},{4,123},{5,124},{6,125},{7,126},{8... | collective-permute-start | bytes 9224 | tf_op jit(solution)/shard_map/ppermute | solution.py:34
  11.0 25.4 %collective-permute-start.1 = (f32[1,6,12,64]{3,2,1,0:T(8,128)S(1)}, f32[1,6,12,64]{3,2,1,0:T(8,128)S(1)}, u32[]{:S(2)}, u32[]{:S(2)}) collective-permute-start(f32[1,6,12,64]{3,2,1,0:T(8,128)S(1)} %slice.864), channel_id=1, source_target_pairs={{0,120},{8,0},{16,8},{24,16},{32,24},{40,32},{48,40},{56,48},{64,5... | collective-permute-start | bytes 55304 | tf_op jit(solution)/shard_map/ppermute | solution.py:23
  14.4 108.9 %copy-start.12 = (f32[6144,1]{0,1:T(1,128)}, f32[6144,1]{0,1:T(1,128)S(1)}, u32[]{:S(2)}) copy-start(f32[6144,1]{0,1:T(1,128)S(1)} %get-tuple-element.277) | copy-start | bytes 73732
  51.7 29.9 %all-to-all-start = ((f32[128,24,128]{2,1,0:T(8,128)}), f32[128,24,128]{2,1,0:T(8,128)S(1)}, u32[]{:S(2)}, u32[]{:S(2)}) async-start(f32[128,24,128]{2,1,0:T(8,128)} %pad_maximum_fusion.4), calls=%async_computation | async-start | bytes 3145728 | tf_op jit(solution)/shard_map/all_to_all | solution.py:89
  88.6 29.6 %all-to-all-start.1 = ((f32[128,24,128]{2,1,0:T(8,128)}), f32[128,24,128]{2,1,0:T(8,128)S(1)}, u32[]{:S(2)}, u32[]{:S(2)}) async-start(f32[128,24,128]{2,1,0:T(8,128)} %copy.191), calls=%async_computation.1 | async-start | bytes 3145728 | tf_op jit(solution)/shard_map/all_to_all | solution.py:89
  139.6 6.9 %collective-permute-start.3 = (f32[12,12,64]{2,1,0:T(8,128)S(1)}, f32[12,12,64]{2,1,0:T(8,128)S(1)}, u32[]{:S(2)}, u32[]{:S(2)}) collective-permute-start(f32[12,12,64]{2,1,0:T(8,128)S(1)} %slice_bitcast_fusion.20), channel_id=1, source_target_pairs={{0,1},{1,2},{2,3},{3,4},{4,5},{5,6},{6,7},{7,0},{8,9},{9,10},{10,1... | collective-permute-start | bytes 110600 | tf_op jit(solution)/shard_map/ppermute | solution.py:23
  139.7 7.2 %collective-permute-start.4 = (f32[6,12,64]{2,1,0:T(8,128)S(1)}, f32[6,12,64]{2,1,0:T(8,128)S(1)}, u32[]{:S(2)}, u32[]{:S(2)}) collective-permute-start(f32[6,12,64]{2,1,0:T(8,128)S(1)} %slice_bitcast_fusion.24), channel_id=1, source_target_pairs={{0,8},{8,16},{16,24},{24,32},{32,40},{40,48},{48,56},{56,64},{64,7... | collective-permute-start | bytes 55304 | tf_op jit(solution)/shard_map/ppermute | solution.py:23
  139.8 10.1 %collective-permute-start.5 = (f32[12,64]{1,0:T(8,128)S(1)}, f32[12,64]{1,0:T(8,128)S(1)}, u32[]{:S(2)}, u32[]{:S(2)}) collective-permute-start(f32[12,64]{1,0:T(8,128)S(1)} %slice_bitcast_fusion.28), channel_id=1, source_target_pairs={{0,9},{1,10},{2,11},{3,12},{4,13},{5,14},{6,15},{7,8},{8,17},{9,18... | collective-permute-start | bytes 9224 | tf_op jit(solution)/shard_map/ppermute | solution.py:34
  150.2 6.1 %collective-permute-start.6 = (f32[12,1,12,64]{3,2,1,0:T(8,128)S(1)}, f32[12,1,12,64]{3,2,1,0:T(8,128)S(1)}, u32[]{:S(2)}, u32[]{:S(2)}) collective-permute-start(f32[12,1,12,64]{3,2,1,0:T(8,128)S(1)} %slice.1035), channel_id=1, source_target_pairs={{0,7},{1,0},{2,1},{3,2},{4,3},{5,4},{6,5},{7,6},{8,15},{9,8},{10,9... | collective-permute-start | bytes 110600 | tf_op jit(solution)/shard_map/ppermute | solution.py:23
  152.2 4.1 collective-permute-start.7
  153.2 3.1 collective-permute-start.8
  210.4 29.4 %all-to-all-start.3 = ((f32[128,24,128]{2,1,0:T(8,128)}), f32[128,24,128]{2,1,0:T(8,128)S(1)}, u32[]{:S(2)}, u32[]{:S(2)}) async-start(f32[128,24,128]{2,1,0:T(8,128)} %copy.210), calls=%async_computation.3 | async-start | bytes 3145728 | tf_op jit(solution)/shard_map/all_to_all | solution.py:89
  264.0 6.7 %collective-permute-start.9 = (f32[12,12,64]{2,1,0:T(8,128)S(1)}, f32[12,12,64]{2,1,0:T(8,128)S(1)}, u32[]{:S(2)}, u32[]{:S(2)}) collective-permute-start(f32[12,12,64]{2,1,0:T(8,128)S(1)} %slice_bitcast_fusion.19), channel_id=1, source_target_pairs={{0,1},{1,2},{2,3},{3,4},{4,5},{5,6},{6,7},{7,0},{8,9},{9,10},{10,1... | collective-permute-start | bytes 110600 | tf_op jit(solution)/shard_map/ppermute | solution.py:23
  265.9 7.2 %collective-permute-start.10 = (f32[6,12,64]{2,1,0:T(8,128)S(1)}, f32[6,12,64]{2,1,0:T(8,128)S(1)}, u32[]{:S(2)}, u32[]{:S(2)}) collective-permute-start(f32[6,12,64]{2,1,0:T(8,128)S(1)} %slice_bitcast_fusion.23), channel_id=1, source_target_pairs={{0,8},{8,16},{16,24},{24,32},{32,40},{40,48},{48,56},{56,64},{64,7... | collective-permute-start | bytes 55304 | tf_op jit(solution)/shard_map/ppermute | solution.py:23
  265.9 10.1 %collective-permute-start.11 = (f32[12,64]{1,0:T(8,128)S(1)}, f32[12,64]{1,0:T(8,128)S(1)}, u32[]{:S(2)}, u32[]{:S(2)}) collective-permute-start(f32[12,64]{1,0:T(8,128)S(1)} %slice_bitcast_fusion.27), channel_id=1, source_target_pairs={{0,9},{1,10},{2,11},{3,12},{4,13},{5,14},{6,15},{7,8},{8,17},{9,18... | collective-permute-start | bytes 9224 | tf_op jit(solution)/shard_map/ppermute | solution.py:34
  276.4 6.1 %collective-permute-start.12 = (f32[12,1,12,64]{3,2,1,0:T(8,128)S(1)}, f32[12,1,12,64]{3,2,1,0:T(8,128)S(1)}, u32[]{:S(2)}, u32[]{:S(2)}) collective-permute-start(f32[12,1,12,64]{3,2,1,0:T(8,128)S(1)} %slice.1060), channel_id=1, source_target_pairs={{0,7},{1,0},{2,1},{3,2},{4,3},{5,4},{6,5},{7,6},{8,15},{9,8},{10,9... | collective-permute-start | bytes 110600 | tf_op jit(solution)/shard_map/ppermute | solution.py:23
  278.3 4.1 collective-permute-start.13
  279.4 3.1 collective-permute-start.14
  338.0 29.4 %all-to-all-start.5 = ((f32[128,24,128]{2,1,0:T(8,128)}), f32[128,24,128]{2,1,0:T(8,128)S(1)}, u32[]{:S(2)}, u32[]{:S(2)}) async-start(f32[128,24,128]{2,1,0:T(8,128)} %copy.229), calls=%async_computation.5 | async-start | bytes 3145728 | tf_op jit(solution)/shard_map/all_to_all | solution.py:89
  390.6 6.9 %collective-permute-start.15 = (f32[12,12,64]{2,1,0:T(8,128)S(1)}, f32[12,12,64]{2,1,0:T(8,128)S(1)}, u32[]{:S(2)}, u32[]{:S(2)}) collective-permute-start(f32[12,12,64]{2,1,0:T(8,128)S(1)} %slice_bitcast_fusion.18), channel_id=1, source_target_pairs={{0,1},{1,2},{2,3},{3,4},{4,5},{5,6},{6,7},{7,0},{8,9},{9,10},{10,1... | collective-permute-start | bytes 110600 | tf_op jit(solution)/shard_map/ppermute | solution.py:23
  390.8 7.2 %collective-permute-start.16 = (f32[6,12,64]{2,1,0:T(8,128)S(1)}, f32[6,12,64]{2,1,0:T(8,128)S(1)}, u32[]{:S(2)}, u32[]{:S(2)}) collective-permute-start(f32[6,12,64]{2,1,0:T(8,128)S(1)} %slice_bitcast_fusion.22), channel_id=1, source_target_pairs={{0,8},{8,16},{16,24},{24,32},{32,40},{40,48},{48,56},{56,64},{64,7... | collective-permute-start | bytes 55304 | tf_op jit(solution)/shard_map/ppermute | solution.py:23
  390.8 10.1 %collective-permute-start.17 = (f32[12,64]{1,0:T(8,128)S(1)}, f32[12,64]{1,0:T(8,128)S(1)}, u32[]{:S(2)}, u32[]{:S(2)}) collective-permute-start(f32[12,64]{1,0:T(8,128)S(1)} %slice_bitcast_fusion.26), channel_id=1, source_target_pairs={{0,9},{1,10},{2,11},{3,12},{4,13},{5,14},{6,15},{7,8},{8,17},{9,18... | collective-permute-start | bytes 9224 | tf_op jit(solution)/shard_map/ppermute | solution.py:34
  401.2 6.1 %collective-permute-start.18 = (f32[12,1,12,64]{3,2,1,0:T(8,128)S(1)}, f32[12,1,12,64]{3,2,1,0:T(8,128)S(1)}, u32[]{:S(2)}, u32[]{:S(2)}) collective-permute-start(f32[12,1,12,64]{3,2,1,0:T(8,128)S(1)} %slice.1085), channel_id=1, source_target_pairs={{0,7},{1,0},{2,1},{3,2},{4,3},{5,4},{6,5},{7,6},{8,15},{9,8},{10,9... | collective-permute-start | bytes 110600 | tf_op jit(solution)/shard_map/ppermute | solution.py:23
  403.2 4.1 collective-permute-start.19
  404.2 3.1 collective-permute-start.20
  462.1 29.4 %all-to-all-start.7 = ((f32[128,24,128]{2,1,0:T(8,128)}), f32[128,24,128]{2,1,0:T(8,128)S(1)}, u32[]{:S(2)}, u32[]{:S(2)}) async-start(f32[128,24,128]{2,1,0:T(8,128)} %copy.248), calls=%async_computation.7 | async-start | bytes 3145728 | tf_op jit(solution)/shard_map/all_to_all | solution.py:89
  513.1 6.9 %collective-permute-start.21 = (f32[12,12,64]{2,1,0:T(8,128)S(1)}, f32[12,12,64]{2,1,0:T(8,128)S(1)}, u32[]{:S(2)}, u32[]{:S(2)}) collective-permute-start(f32[12,12,64]{2,1,0:T(8,128)S(1)} %slice_bitcast_fusion.17), channel_id=1, source_target_pairs={{0,1},{1,2},{2,3},{3,4},{4,5},{5,6},{6,7},{7,0},{8,9},{9,10},{10,1... | collective-permute-start | bytes 110600 | tf_op jit(solution)/shard_map/ppermute | solution.py:23
  513.2 7.2 %collective-permute-start.22 = (f32[6,12,64]{2,1,0:T(8,128)S(1)}, f32[6,12,64]{2,1,0:T(8,128)S(1)}, u32[]{:S(2)}, u32[]{:S(2)}) collective-permute-start(f32[6,12,64]{2,1,0:T(8,128)S(1)} %slice_bitcast_fusion.21), channel_id=1, source_target_pairs={{0,8},{8,16},{16,24},{24,32},{32,40},{40,48},{48,56},{56,64},{64,7... | collective-permute-start | bytes 55304 | tf_op jit(solution)/shard_map/ppermute | solution.py:23
  513.3 9.9 %collective-permute-start.23 = (f32[12,64]{1,0:T(8,128)S(1)}, f32[12,64]{1,0:T(8,128)S(1)}, u32[]{:S(2)}, u32[]{:S(2)}) collective-permute-start(f32[12,64]{1,0:T(8,128)S(1)} %slice_bitcast_fusion.25), channel_id=1, source_target_pairs={{0,9},{1,10},{2,11},{3,12},{4,13},{5,14},{6,15},{7,8},{8,17},{9,18... | collective-permute-start | bytes 9224 | tf_op jit(solution)/shard_map/ppermute | solution.py:34
  (26 other events, 227.7 us)

commit v6 on v5

--- a/solution.py
+++ b/solution.py
@@ -32,6 +32,42 @@
         for v in range(count_y)
     ]
     return lax.ppermute(value, ("gx", "gy"), pairs)
+
+
+def neighbour(value, dx, dy):
+    count_x = lax.axis_size("gx")
+    count_y = lax.axis_size("gy")
+    pairs = [
+        (u * count_y + v, ((u - dx) % count_x) * count_y + (v - dy) % count_y)
+        for u in range(count_x)
+        for v in range(count_y)
+    ]
+    return lax.ppermute(value, ("gx", "gy"), pairs)
+
+
+def extend(values):
+    face_x = neighbour(values[:1], 1, 0)
+    face_y = neighbour(values[:, :1], 0, 1)
+    corner = neighbour(values[:1, :1], 1, 1)
+    return jnp.concatenate(
+        [jnp.concatenate([values, face_y], axis=1), jnp.concatenate([face_x, corner], axis=1)],
+        axis=0,
+    )
+
+
+def combine(partial, rows_x, rows_y):
+    from_xm = neighbour(partial[rows_x], -1, 0)
+    from_xp = neighbour(partial[0], 1, 0)
+    from_ym = neighbour(partial[:, rows_y], 0, -1)
+    from_yp = neighbour(partial[:, 0], 0, 1)
+    corner_mm = neighbour(partial[rows_x, rows_y], -1, -1)
+    corner_mp = neighbour(partial[rows_x, 0], -1, 1)
+    corner_pm = neighbour(partial[0, rows_y], 1, -1)
+    corner_pp = neighbour(partial[0, 0], 1, 1)
+    total = partial.at[0].add(from_xm).at[rows_x].add(from_xp)
+    total = total.at[:, 0].add(from_ym).at[:, rows_y].add(from_yp)
+    total = total.at[0, 0].add(corner_mm).at[0, rows_y].add(corner_mp)
+    return total.at[rows_x, 0].add(corner_pm).at[rows_x, rows_y].add(corner_pp)
 
 
 def cell_ranges():
@@ -72,7 +108,7 @@
     atoms = coupling.shape[0]
     cells = CX * CY * CZ
     owners = lax.axis_size(("gx", "gy"))
-    local_pot = potential.reshape(rows_x, rows_y, ZN, 1)
+    local_pot = extend(potential.reshape(rows_x, rows_y, ZN, 1))
     cell_mask = (pair_cell[0][:, None] == jnp.arange(cells, dtype=jnp.int32)[None, :]).astype(jnp.float32)
     one_hot = (
         slot_atom[0][:, None] == jnp.arange(atoms, dtype=jnp.int32)[None, :]
@@ -101,17 +137,7 @@
         )
 
     def apply_operator(current):
-        face_x = shifted(current[:1], "gx", -1)
-        face_y = shifted(current[:, :1], "gy", -1)
-        corner = diagonal(current[:1, :1], -1)
-        extended = jnp.concatenate(
-            [
-                jnp.concatenate([current, face_y], axis=1),
-                jnp.concatenate([face_x, corner], axis=1),
-            ],
-            axis=0,
-        )
-        cell_in = gather_cells(extended)
+        cell_in = gather_cells(current)
         every_cell = jnp.dot(tile_all, cell_in, precision=DENSE)
         picked = None
         for c in range(cells):
@@ -127,15 +153,10 @@
         spread = jnp.dot(cell_matrix, cell_in, precision=DENSE) + jnp.dot(
             tile_t, spread_in, precision=DENSE
         )
-        summed = scatter_cells(spread, W)
-        from_y = shifted(summed[:rows_x, rows_y], "gy", 1)
-        from_x = shifted(summed[rows_x, :rows_y], "gx", 1)
-        from_corner = diagonal(summed[rows_x, rows_y], 1)
-        summed = summed[:rows_x, :rows_y].at[:, 0].add(from_y)
-        summed = summed.at[0].add(from_x).at[0, 0].add(from_corner)
+        summed = combine(scatter_cells(spread, W), rows_x, rows_y)
         return summed + local_pot * current
 
-    previous = wavefunctions.reshape(rows_x, rows_y, ZN, W)
+    previous = extend(wavefunctions.reshape(rows_x, rows_y, ZN, W))
     for filter_index in range(FILTERS):
         lower_bound = bounds[filter_index, 0]
         low_end = bounds[filter_index, 1]
@@ -153,7 +174,7 @@
         current = following
         sigma_now = sigma_next
         previous = current
-    return previous.reshape(rows_x, rows_y * ZN * W)
+    return previous[:rows_x, :rows_y].reshape(rows_x, rows_y * ZN * W)
 
 
 def solution(mesh):

time: 533 us -> 649 us (1.22)
  waiting for transfers between devices: 156 us -> 57.5 us
  blocking collectives: 98 us -> 180 us
  other arithmetic: 16.3 us -> 65.3 us
  starting transfers between devices: 49.3 us -> 94.3 us
  local copies, waits for them, and re-layouts: 99 us -> 130 us
  matrix products: 97.2 us -> 104 us
    all_to_all x3 -> x6, blocking collectives: 98 us -> 180 us  [exchange(): lax.all_to_all(values, ('gx', 'gy'), split_axis=0, concat_axis=0, tiled=T...]
    all_to_all x5 -> x2, waiting for transfers between devices: 112 us -> 30.1 us  [exchange(): lax.all_to_all(values, ('gx', 'gy'), split_axis=0, concat_axis=0, tiled=T...]
    ppermute x24 -> x38, starting transfers between devices: 24.7 us -> 82.2 us  [neighbour(): return lax.ppermute(value, ('gx', 'gy'), pairs)]
    scatter-add x12 -> x28, other arithmetic: 1.02 us -> 27.6 us  [the longest x8 13 us: combine(): total = total.at[0, 0].add(corner_mm).at[0, rows_y].add(corner_mp)]
    ppermute x24 -> x38, waiting for transfers between devices: 44.2 us -> 27.4 us  [neighbour(): return lax.ppermute(value, ('gx', 'gy'), pairs)]
    all_to_all x5 -> x2, starting transfers between devices: 24.6 us -> 12.1 us  [exchange(): lax.all_to_all(values, ('gx', 'gy'), split_axis=0, concat_axis=0, tiled=T...]
    unnamed x74 -> x70, local copies, waits for them, and re-layouts: 18.3 us -> 16.1 us
  transfers between devices with their start and end apart: 29 -> 40, of which waited for: 20 -> 6; matrix products, arithmetic and copies ran while one was open for 6% -> 13% of each run, Pallas kernels for 0% -> 0%
where the time goes in v6:
time: 649 us; the launch traced here: 640 us
  blocking collectives  180 us (28%)
  local copies, waits for them, and re-layouts  130 us (20%)
  matrix products  104 us (16%)
  starting transfers between devices  94.3 us (15%)
  other arithmetic  65.3 us (10%)
  waiting for transfers between devices  57.5 us (9%)
  between operations  8.35 us (1%)
    all_to_all x6, blocking collectives, exchange(): lax.all_to_all(values, ('gx', 'gy'), split_axis=0, concat_axis=0, tiled=T...  180 us
    ppermute x38, starting transfers between devices, neighbour(): return lax.ppermute(value, ('gx', 'gy'), pairs)  82.2 us
    dot_general x4, matrix products, apply_operator(): jnp.dot(tile_t, spread_in, precision=DENSE)  45.4 us
    dot_general x4, matrix products, apply_operator(): every_cell = jnp.dot(tile_all, cell_in, precision=DENSE)  31.5 us
    all_to_all x2, waiting for transfers between devices, exchange(): lax.all_to_all(values, ('gx', 'gy'), split_axis=0, concat_axis=0, tiled=T...  30.1 us
    ppermute x38, waiting for transfers between devices, neighbour(): return lax.ppermute(value, ('gx', 'gy'), pairs)  27.4 us
    unnamed x70, local copies, waits for them, and re-layouts  16.1 us
    add x4, local copies, waits for them, and re-layouts, apply_operator(): picked = term if picked is None else picked + term  13.5 us
  transfers between devices with their start and end apart: 40, of which 6 were waited for; matrix products, arithmetic and copies ran while one was open for 13% of the time, Pallas kernels for 0%

profile of v6, /device:TPU:0, one launch (start us, length us, event | category | flops | bytes accessed | tf_op | source)
XLA Modules:
  0.0 639.8 jit_solution(12465253044639309216)
XLA Ops:
  14.4 14.1 %copy.308 = f32[1,256,18,343]{3,2,1,0:T(8,128)} copy(f32[1,256,18,343]{1,0,3,2:T(1,128)} %param.84) | data formatting | bytes 12644352
  28.5 8.0 %pad.164.clone = f32[256,24,343]{2,1,0:T(8,128)} pad(f32[256,18,343]{2,1,0:T(8,128)} %bitcast.409, f32[]{:T(128)} %constant.811.clone.1), padding=0_0x0_6x0_0 | pad | bytes 14751748 | tf_op jit(solution)/shard_map/jit(_pad)/pad | solution.py:117
  37.9 7.9 %fusion.171 = f32[6144,256]{0,1:T(8,128)S(1)} fusion(f32[6144,343]{1,0:T(8,128)} %bitcast.401, f32[343,256]{1,0:T(8,128)S(1)} %reshape.1347), kind=kOutput, calls=%fused_computation.372 | convolution fusion | flops 3236954112 | bytes 15072256 | tf_op jit(solution)/shard_map/dot_general | solution.py:141
  54.5 6.3 all-to-all-start
  62.6 22.5 %all-to-all-done = f32[128,24,128]{2,1,0:T(8,128)} async-done(((f32[128,24,128]{2,1,0:T(8,128)}), f32[128,24,128]{2,1,0:T(8,128)}, u32[]{:S(2)}, u32[]{:S(2)}) %all-to-all-start) | async-done | bytes 1572896 | tf_op jit(solution)/shard_map/all_to_all | solution.py:125
  98.6 5.8 all-to-all-start.1
  121.1 7.6 %all-to-all-done.1 = f32[128,24,128]{2,1,0:T(8,128)} async-done(((f32[128,24,128]{2,1,0:T(8,128)}), f32[128,24,128]{2,1,0:T(8,128)}, u32[]{:S(2)}, u32[]{:S(2)}) %all-to-all-start.1) | async-done | bytes 1572896 | tf_op jit(solution)/shard_map/all_to_all | solution.py:125
  138.7 11.4 %fusion = f32[343,256]{1,0:T(8,128)S(1)} fusion(f32[6144,343]{1,0:T(8,128)} %bitcast.402, f32[6144,64]{0,1:T(8,128)S(1)} %get-tuple-element.470, f32[6144,64]{0,1:T(8,128)S(1)} %get-tuple-element.471, f32[6144,64]{0,1:T(8,128)S(1)} %get-tuple-element.472, f32[6144,64]{0,1:T(8,128)S(1)} %get-tuple-element.469), kind=kOutput, calls=%fused_computation | convolution fusion | flops 3241672704 | bytes 15072256 | tf_op jit(solution)/shard_map/dot_general | solution.py:153
  156.1 7.2 %collective-permute-done.3 = f32[7,12,64]{2,1,0:T(8,128)S(1)} collective-permute-done((f32[7,12,64]{2,1,0:T(8,128)S(1)}, f32[7,12,64]{2,1,0:T(8,128)S(1)}, u32[]{:S(2)}, u32[]{:S(2)}) %collective-permute-start.3) | collective-permute-done | bytes 21536 | tf_op jit(solution)/shard_map/ppermute | solution.py:45
  169.2 5.7 collective-permute-start.9
  174.9 4.8 collective-permute-start.10
  185.8 7.9 %fusion.172 = f32[6144,256]{0,1:T(8,128)S(1)} fusion(f32[6144,343]{1,0:T(8,128)} %bitcast.403, f32[343,256]{1,0:T(8,128)S(1)} %reshape.1364), kind=kOutput, calls=%fused_computation.373 | convolution fusion | flops 3236954112 | bytes 15072256 | tf_op jit(solution)/shard_map/dot_general | solution.py:141
  201.3 33.2 %all_to_all.40 = f32[128,24,128]{2,1,0:T(8,128)S(1)} all-to-all(f32[128,24,128]{2,1,0:T(8,128)S(1)} %pad_maximum_fusion.6), channel_id=1, replica_groups=mesh['gx'=16,'gy'=8] {'gx','gy'}, dimensions={0} | all-to-all | bytes 3145728 | tf_op jit(solution)/shard_map/all_to_all | solution.py:125
  248.4 29.7 %all_to_all.41 = f32[128,24,128]{2,1,0:T(8,128)S(1)} all-to-all(f32[128,24,128]{2,1,0:T(8,128)} %copy.226), channel_id=1, replica_groups=mesh['gx'=16,'gy'=8] {'gx','gy'}, dimensions={0} | all-to-all | bytes 3145728 | tf_op jit(solution)/shard_map/all_to_all | solution.py:125
  286.2 11.4 %fusion.8 = f32[343,256]{1,0:T(8,128)S(1)} fusion(f32[6144,343]{1,0:T(8,128)} %bitcast.404, f32[6144,64]{0,1:T(8,128)S(1)} %get-tuple-element.462, f32[6144,64]{0,1:T(8,128)S(1)} %get-tuple-element.463, f32[6144,64]{0,1:T(8,128)S(1)} %get-tuple-element.464, f32[6144,64]{0,1:T(8,128)S(1)} %get-tuple-element.461), kind=kOutput, calls=%fused_computation.8 | convolution fusion | flops 3241672704 | bytes 15072256 | tf_op jit(solution)/shard_map/dot_general | solution.py:153
  307.0 6.5 %collective-permute-done.14 = f32[7,12,64]{2,1,0:T(8,128)S(1)} collective-permute-done((f32[7,12,64]{2,1,0:T(8,128)S(1)}, f32[7,12,64]{2,1,0:T(8,128)S(1)}, u32[]{:S(2)}, u32[]{:S(2)}) %collective-permute-start.14) | collective-permute-done | bytes 21536 | tf_op jit(solution)/shard_map/ppermute | solution.py:45
  320.1 5.7 collective-permute-start.20
  327.2 4.8 collective-permute-start.21
  344.7 7.9 %fusion.173 = f32[6144,256]{0,1:T(8,128)S(1)} fusion(f32[6144,343]{1,0:T(8,128)} %bitcast.405, f32[343,256]{1,0:T(8,128)S(1)} %reshape.1376), kind=kOutput, calls=%fused_computation.374 | convolution fusion | flops 3236954112 | bytes 15072256 | tf_op jit(solution)/shard_map/dot_general | solution.py:141
  360.2 29.0 %all_to_all.42 = f32[128,24,128]{2,1,0:T(8,128)S(1)} all-to-all(f32[128,24,128]{2,1,0:T(8,128)S(1)} %pad_maximum_fusion.8), channel_id=1, replica_groups=mesh['gx'=16,'gy'=8] {'gx','gy'}, dimensions={0} | all-to-all | bytes 3145728 | tf_op jit(solution)/shard_map/all_to_all | solution.py:125
  401.1 29.7 %all_to_all.43 = f32[128,24,128]{2,1,0:T(8,128)S(1)} all-to-all(f32[128,24,128]{2,1,0:T(8,128)} %copy.246), channel_id=1, replica_groups=mesh['gx'=16,'gy'=8] {'gx','gy'}, dimensions={0} | all-to-all | bytes 3145728 | tf_op jit(solution)/shard_map/all_to_all | solution.py:125
  438.9 11.3 %fusion.16 = f32[343,256]{1,0:T(8,128)S(1)} fusion(f32[6144,343]{1,0:T(8,128)} %bitcast.406, f32[6144,64]{0,1:T(8,128)S(1)} %get-tuple-element.454, f32[6144,64]{0,1:T(8,128)S(1)} %get-tuple-element.455, f32[6144,64]{0,1:T(8,128)S(1)} %get-tuple-element.456, f32[6144,64]{0,1:T(8,128)S(1)} %get-tuple-element.453), kind=kOutput, calls=%fused_computation.16 | convolution fusion | flops 3241672704 | bytes 15072256 | tf_op jit(solution)/shard_map/dot_general | solution.py:153
  459.7 6.5 %collective-permute-done.22 = f32[7,12,64]{2,1,0:T(8,128)S(1)} collective-permute-done((f32[7,12,64]{2,1,0:T(8,128)S(1)}, f32[7,12,64]{2,1,0:T(8,128)S(1)}, u32[]{:S(2)}, u32[]{:S(2)}) %collective-permute-start.22) | collective-permute-done | bytes 21536 | tf_op jit(solution)/shard_map/ppermute | solution.py:45
  475.7 5.7 collective-permute-start.28
  482.9 4.8 collective-permute-start.29
  502.2 7.9 %fusion.174 = f32[6144,256]{0,1:T(8,128)S(1)} fusion(f32[6144,343]{1,0:T(8,128)} %bitcast.407, f32[343,256]{1,0:T(8,128)S(1)} %reshape.1388), kind=kOutput, calls=%fused_computation.375 | convolution fusion | flops 3236954112 | bytes 15072256 | tf_op jit(solution)/shard_map/dot_general | solution.py:141
  517.7 29.0 %all_to_all.44 = f32[128,24,128]{2,1,0:T(8,128)S(1)} all-to-all(f32[128,24,128]{2,1,0:T(8,128)S(1)} %pad_maximum_fusion.10), channel_id=1, replica_groups=mesh['gx'=16,'gy'=8] {'gx','gy'}, dimensions={0} | all-to-all | bytes 3145728 | tf_op jit(solution)/shard_map/all_to_all | solution.py:125
  558.4 29.7 %all_to_all.45 = f32[128,24,128]{2,1,0:T(8,128)S(1)} all-to-all(f32[128,24,128]{2,1,0:T(8,128)} %copy.266), channel_id=1, replica_groups=mesh['gx'=16,'gy'=8] {'gx','gy'}, dimensions={0} | all-to-all | bytes 3145728 | tf_op jit(solution)/shard_map/all_to_all | solution.py:125
  596.1 11.3 %fusion.24 = f32[343,256]{1,0:T(8,128)S(1)} fusion(f32[6144,343]{1,0:T(8,128)} %bitcast.408, f32[6144,64]{0,1:T(8,128)S(1)} %get-tuple-element.446, f32[6144,64]{0,1:T(8,128)S(1)} %get-tuple-element.447, f32[6144,64]{0,1:T(8,128)S(1)} %get-tuple-element.448, f32[6144,64]{0,1:T(8,128)S(1)} %get-tuple-element.445), kind=kOutput, calls=%fused_computation.24 | convolution fusion | flops 3241672704 | bytes 15072256 | tf_op jit(solution)/shard_map/dot_general | solution.py:153
  613.5 7.2 %collective-permute-done.30 = f32[7,12,64]{2,1,0:T(8,128)S(1)} collective-permute-done((f32[7,12,64]{2,1,0:T(8,128)S(1)}, f32[7,12,64]{2,1,0:T(8,128)S(1)}, u32[]{:S(2)}, u32[]{:S(2)}) %collective-permute-start.30) | collective-permute-done | bytes 21536 | tf_op jit(solution)/shard_map/ppermute | solution.py:45
  625.7 5.7 collective-permute-start.36
  631.5 4.8 collective-permute-start.37
  (324 shorter events, 240.7 us)
Async XLA Ops:
  1.2 35.3 %collective-permute-start = (f32[12,1,12,64]{3,2,1,0:T(8,128)S(1)}, f32[12,1,12,64]{3,2,1,0:T(8,128)S(1)}, u32[]{:S(2)}, u32[]{:S(2)}) collective-permute-start(f32[12,1,12,64]{3,2,1,0:T(8,128)S(1)} %slice.1612), channel_id=1, source_target_pairs={{0,7},{1,0},{2,1},{3,2},{4,3},{5,4},{6,5},{7,6},{8,15},{9,8},{10,9... | collective-permute-start | bytes 110600 | tf_op jit(solution)/shard_map/ppermute | solution.py:45
  5.3 31.2 %collective-permute-start.2 = (f32[1,1,12,64]{3,2,1,0:T(8,128)S(1)}, f32[1,1,12,64]{3,2,1,0:T(8,128)S(1)}, u32[]{:S(2)}, u32[]{:S(2)}) collective-permute-start(f32[1,1,12,64]{3,2,1,0:T(8,128)S(1)} %slice.1614), channel_id=1, source_target_pairs={{0,127},{1,120},{2,121},{3,122},{4,123},{5,124},{6,125},{7,126},{8... | collective-permute-start | bytes 9224 | tf_op jit(solution)/shard_map/ppermute | solution.py:45
  11.0 25.5 %collective-permute-start.1 = (f32[1,6,12,64]{3,2,1,0:T(8,128)S(1)}, f32[1,6,12,64]{3,2,1,0:T(8,128)S(1)}, u32[]{:S(2)}, u32[]{:S(2)}) collective-permute-start(f32[1,6,12,64]{3,2,1,0:T(8,128)S(1)} %slice.1446), channel_id=1, source_target_pairs={{0,120},{1,121},{2,122},{3,123},{4,124},{5,125},{6,126},{7,127},{8... | collective-permute-start | bytes 55304 | tf_op jit(solution)/shard_map/ppermute | solution.py:45
  54.5 30.6 %all-to-all-start = ((f32[128,24,128]{2,1,0:T(8,128)}), f32[128,24,128]{2,1,0:T(8,128)}, u32[]{:S(2)}, u32[]{:S(2)}) async-start(f32[128,24,128]{2,1,0:T(8,128)} %pad_maximum_fusion.4), calls=%async_computation | async-start | bytes 3145728 | tf_op jit(solution)/shard_map/all_to_all | solution.py:125
  98.6 30.1 %all-to-all-start.1 = ((f32[128,24,128]{2,1,0:T(8,128)}), f32[128,24,128]{2,1,0:T(8,128)}, u32[]{:S(2)}, u32[]{:S(2)}) async-start(f32[128,24,128]{2,1,0:T(8,128)} %copy.205), calls=%async_computation.1 | async-start | bytes 3145728 | tf_op jit(solution)/shard_map/all_to_all | solution.py:125
  105.2 58.3 %collective-permute-start.11 = (f32[12,1,12,1]{2,1,0,3:T(1,128)}, f32[12,1,12,1]{2,1,0,3:T(1,128)}, u32[]{:S(2)}, u32[]{:S(2)}) collective-permute-start(f32[12,1,12,1]{2,1,0,3:T(1,128)} %slice.1652), channel_id=1, source_target_pairs={{0,7},{1,0},{2,1},{3,2},{4,3},{5,4},{6,5},{7,6},{8,15},{9,8},{10,9... | collective-permute-start | bytes 1736 | tf_op jit(solution)/shard_map/ppermute | solution.py:45
  108.8 54.6 %collective-permute-start.13 = (f32[1,1,12,1]{2,1,0,3:T(1,128)}, f32[1,1,12,1]{2,1,0,3:T(1,128)}, u32[]{:S(2)}, u32[]{:S(2)}) collective-permute-start(f32[1,1,12,1]{2,1,0,3:T(1,128)} %slice.1653), channel_id=1, source_target_pairs={{0,127},{1,120},{2,121},{3,122},{4,123},{5,124},{6,125},{7,126},{8... | collective-permute-start | bytes 152 | tf_op jit(solution)/shard_map/ppermute | solution.py:45
  113.9 49.6 %collective-permute-start.12 = (f32[1,6,12,1]{2,1,0,3:T(8,128)}, f32[1,6,12,1]{2,1,0,3:T(8,128)S(1)}, u32[]{:S(2)}, u32[]{:S(2)}) collective-permute-start(f32[1,6,12,1]{2,1,0,3:T(8,128)} %bitcast.53), channel_id=1, source_target_pairs={{0,120},{1,121},{2,122},{3,123},{4,124},{5,125},{6,126},{7,127},{8... | collective-permute-start | bytes 872 | tf_op jit(solution)/shard_map/ppermute | solution.py:45
  156.0 7.3 %collective-permute-start.3 = (f32[7,12,64]{2,1,0:T(8,128)S(1)}, f32[7,12,64]{2,1,0:T(8,128)S(1)}, u32[]{:S(2)}, u32[]{:S(2)}) collective-permute-start(f32[7,12,64]{2,1,0:T(8,128)S(1)} %slice_bitcast_fusion.35), channel_id=1, source_target_pairs={{0,8},{1,9},{2,10},{3,11},{4,12},{5,13},{6,14},{7,15},{8,16},{9,17... | collective-permute-start | bytes 64520 | tf_op jit(solution)/shard_map/ppermute | solution.py:45
  164.2 10.7 %collective-permute-start.5 = (f32[13,12,64]{2,1,0:T(8,128)S(1)}, f32[13,12,64]{2,1,0:T(8,128)S(1)}, u32[]{:S(2)}, u32[]{:S(2)}) collective-permute-start(f32[13,12,64]{2,1,0:T(8,128)S(1)} %get-tuple-element.522), channel_id=1, source_target_pairs={{0,1},{1,2},{2,3},{3,4},{4,5},{5,6},{6,7},{7,0},{8,9},{9,10},{10,1... | collective-permute-start | bytes 119816 | tf_op jit(solution)/shard_map/ppermute | solution.py:45
  164.5 15.3 %collective-permute-start.6 = (f32[13,12,64]{2,1,0:T(8,128)S(1)}, f32[13,12,64]{2,1,0:T(8,128)S(1)}, u32[]{:S(2)}, u32[]{:S(2)}) collective-permute-start(f32[13,12,64]{2,1,0:T(8,128)S(1)} %get-tuple-element.521), channel_id=1, source_target_pairs={{0,7},{1,0},{2,1},{3,2},{4,3},{5,4},{6,5},{7,6},{8,15},{9,8},{10,9... | collective-permute-start | bytes 119816 | tf_op jit(solution)/shard_map/ppermute | solution.py:45
  168.6 11.2 %collective-permute-start.7 = (f32[12,64]{1,0:T(8,128)S(1)}, f32[12,64]{1,0:T(8,128)S(1)}, u32[]{:S(2)}, u32[]{:S(2)}) collective-permute-start(f32[12,64]{1,0:T(8,128)S(1)} %get-tuple-element.520), channel_id=1, source_target_pairs={{0,9},{1,10},{2,11},{3,12},{4,13},{5,14},{6,15},{7,8},{8,17},{9,18... | collective-permute-start | bytes 9224 | tf_op jit(solution)/shard_map/ppermute | solution.py:45
  168.6 11.2 %collective-permute-start.8 = (f32[12,64]{1,0:T(8,128)S(1)}, f32[12,64]{1,0:T(8,128)S(1)}, u32[]{:S(2)}, u32[]{:S(2)}) collective-permute-start(f32[12,64]{1,0:T(8,128)S(1)} %get-tuple-element.519), channel_id=1, source_target_pairs={{0,15},{1,8},{2,9},{3,10},{4,11},{5,12},{6,13},{7,14},{8,23},{9,16... | collective-permute-start | bytes 9224 | tf_op jit(solution)/shard_map/ppermute | solution.py:45
  169.2 12.6 %collective-permute-start.9 = (f32[12,64]{1,0:T(8,128)S(1)}, f32[12,64]{1,0:T(8,128)S(1)}, u32[]{:S(2)}, u32[]{:S(2)}) collective-permute-start(f32[12,64]{1,0:T(8,128)S(1)} %get-tuple-element.518), channel_id=1, source_target_pairs={{0,121},{1,122},{2,123},{3,124},{4,125},{5,126},{6,127},{7,120},{8... | collective-permute-start | bytes 9224 | tf_op jit(solution)/shard_map/ppermute | solution.py:45
  315.1 12.1 %collective-permute-start.16 = (f32[13,12,64]{2,1,0:T(8,128)S(1)}, f32[13,12,64]{2,1,0:T(8,128)S(1)}, u32[]{:S(2)}, u32[]{:S(2)}) collective-permute-start(f32[13,12,64]{2,1,0:T(8,128)S(1)} %get-tuple-element.512), channel_id=1, source_target_pairs={{0,1},{1,2},{2,3},{3,4},{4,5},{5,6},{6,7},{7,0},{8,9},{9,10},{10,1... | collective-permute-start | bytes 119816 | tf_op jit(solution)/shard_map/ppermute | solution.py:45
  315.4 18.2 %collective-permute-start.17 = (f32[13,12,64]{2,1,0:T(8,128)S(1)}, f32[13,12,64]{2,1,0:T(8,128)S(1)}, u32[]{:S(2)}, u32[]{:S(2)}) collective-permute-start(f32[13,12,64]{2,1,0:T(8,128)S(1)} %get-tuple-element.511), channel_id=1, source_target_pairs={{0,7},{1,0},{2,1},{3,2},{4,3},{5,4},{6,5},{7,6},{8,15},{9,8},{10,9... | collective-permute-start | bytes 119816 | tf_op jit(solution)/shard_map/ppermute | solution.py:45
  319.5 15.7 %collective-permute-start.18 = (f32[12,64]{1,0:T(8,128)S(1)}, f32[12,64]{1,0:T(8,128)S(1)}, u32[]{:S(2)}, u32[]{:S(2)}) collective-permute-start(f32[12,64]{1,0:T(8,128)S(1)} %get-tuple-element.510), channel_id=1, source_target_pairs={{0,9},{1,10},{2,11},{3,12},{4,13},{5,14},{6,15},{7,8},{8,17},{9,18... | collective-permute-start | bytes 9224 | tf_op jit(solution)/shard_map/ppermute | solution.py:45
  319.5 17.0 %collective-permute-start.19 = (f32[12,64]{1,0:T(8,128)S(1)}, f32[12,64]{1,0:T(8,128)S(1)}, u32[]{:S(2)}, u32[]{:S(2)}) collective-permute-start(f32[12,64]{1,0:T(8,128)S(1)} %get-tuple-element.509), channel_id=1, source_target_pairs={{0,15},{1,8},{2,9},{3,10},{4,11},{5,12},{6,13},{7,14},{8,23},{9,16... | collective-permute-start | bytes 9224 | tf_op jit(solution)/shard_map/ppermute | solution.py:45
  320.1 19.7 %collective-permute-start.20 = (f32[12,64]{1,0:T(8,128)S(1)}, f32[12,64]{1,0:T(8,128)S(1)}, u32[]{:S(2)}, u32[]{:S(2)}) collective-permute-start(f32[12,64]{1,0:T(8,128)S(1)} %get-tuple-element.508), channel_id=1, source_target_pairs={{0,121},{1,122},{2,123},{3,124},{4,125},{5,126},{6,127},{7,120},{8... | collective-permute-start | bytes 9224 | tf_op jit(solution)/shard_map/ppermute | solution.py:45
  327.2 13.8 %collective-permute-start.21 = (f32[12,64]{1,0:T(8,128)S(1)}, f32[12,64]{1,0:T(8,128)S(1)}, u32[]{:S(2)}, u32[]{:S(2)}) collective-permute-start(f32[12,64]{1,0:T(8,128)S(1)} %get-tuple-element.507), channel_id=1, source_target_pairs={{0,127},{1,120},{2,121},{3,122},{4,123},{5,124},{6,125},{7,126},{8... | collective-permute-start | bytes 9224 | tf_op jit(solution)/shard_map/ppermute | solution.py:45
  467.6 8.1 %collective-permute-start.23 = (f32[7,12,64]{2,1,0:T(8,128)S(1)}, f32[7,12,64]{2,1,0:T(8,128)S(1)}, u32[]{:S(2)}, u32[]{:S(2)}) collective-permute-start(f32[7,12,64]{2,1,0:T(8,128)S(1)} %get-tuple-element.503), channel_id=1, source_target_pairs={{0,120},{1,121},{2,122},{3,123},{4,124},{5,125},{6,126},{7,127},{8... | collective-permute-start | bytes 64520 | tf_op jit(solution)/shard_map/ppermute | solution.py:45
  470.7 12.1 %collective-permute-start.24 = (f32[13,12,64]{2,1,0:T(8,128)S(1)}, f32[13,12,64]{2,1,0:T(8,128)S(1)}, u32[]{:S(2)}, u32[]{:S(2)}) collective-permute-start(f32[13,12,64]{2,1,0:T(8,128)S(1)} %get-tuple-element.502), channel_id=1, source_target_pairs={{0,1},{1,2},{2,3},{3,4},{4,5},{5,6},{6,7},{7,0},{8,9},{9,10},{10,1... | collective-permute-start | bytes 119816 | tf_op jit(solution)/shard_map/ppermute | solution.py:45
  471.0 18.2 %collective-permute-start.25 = (f32[13,12,64]{2,1,0:T(8,128)S(1)}, f32[13,12,64]{2,1,0:T(8,128)S(1)}, u32[]{:S(2)}, u32[]{:S(2)}) collective-permute-start(f32[13,12,64]{2,1,0:T(8,128)S(1)} %get-tuple-element.501), channel_id=1, source_target_pairs={{0,7},{1,0},{2,1},{3,2},{4,3},{5,4},{6,5},{7,6},{8,15},{9,8},{10,9... | collective-permute-start | bytes 119816 | tf_op jit(solution)/shard_map/ppermute | solution.py:45
  475.2 15.7 %collective-permute-start.26 = (f32[12,64]{1,0:T(8,128)S(1)}, f32[12,64]{1,0:T(8,128)S(1)}, u32[]{:S(2)}, u32[]{:S(2)}) collective-permute-start(f32[12,64]{1,0:T(8,128)S(1)} %get-tuple-element.500), channel_id=1, source_target_pairs={{0,9},{1,10},{2,11},{3,12},{4,13},{5,14},{6,15},{7,8},{8,17},{9,18... | collective-permute-start | bytes 9224 | tf_op jit(solution)/shard_map/ppermute | solution.py:45
  475.2 17.0 %collective-permute-start.27 = (f32[12,64]{1,0:T(8,128)S(1)}, f32[12,64]{1,0:T(8,128)S(1)}, u32[]{:S(2)}, u32[]{:S(2)}) collective-permute-start(f32[12,64]{1,0:T(8,128)S(1)} %get-tuple-element.499), channel_id=1, source_target_pairs={{0,15},{1,8},{2,9},{3,10},{4,11},{5,12},{6,13},{7,14},{8,23},{9,16... | collective-permute-start | bytes 9224 | tf_op jit(solution)/shard_map/ppermute | solution.py:45
  475.7 19.7 %collective-permute-start.28 = (f32[12,64]{1,0:T(8,128)S(1)}, f32[12,64]{1,0:T(8,128)S(1)}, u32[]{:S(2)}, u32[]{:S(2)}) collective-permute-start(f32[12,64]{1,0:T(8,128)S(1)} %get-tuple-element.498), channel_id=1, source_target_pairs={{0,121},{1,122},{2,123},{3,124},{4,125},{5,126},{6,127},{7,120},{8... | collective-permute-start | bytes 9224 | tf_op jit(solution)/shard_map/ppermute | solution.py:45
  482.9 13.8 %collective-permute-start.29 = (f32[12,64]{1,0:T(8,128)S(1)}, f32[12,64]{1,0:T(8,128)S(1)}, u32[]{:S(2)}, u32[]{:S(2)}) collective-permute-start(f32[12,64]{1,0:T(8,128)S(1)} %get-tuple-element.497), channel_id=1, source_target_pairs={{0,127},{1,120},{2,121},{3,122},{4,123},{5,124},{6,125},{7,126},{8... | collective-permute-start | bytes 9224 | tf_op jit(solution)/shard_map/ppermute | solution.py:45
  621.0 10.5 %collective-permute-start.32 = (f32[13,12,64]{2,1,0:T(8,128)S(1)}, f32[13,12,64]{2,1,0:T(8,128)S(1)}, u32[]{:S(2)}, u32[]{:S(2)}) collective-permute-start(f32[13,12,64]{2,1,0:T(8,128)S(1)} %get-tuple-element.490), channel_id=1, source_target_pairs={{0,1},{1,2},{2,3},{3,4},{4,5},{5,6},{6,7},{7,0},{8,9},{9,10},{10,1... | collective-permute-start | bytes 119816 | tf_op jit(solution)/shard_map/ppermute | solution.py:45
  621.1 15.3 %collective-permute-start.33 = (f32[13,12,64]{2,1,0:T(8,128)S(1)}, f32[13,12,64]{2,1,0:T(8,128)S(1)}, u32[]{:S(2)}, u32[]{:S(2)}) collective-permute-start(f32[13,12,64]{2,1,0:T(8,128)S(1)} %get-tuple-element.489), channel_id=1, source_target_pairs={{0,7},{1,0},{2,1},{3,2},{4,3},{5,4},{6,5},{7,6},{8,15},{9,8},{10,9... | collective-permute-start | bytes 119816 | tf_op jit(solution)/shard_map/ppermute | solution.py:45
  625.2 11.2 %collective-permute-start.34 = (f32[12,64]{1,0:T(8,128)S(1)}, f32[12,64]{1,0:T(8,128)S(1)}, u32[]{:S(2)}, u32[]{:S(2)}) collective-permute-start(f32[12,64]{1,0:T(8,128)S(1)} %get-tuple-element.488), channel_id=1, source_target_pairs={{0,9},{1,10},{2,11},{3,12},{4,13},{5,14},{6,15},{7,8},{8,17},{9,18... | collective-permute-start | bytes 9224 | tf_op jit(solution)/shard_map/ppermute | solution.py:45
  625.2 11.2 %collective-permute-start.35 = (f32[12,64]{1,0:T(8,128)S(1)}, f32[12,64]{1,0:T(8,128)S(1)}, u32[]{:S(2)}, u32[]{:S(2)}) collective-permute-start(f32[12,64]{1,0:T(8,128)S(1)} %get-tuple-element.487), channel_id=1, source_target_pairs={{0,15},{1,8},{2,9},{3,10},{4,11},{5,12},{6,13},{7,14},{8,23},{9,16... | collective-permute-start | bytes 9224 | tf_op jit(solution)/shard_map/ppermute | solution.py:45
  625.7 12.6 %collective-permute-start.36 = (f32[12,64]{1,0:T(8,128)S(1)}, f32[12,64]{1,0:T(8,128)S(1)}, u32[]{:S(2)}, u32[]{:S(2)}) collective-permute-start(f32[12,64]{1,0:T(8,128)S(1)} %get-tuple-element.486), channel_id=1, source_target_pairs={{0,121},{1,122},{2,123},{3,124},{4,125},{5,126},{6,127},{7,120},{8... | collective-permute-start | bytes 9224 | tf_op jit(solution)/shard_map/ppermute | solution.py:45
  (33 other events, 1355.1 us)

commit v7 on v5

--- a/solution.py
+++ b/solution.py
@@ -119,14 +119,13 @@
             picked = term if picked is None else picked + term
         picked = picked.reshape(owners, CAP, rows, W)
         send = jnp.concatenate([picked[:, k] for k in range(CAP)], axis=-1)
+        kinetic = lax.optimization_barrier(jnp.dot(cell_matrix, cell_in, precision=DENSE))
         returned = exchange(owner_work(exchange(send)))
         by_slot = jnp.stack(
             [returned[:, :, k * W : (k + 1) * W] for k in range(CAP)], axis=1
         ).reshape(slots * rows, W)
         spread_in = jnp.concatenate([by_slot * mask_all[:, c : c + 1] for c in range(cells)], axis=1)
-        spread = jnp.dot(cell_matrix, cell_in, precision=DENSE) + jnp.dot(
-            tile_t, spread_in, precision=DENSE
-        )
+        spread = kinetic + jnp.dot(tile_t, spread_in, precision=DENSE)
         summed = scatter_cells(spread, W)
         from_y = shifted(summed[:rows_x, rows_y], "gy", 1)
         from_x = shifted(summed[rows_x, :rows_y], "gx", 1)

time: 533 us -> 532 us (level)
    unnamed x74 -> x78, local copies, waits for them, and re-layouts: 18.3 us -> 18.9 us
  transfers between devices with their start and end apart: 29 -> 29, of which waited for: 20 -> 20; matrix products, arithmetic and copies ran while one was open for 6% -> 7% of each run, Pallas kernels for 0% -> 0%
where the time goes in v7:
time: 532 us; the launch traced here: 524 us
  waiting for transfers between devices  152 us (29%)
  matrix products  100 us (19%)
  local copies, waits for them, and re-layouts  99.5 us (19%)
  blocking collectives  98 us (18%)
  starting transfers between devices  49.4 us (9%)
  other arithmetic  16.3 us (3%)
  between operations  8 us (2%)
    all_to_all x5, waiting for transfers between devices, exchange(): lax.all_to_all(values, ('gx', 'gy'), split_axis=0, concat_axis=0, tiled=T...  108 us
    all_to_all x3, blocking collectives, exchange(): lax.all_to_all(values, ('gx', 'gy'), split_axis=0, concat_axis=0, tiled=T...  98 us
    dot_general x4, matrix products, apply_operator(): spread = kinetic + jnp.dot(tile_t, spread_in, precision=DENSE)  45.5 us
    dot_general x4, matrix products, apply_operator(): every_cell = jnp.dot(tile_all, cell_in, precision=DENSE)  31.5 us
    all_to_all x5, starting transfers between devices, exchange(): lax.all_to_all(values, ('gx', 'gy'), split_axis=0, concat_axis=0, tiled=T...  24.7 us
    ppermute x16, waiting for transfers between devices, shifted(): return lax.ppermute(value, axis, pairs)  23.1 us
    ppermute x8, waiting for transfers between devices, diagonal(): return lax.ppermute(value, ('gx', 'gy'), pairs)  21 us
    unnamed x78, local copies, waits for them, and re-layouts  18.9 us
  transfers between devices with their start and end apart: 29, of which 20 were waited for; matrix products, arithmetic and copies ran while one was open for 7% of the time, Pallas kernels for 0%

profile of v7, /device:TPU:0, one launch (start us, length us, event | category | flops | bytes accessed | tf_op | source)
XLA Modules:
  0.0 523.5 jit_solution(13400894658271136891)
XLA Ops:
  1.2 4.1 collective-permute-start
  5.3 4.6 collective-permute-start.2
  14.4 14.1 %copy.285 = f32[1,256,18,343]{3,2,1,0:T(8,128)} copy(f32[1,256,18,343]{1,0,3,2:T(1,128)} %param.44) | data formatting | bytes 12644352
  28.5 8.0 %pad.100.clone = f32[256,24,343]{2,1,0:T(8,128)} pad(f32[256,18,343]{2,1,0:T(8,128)} %bitcast.300, f32[]{:T(128)} %constant.363.clone.1), padding=0_0x0_6x0_0 | pad | bytes 14751748 | tf_op jit(solution)/shard_map/jit(_pad)/pad | solution.py:81
  37.4 7.9 %fusion.187 = f32[6144,256]{0,1:T(8,128)S(1)} fusion(f32[6144,343]{1,0:T(8,128)} %bitcast.292, f32[343,256]{1,0:T(8,128)S(1)} %reshape.637), kind=kOutput, calls=%fused_computation.332 | convolution fusion | flops 3236954112 | bytes 15072256 | tf_op jit(solution)/shard_map/dot_general | solution.py:115
  51.9 5.2 all-to-all-start
  59.8 21.9 %all-to-all-done = f32[128,24,128]{2,1,0:T(8,128)S(1)} async-done(((f32[128,24,128]{2,1,0:T(8,128)}), f32[128,24,128]{2,1,0:T(8,128)S(1)}, u32[]{:S(2)}, u32[]{:S(2)}) %all-to-all-start) | async-done | bytes 1572896 | tf_op jit(solution)/shard_map/all_to_all | solution.py:89
  88.7 4.9 all-to-all-start.1
  99.1 19.2 %all-to-all-done.1 = f32[128,24,128]{2,1,0:T(8,128)S(1)} async-done(((f32[128,24,128]{2,1,0:T(8,128)}), f32[128,24,128]{2,1,0:T(8,128)S(1)}, u32[]{:S(2)}, u32[]{:S(2)}) %all-to-all-start.1) | async-done | bytes 1572896 | tf_op jit(solution)/shard_map/all_to_all | solution.py:89
  124.4 11.4 %fusion.81 = f32[343,256]{1,0:T(8,128)S(1)} fusion(f32[343,256]{1,0:T(8,128)S(1)} %copy-done.16, f32[6144,343]{1,0:T(8,128)} %bitcast.293, f32[6144,64]{0,1:T(8,128)S(1)} %get-tuple-element.238, f32[6144,64]{0,1:T(8,128)S(1)} %get-tuple-element.239, f32[6144,64]{0,1:T(8,128)S(1)} %get-tuple-element.240, f32[6144,64]{0,1:T(8,128)S(1)} %get-tuple-element.237), kind=kOutput, calls=%fused_computation.115 | convolution fusion | flops 3241760512 | bytes 15423488 | tf_op jit(solution)/shard_map/dot_general | solution.py:128
  140.9 5.5 %collective-permute-done.3 = f32[12,12,64]{2,1,0:T(8,128)S(1)} collective-permute-done((f32[12,12,64]{2,1,0:T(8,128)S(1)}, f32[12,12,64]{2,1,0:T(8,128)S(1)}, u32[]{:S(2)}, u32[]{:S(2)}) %collective-permute-start.3) | collective-permute-done | bytes 36896 | tf_op jit(solution)/shard_map/ppermute | solution.py:23
  153.2 3.1 collective-permute-done.8
  157.1 7.9 %fusion.188 = f32[6144,256]{0,1:T(8,128)S(1)} fusion(f32[6144,343]{1,0:T(8,128)} %bitcast.294, f32[343,256]{1,0:T(8,128)S(1)} %reshape.646), kind=kOutput, calls=%fused_computation.333 | convolution fusion | flops 3236954112 | bytes 15072256 | tf_op jit(solution)/shard_map/dot_general | solution.py:115
  170.5 32.7 %all_to_all.40 = f32[128,24,128]{2,1,0:T(8,128)S(1)} all-to-all(f32[128,24,128]{2,1,0:T(8,128)S(1)} %pad_maximum_fusion.6), channel_id=1, replica_groups=mesh['gx'=16,'gy'=8] {'gx','gy'}, dimensions={0} | all-to-all | bytes 3145728 | tf_op jit(solution)/shard_map/all_to_all | solution.py:89
  210.3 4.8 all-to-all-start.3
  216.5 23.3 %all-to-all-done.3 = f32[128,24,128]{2,1,0:T(8,128)S(1)} async-done(((f32[128,24,128]{2,1,0:T(8,128)}), f32[128,24,128]{2,1,0:T(8,128)S(1)}, u32[]{:S(2)}, u32[]{:S(2)}) %all-to-all-start.3) | async-done | bytes 1572896 | tf_op jit(solution)/shard_map/all_to_all | solution.py:89
  245.8 11.4 %fusion.78 = f32[343,256]{1,0:T(8,128)S(1)} fusion(f32[343,256]{1,0:T(8,128)S(1)} %copy-done.17, f32[6144,343]{1,0:T(8,128)} %bitcast.295, f32[6144,64]{0,1:T(8,128)S(1)} %get-tuple-element.230, f32[6144,64]{0,1:T(8,128)S(1)} %get-tuple-element.231, f32[6144,64]{0,1:T(8,128)S(1)} %get-tuple-element.232, f32[6144,64]{0,1:T(8,128)S(1)} %get-tuple-element.229), kind=kOutput, calls=%fused_computation.114 | convolution fusion | flops 3241760512 | bytes 15423488 | tf_op jit(solution)/shard_map/dot_general | solution.py:128
  266.8 3.7 collective-permute-done.9
  279.1 3.1 collective-permute-done.14
  283.8 7.9 %fusion.189 = f32[6144,256]{0,1:T(8,128)S(1)} fusion(f32[6144,343]{1,0:T(8,128)} %bitcast.296, f32[343,256]{1,0:T(8,128)S(1)} %reshape.653), kind=kOutput, calls=%fused_computation.334 | convolution fusion | flops 3236954112 | bytes 15072256 | tf_op jit(solution)/shard_map/dot_general | solution.py:115
  297.1 32.7 %all_to_all.41 = f32[128,24,128]{2,1,0:T(8,128)S(1)} all-to-all(f32[128,24,128]{2,1,0:T(8,128)S(1)} %pad_maximum_fusion.8), channel_id=1, replica_groups=mesh['gx'=16,'gy'=8] {'gx','gy'}, dimensions={0} | all-to-all | bytes 3145728 | tf_op jit(solution)/shard_map/all_to_all | solution.py:89
  337.7 4.8 all-to-all-start.5
  347.7 19.4 %all-to-all-done.5 = f32[128,24,128]{2,1,0:T(8,128)S(1)} async-done(((f32[128,24,128]{2,1,0:T(8,128)}), f32[128,24,128]{2,1,0:T(8,128)S(1)}, u32[]{:S(2)}, u32[]{:S(2)}) %all-to-all-start.5) | async-done | bytes 1572896 | tf_op jit(solution)/shard_map/all_to_all | solution.py:89
  373.7 11.4 %fusion.75 = f32[343,256]{1,0:T(8,128)S(1)} fusion(f32[343,256]{1,0:T(8,128)S(1)} %copy-done.18, f32[6144,343]{1,0:T(8,128)} %bitcast.297, f32[6144,64]{0,1:T(8,128)S(1)} %get-tuple-element.222, f32[6144,64]{0,1:T(8,128)S(1)} %get-tuple-element.223, f32[6144,64]{0,1:T(8,128)S(1)} %get-tuple-element.224, f32[6144,64]{0,1:T(8,128)S(1)} %get-tuple-element.221), kind=kOutput, calls=%fused_computation.113 | convolution fusion | flops 3241760512 | bytes 15423488 | tf_op jit(solution)/shard_map/dot_general | solution.py:128
  391.3 5.5 %collective-permute-done.15 = f32[12,12,64]{2,1,0:T(8,128)S(1)} collective-permute-done((f32[12,12,64]{2,1,0:T(8,128)S(1)}, f32[12,12,64]{2,1,0:T(8,128)S(1)}, u32[]{:S(2)}, u32[]{:S(2)}) %collective-permute-start.15) | collective-permute-done | bytes 36896 | tf_op jit(solution)/shard_map/ppermute | solution.py:23
  403.6 3.1 collective-permute-done.20
  408.3 7.9 %fusion.190 = f32[6144,256]{0,1:T(8,128)S(1)} fusion(f32[6144,343]{1,0:T(8,128)} %bitcast.298, f32[343,256]{1,0:T(8,128)S(1)} %reshape.660), kind=kOutput, calls=%fused_computation.335 | convolution fusion | flops 3236954112 | bytes 15072256 | tf_op jit(solution)/shard_map/dot_general | solution.py:115
  421.6 32.7 %all_to_all.42 = f32[128,24,128]{2,1,0:T(8,128)S(1)} all-to-all(f32[128,24,128]{2,1,0:T(8,128)S(1)} %pad_maximum_fusion.10), channel_id=1, replica_groups=mesh['gx'=16,'gy'=8] {'gx','gy'}, dimensions={0} | all-to-all | bytes 3145728 | tf_op jit(solution)/shard_map/all_to_all | solution.py:89
  461.5 4.9 all-to-all-start.7
  467.0 24.0 %all-to-all-done.7 = f32[128,24,128]{2,1,0:T(8,128)S(1)} async-done(((f32[128,24,128]{2,1,0:T(8,128)}), f32[128,24,128]{2,1,0:T(8,128)S(1)}, u32[]{:S(2)}, u32[]{:S(2)}) %all-to-all-start.7) | async-done | bytes 1572896 | tf_op jit(solution)/shard_map/all_to_all | solution.py:89
  496.9 11.4 %fusion.72 = f32[343,256]{1,0:T(8,128)S(1)} fusion(f32[343,256]{1,0:T(8,128)S(1)} %convolution_bitcast_fusion, f32[6144,343]{1,0:T(8,128)} %bitcast.299, f32[6144,64]{0,1:T(8,128)S(1)} %get-tuple-element.214, f32[6144,64]{0,1:T(8,128)S(1)} %get-tuple-element.215, f32[6144,64]{0,1:T(8,128)S(1)} %get-tuple-element.216, f32[6144,64]{0,1:T(8,128)S(1)} %get-tuple-element.213), kind=kOutput, calls=%fused_computation.112 | convolution fusion | flops 3241760512 | bytes 15423488 | tf_op jit(solution)/shard_map/dot_general | solution.py:128
  513.2 5.7 %collective-permute-done.21 = f32[12,12,64]{2,1,0:T(8,128)S(1)} collective-permute-done((f32[12,12,64]{2,1,0:T(8,128)S(1)}, f32[12,12,64]{2,1,0:T(8,128)S(1)}, u32[]{:S(2)}, u32[]{:S(2)}) %collective-permute-start.21) | collective-permute-done | bytes 36896 | tf_op jit(solution)/shard_map/ppermute | solution.py:23
  (291 shorter events, 147.5 us)
Async XLA Ops:
  0.0 98.0 %copy-start = (f32[343,343]{1,0:T(8,128)S(1)}, f32[343,343]{1,0:T(8,128)}, u32[]{:S(2)}) copy-start(f32[343,343]{1,0:T(8,128)} %param.42) | copy-start | bytes 1411792
  1.2 27.3 %copy-start.5 = (f32[12,6,12,64]{3,2,1,0:T(8,128)}, f32[12,6,12,64]{3,2,1,0:T(8,128)S(1)}, u32[]{:S(2)}) copy-start(f32[12,6,12,64]{3,2,1,0:T(8,128)S(1)} %reshape.636) | copy-start | bytes 663556
  1.2 35.3 %collective-permute-start = (f32[12,1,12,64]{3,2,1,0:T(8,128)S(1)}, f32[12,1,12,64]{3,2,1,0:T(8,128)S(1)}, u32[]{:S(2)}, u32[]{:S(2)}) collective-permute-start(f32[12,1,12,64]{3,2,1,0:T(8,128)S(1)} %slice.1004), channel_id=1, source_target_pairs={{0,7},{1,0},{2,1},{3,2},{4,3},{5,4},{6,5},{7,6},{8,15},{9,8},{10,9... | collective-permute-start | bytes 110600 | tf_op jit(solution)/shard_map/ppermute | solution.py:23
  5.3 31.2 %collective-permute-start.2 = (f32[1,1,12,64]{3,2,1,0:T(8,128)S(1)}, f32[1,1,12,64]{3,2,1,0:T(8,128)S(1)}, u32[]{:S(2)}, u32[]{:S(2)}) collective-permute-start(f32[1,1,12,64]{3,2,1,0:T(8,128)S(1)} %slice.1006), channel_id=1, source_target_pairs={{0,127},{1,120},{2,121},{3,122},{4,123},{5,124},{6,125},{7,126},{8... | collective-permute-start | bytes 9224 | tf_op jit(solution)/shard_map/ppermute | solution.py:34
  11.0 25.5 %collective-permute-start.1 = (f32[1,6,12,64]{3,2,1,0:T(8,128)S(1)}, f32[1,6,12,64]{3,2,1,0:T(8,128)S(1)}, u32[]{:S(2)}, u32[]{:S(2)}) collective-permute-start(f32[1,6,12,64]{3,2,1,0:T(8,128)S(1)} %slice.864), channel_id=1, source_target_pairs={{0,120},{8,0},{16,8},{24,16},{32,24},{40,32},{48,40},{56,48},{64,5... | collective-permute-start | bytes 55304 | tf_op jit(solution)/shard_map/ppermute | solution.py:23
  14.4 109.0 %copy-start.11 = (f32[6144,1]{0,1:T(1,128)}, f32[6144,1]{0,1:T(1,128)S(1)}, u32[]{:S(2)}) copy-start(f32[6144,1]{0,1:T(1,128)S(1)} %get-tuple-element.277) | copy-start | bytes 73732
  51.9 29.9 %all-to-all-start = ((f32[128,24,128]{2,1,0:T(8,128)}), f32[128,24,128]{2,1,0:T(8,128)S(1)}, u32[]{:S(2)}, u32[]{:S(2)}) async-start(f32[128,24,128]{2,1,0:T(8,128)} %pad_maximum_fusion.4), calls=%async_computation | async-start | bytes 3145728 | tf_op jit(solution)/shard_map/all_to_all | solution.py:89
  88.7 29.6 %all-to-all-start.1 = ((f32[128,24,128]{2,1,0:T(8,128)}), f32[128,24,128]{2,1,0:T(8,128)S(1)}, u32[]{:S(2)}, u32[]{:S(2)}) async-start(f32[128,24,128]{2,1,0:T(8,128)} %copy.191), calls=%async_computation.1 | async-start | bytes 3145728 | tf_op jit(solution)/shard_map/all_to_all | solution.py:89
  139.5 6.9 %collective-permute-start.3 = (f32[12,12,64]{2,1,0:T(8,128)S(1)}, f32[12,12,64]{2,1,0:T(8,128)S(1)}, u32[]{:S(2)}, u32[]{:S(2)}) collective-permute-start(f32[12,12,64]{2,1,0:T(8,128)S(1)} %slice_bitcast_fusion.20), channel_id=1, source_target_pairs={{0,1},{1,2},{2,3},{3,4},{4,5},{5,6},{6,7},{7,0},{8,9},{9,10},{10,1... | collective-permute-start | bytes 110600 | tf_op jit(solution)/shard_map/ppermute | solution.py:23
  139.7 7.2 %collective-permute-start.4 = (f32[6,12,64]{2,1,0:T(8,128)S(1)}, f32[6,12,64]{2,1,0:T(8,128)S(1)}, u32[]{:S(2)}, u32[]{:S(2)}) collective-permute-start(f32[6,12,64]{2,1,0:T(8,128)S(1)} %slice_bitcast_fusion.24), channel_id=1, source_target_pairs={{0,8},{8,16},{16,24},{24,32},{32,40},{40,48},{48,56},{56,64},{64,7... | collective-permute-start | bytes 55304 | tf_op jit(solution)/shard_map/ppermute | solution.py:23
  139.8 10.1 %collective-permute-start.5 = (f32[12,64]{1,0:T(8,128)S(1)}, f32[12,64]{1,0:T(8,128)S(1)}, u32[]{:S(2)}, u32[]{:S(2)}) collective-permute-start(f32[12,64]{1,0:T(8,128)S(1)} %slice_bitcast_fusion.28), channel_id=1, source_target_pairs={{0,9},{1,10},{2,11},{3,12},{4,13},{5,14},{6,15},{7,8},{8,17},{9,18... | collective-permute-start | bytes 9224 | tf_op jit(solution)/shard_map/ppermute | solution.py:34
  150.2 6.1 %collective-permute-start.6 = (f32[12,1,12,64]{3,2,1,0:T(8,128)S(1)}, f32[12,1,12,64]{3,2,1,0:T(8,128)S(1)}, u32[]{:S(2)}, u32[]{:S(2)}) collective-permute-start(f32[12,1,12,64]{3,2,1,0:T(8,128)S(1)} %slice.1035), channel_id=1, source_target_pairs={{0,7},{1,0},{2,1},{3,2},{4,3},{5,4},{6,5},{7,6},{8,15},{9,8},{10,9... | collective-permute-start | bytes 110600 | tf_op jit(solution)/shard_map/ppermute | solution.py:23
  152.1 4.1 collective-permute-start.7
  153.2 3.1 collective-permute-start.8
  210.3 29.4 %all-to-all-start.3 = ((f32[128,24,128]{2,1,0:T(8,128)}), f32[128,24,128]{2,1,0:T(8,128)S(1)}, u32[]{:S(2)}, u32[]{:S(2)}) async-start(f32[128,24,128]{2,1,0:T(8,128)} %copy.210), calls=%async_computation.3 | async-start | bytes 3145728 | tf_op jit(solution)/shard_map/all_to_all | solution.py:89
  263.8 6.7 %collective-permute-start.9 = (f32[12,12,64]{2,1,0:T(8,128)S(1)}, f32[12,12,64]{2,1,0:T(8,128)S(1)}, u32[]{:S(2)}, u32[]{:S(2)}) collective-permute-start(f32[12,12,64]{2,1,0:T(8,128)S(1)} %slice_bitcast_fusion.19), channel_id=1, source_target_pairs={{0,1},{1,2},{2,3},{3,4},{4,5},{5,6},{6,7},{7,0},{8,9},{9,10},{10,1... | collective-permute-start | bytes 110600 | tf_op jit(solution)/shard_map/ppermute | solution.py:23
  265.6 7.2 %collective-permute-start.10 = (f32[6,12,64]{2,1,0:T(8,128)S(1)}, f32[6,12,64]{2,1,0:T(8,128)S(1)}, u32[]{:S(2)}, u32[]{:S(2)}) collective-permute-start(f32[6,12,64]{2,1,0:T(8,128)S(1)} %slice_bitcast_fusion.23), channel_id=1, source_target_pairs={{0,8},{8,16},{16,24},{24,32},{32,40},{40,48},{48,56},{56,64},{64,7... | collective-permute-start | bytes 55304 | tf_op jit(solution)/shard_map/ppermute | solution.py:23
  265.7 10.1 %collective-permute-start.11 = (f32[12,64]{1,0:T(8,128)S(1)}, f32[12,64]{1,0:T(8,128)S(1)}, u32[]{:S(2)}, u32[]{:S(2)}) collective-permute-start(f32[12,64]{1,0:T(8,128)S(1)} %slice_bitcast_fusion.27), channel_id=1, source_target_pairs={{0,9},{1,10},{2,11},{3,12},{4,13},{5,14},{6,15},{7,8},{8,17},{9,18... | collective-permute-start | bytes 9224 | tf_op jit(solution)/shard_map/ppermute | solution.py:34
  276.1 6.1 %collective-permute-start.12 = (f32[12,1,12,64]{3,2,1,0:T(8,128)S(1)}, f32[12,1,12,64]{3,2,1,0:T(8,128)S(1)}, u32[]{:S(2)}, u32[]{:S(2)}) collective-permute-start(f32[12,1,12,64]{3,2,1,0:T(8,128)S(1)} %slice.1060), channel_id=1, source_target_pairs={{0,7},{1,0},{2,1},{3,2},{4,3},{5,4},{6,5},{7,6},{8,15},{9,8},{10,9... | collective-permute-start | bytes 110600 | tf_op jit(solution)/shard_map/ppermute | solution.py:23
  278.0 4.1 collective-permute-start.13
  279.1 3.1 collective-permute-start.14
  337.7 29.4 %all-to-all-start.5 = ((f32[128,24,128]{2,1,0:T(8,128)}), f32[128,24,128]{2,1,0:T(8,128)S(1)}, u32[]{:S(2)}, u32[]{:S(2)}) async-start(f32[128,24,128]{2,1,0:T(8,128)} %copy.229), calls=%async_computation.5 | async-start | bytes 3145728 | tf_op jit(solution)/shard_map/all_to_all | solution.py:89
  389.9 6.9 %collective-permute-start.15 = (f32[12,12,64]{2,1,0:T(8,128)S(1)}, f32[12,12,64]{2,1,0:T(8,128)S(1)}, u32[]{:S(2)}, u32[]{:S(2)}) collective-permute-start(f32[12,12,64]{2,1,0:T(8,128)S(1)} %slice_bitcast_fusion.18), channel_id=1, source_target_pairs={{0,1},{1,2},{2,3},{3,4},{4,5},{5,6},{6,7},{7,0},{8,9},{9,10},{10,1... | collective-permute-start | bytes 110600 | tf_op jit(solution)/shard_map/ppermute | solution.py:23
  390.1 7.2 %collective-permute-start.16 = (f32[6,12,64]{2,1,0:T(8,128)S(1)}, f32[6,12,64]{2,1,0:T(8,128)S(1)}, u32[]{:S(2)}, u32[]{:S(2)}) collective-permute-start(f32[6,12,64]{2,1,0:T(8,128)S(1)} %slice_bitcast_fusion.22), channel_id=1, source_target_pairs={{0,8},{8,16},{16,24},{24,32},{32,40},{40,48},{48,56},{56,64},{64,7... | collective-permute-start | bytes 55304 | tf_op jit(solution)/shard_map/ppermute | solution.py:23
  390.2 10.1 %collective-permute-start.17 = (f32[12,64]{1,0:T(8,128)S(1)}, f32[12,64]{1,0:T(8,128)S(1)}, u32[]{:S(2)}, u32[]{:S(2)}) collective-permute-start(f32[12,64]{1,0:T(8,128)S(1)} %slice_bitcast_fusion.26), channel_id=1, source_target_pairs={{0,9},{1,10},{2,11},{3,12},{4,13},{5,14},{6,15},{7,8},{8,17},{9,18... | collective-permute-start | bytes 9224 | tf_op jit(solution)/shard_map/ppermute | solution.py:34
  400.6 6.1 %collective-permute-start.18 = (f32[12,1,12,64]{3,2,1,0:T(8,128)S(1)}, f32[12,1,12,64]{3,2,1,0:T(8,128)S(1)}, u32[]{:S(2)}, u32[]{:S(2)}) collective-permute-start(f32[12,1,12,64]{3,2,1,0:T(8,128)S(1)} %slice.1085), channel_id=1, source_target_pairs={{0,7},{1,0},{2,1},{3,2},{4,3},{5,4},{6,5},{7,6},{8,15},{9,8},{10,9... | collective-permute-start | bytes 110600 | tf_op jit(solution)/shard_map/ppermute | solution.py:23
  402.5 4.1 collective-permute-start.19
  403.6 3.1 collective-permute-start.20
  461.5 29.6 %all-to-all-start.7 = ((f32[128,24,128]{2,1,0:T(8,128)}), f32[128,24,128]{2,1,0:T(8,128)S(1)}, u32[]{:S(2)}, u32[]{:S(2)}) async-start(f32[128,24,128]{2,1,0:T(8,128)} %copy.248), calls=%async_computation.7 | async-start | bytes 3145728 | tf_op jit(solution)/shard_map/all_to_all | solution.py:89
  512.0 6.9 %collective-permute-start.21 = (f32[12,12,64]{2,1,0:T(8,128)S(1)}, f32[12,12,64]{2,1,0:T(8,128)S(1)}, u32[]{:S(2)}, u32[]{:S(2)}) collective-permute-start(f32[12,12,64]{2,1,0:T(8,128)S(1)} %slice_bitcast_fusion.17), channel_id=1, source_target_pairs={{0,1},{1,2},{2,3},{3,4},{4,5},{5,6},{6,7},{7,0},{8,9},{9,10},{10,1... | collective-permute-start | bytes 110600 | tf_op jit(solution)/shard_map/ppermute | solution.py:23
  512.2 7.2 %collective-permute-start.22 = (f32[6,12,64]{2,1,0:T(8,128)S(1)}, f32[6,12,64]{2,1,0:T(8,128)S(1)}, u32[]{:S(2)}, u32[]{:S(2)}) collective-permute-start(f32[6,12,64]{2,1,0:T(8,128)S(1)} %slice_bitcast_fusion.21), channel_id=1, source_target_pairs={{0,8},{8,16},{16,24},{24,32},{32,40},{40,48},{48,56},{56,64},{64,7... | collective-permute-start | bytes 55304 | tf_op jit(solution)/shard_map/ppermute | solution.py:23
  512.3 9.9 %collective-permute-start.23 = (f32[12,64]{1,0:T(8,128)S(1)}, f32[12,64]{1,0:T(8,128)S(1)}, u32[]{:S(2)}, u32[]{:S(2)}) collective-permute-start(f32[12,64]{1,0:T(8,128)S(1)} %slice_bitcast_fusion.25), channel_id=1, source_target_pairs={{0,9},{1,10},{2,11},{3,12},{4,13},{5,14},{6,15},{7,8},{8,17},{9,18... | collective-permute-start | bytes 9224 | tf_op jit(solution)/shard_map/ppermute | solution.py:34
  (28 other events, 216.3 us)

commit v8 on v5

--- a/solution.py
+++ b/solution.py
@@ -54,15 +54,21 @@
 def scatter_cells(cell_out, columns):
     cells = cell_out.shape[1] // columns
     blocks = cell_out.reshape(DEG + 1, DEG + 1, DEG + 1, cells, columns)
-    nx, ny, nz = CX * DEG + 1, CY * DEG + 1, CZ * DEG + 1
+    nx, ny = CX * DEG + 1, CY * DEG + 1
     total = None
     for index, (x0, y0, z0) in enumerate(cell_ranges()):
-        padded = jnp.pad(
-            blocks[:, :, :, index],
-            ((x0, nx - x0 - DEG - 1), (y0, ny - y0 - DEG - 1), (z0, nz - z0 - DEG - 1), (0, 0)),
-        )
-        total = padded if total is None else total + padded
-    return total[:, :, :ZN].at[:, :, 0].add(total[:, :, ZN])
+        block = blocks[:, :, :, index]
+        spans = ((x0, nx - x0 - DEG - 1), (y0, ny - y0 - DEG - 1))
+        if z0 + DEG < ZN:
+            pieces = [jnp.pad(block, spans + ((z0, ZN - z0 - DEG - 1), (0, 0)))]
+        else:
+            pieces = [
+                jnp.pad(block[:, :, :DEG], spans + ((z0, ZN - z0 - DEG), (0, 0))),
+                jnp.pad(block[:, :, DEG:], spans + ((0, ZN - 1), (0, 0))),
+            ]
+        for padded in pieces:
+            total = padded if total is None else total + padded
+    return total
 
 
 def body(wavefunctions, potential, cell_matrix, pair_cell, pair_tile, slot_atom, coupling, bounds):

time: 533 us -> 520 us (0.976)
  local copies, waits for them, and re-layouts: 99 us -> 86.4 us
    scatter-add x4 -> x0, local copies, waits for them, and re-layouts: 11 us -> none  [scatter_cells(): return total[:, :, :ZN].at[:, :, 0].add(total[:, :, ZN])]
    unnamed x74 -> x76, local copies, waits for them, and re-layouts: 18.3 us -> 19.1 us
where the time goes in v8:
time: 520 us; the launch traced here: 512 us
  waiting for transfers between devices  157 us (30%)
  matrix products  97.9 us (19%)
  blocking collectives  97.6 us (19%)
  local copies, waits for them, and re-layouts  86.4 us (17%)
  starting transfers between devices  49.6 us (10%)
  other arithmetic  15.2 us (3%)
  between operations  8.35 us (2%)
    all_to_all x5, waiting for transfers between devices, exchange(): lax.all_to_all(values, ('gx', 'gy'), split_axis=0, concat_axis=0, tiled=T...  112 us
    all_to_all x3, blocking collectives, exchange(): lax.all_to_all(values, ('gx', 'gy'), split_axis=0, concat_axis=0, tiled=T...  97.6 us
    dot_general x4, matrix products, apply_operator(): jnp.dot(tile_t, spread_in, precision=DENSE)  45.5 us
    dot_general x4, matrix products, apply_operator(): every_cell = jnp.dot(tile_all, cell_in, precision=DENSE)  31.5 us
    all_to_all x5, starting transfers between devices, exchange(): lax.all_to_all(values, ('gx', 'gy'), split_axis=0, concat_axis=0, tiled=T...  24.6 us
    ppermute x16, waiting for transfers between devices, shifted(): return lax.ppermute(value, axis, pairs)  24.5 us
    ppermute x8, waiting for transfers between devices, diagonal(): return lax.ppermute(value, ('gx', 'gy'), pairs)  20.4 us
    unnamed x76, local copies, waits for them, and re-layouts  19.1 us
  transfers between devices with their start and end apart: 29, of which 20 were waited for; matrix products, arithmetic and copies ran while one was open for 6% of the time, Pallas kernels for 0%

profile of v8, /device:TPU:0, one launch (start us, length us, event | category | flops | bytes accessed | tf_op | source)
XLA Modules:
  0.0 512.4 jit_solution(18270487828248942439)
XLA Ops:
  1.2 4.1 collective-permute-start
  5.3 4.6 collective-permute-start.2
  14.4 14.1 %copy.285 = f32[1,256,18,343]{3,2,1,0:T(8,128)} copy(f32[1,256,18,343]{1,0,3,2:T(1,128)} %param.36) | data formatting | bytes 12644352
  28.5 8.0 %pad.118.clone = f32[256,24,343]{2,1,0:T(8,128)} pad(f32[256,18,343]{2,1,0:T(8,128)} %bitcast.312, f32[]{:T(128)} %constant.278.clone.1), padding=0_0x0_6x0_0 | pad | bytes 14751748 | tf_op jit(solution)/shard_map/jit(_pad)/pad | solution.py:87
  37.3 7.9 %fusion.179 = f32[6144,256]{0,1:T(8,128)S(1)} fusion(f32[6144,343]{1,0:T(8,128)} %bitcast.304, f32[343,256]{1,0:T(8,128)S(1)} %reshape.508), kind=kOutput, calls=%fused_computation.328 | convolution fusion | flops 3236954112 | bytes 15072256 | tf_op jit(solution)/shard_map/dot_general | solution.py:121
  51.8 5.2 %all-to-all-start = ((f32[128,24,128]{2,1,0:T(8,128)}), f32[128,24,128]{2,1,0:T(8,128)S(1)}, u32[]{:S(2)}, u32[]{:S(2)}) async-start(f32[128,24,128]{2,1,0:T(8,128)} %pad_maximum_fusion.4), calls=%async_computation | async-start | bytes 3145728 | tf_op jit(solution)/shard_map/all_to_all | solution.py:95
  59.7 21.9 %all-to-all-done = f32[128,24,128]{2,1,0:T(8,128)S(1)} async-done(((f32[128,24,128]{2,1,0:T(8,128)}), f32[128,24,128]{2,1,0:T(8,128)S(1)}, u32[]{:S(2)}, u32[]{:S(2)}) %all-to-all-start) | async-done | bytes 1572896 | tf_op jit(solution)/shard_map/all_to_all | solution.py:95
  88.6 4.9 all-to-all-start.1
  98.0 20.2 %all-to-all-done.1 = f32[128,24,128]{2,1,0:T(8,128)S(1)} async-done(((f32[128,24,128]{2,1,0:T(8,128)}), f32[128,24,128]{2,1,0:T(8,128)S(1)}, u32[]{:S(2)}, u32[]{:S(2)}) %all-to-all-start.1) | async-done | bytes 1572896 | tf_op jit(solution)/shard_map/all_to_all | solution.py:95
  124.0 11.4 %fusion = f32[343,256]{1,0:T(8,128)S(1)} fusion(f32[6144,343]{1,0:T(8,128)} %bitcast.305, f32[6144,64]{0,1:T(8,128)S(1)} %get-tuple-element.190, f32[6144,64]{0,1:T(8,128)S(1)} %get-tuple-element.191, f32[6144,64]{0,1:T(8,128)S(1)} %get-tuple-element.192, f32[6144,64]{0,1:T(8,128)S(1)} %get-tuple-element.189), kind=kOutput, calls=%fused_computation | convolution fusion | flops 3241672704 | bytes 15072256 | tf_op jit(solution)/shard_map/dot_general | solution.py:133
  138.3 5.7 %collective-permute-done.3 = f32[12,12,64]{2,1,0:T(8,128)S(1)} collective-permute-done((f32[12,12,64]{2,1,0:T(8,128)S(1)}, f32[12,12,64]{2,1,0:T(8,128)S(1)}, u32[]{:S(2)}, u32[]{:S(2)}) %collective-permute-start.3) | collective-permute-done | bytes 36896 | tf_op jit(solution)/shard_map/ppermute | solution.py:23
  150.9 3.1 collective-permute-done.8
  155.6 7.9 %fusion.180 = f32[6144,256]{0,1:T(8,128)S(1)} fusion(f32[6144,343]{1,0:T(8,128)} %bitcast.306, f32[343,256]{1,0:T(8,128)S(1)} %reshape.517), kind=kOutput, calls=%fused_computation.329 | convolution fusion | flops 3236954112 | bytes 15072256 | tf_op jit(solution)/shard_map/dot_general | solution.py:121
  168.9 32.2 %all_to_all.40 = f32[128,24,128]{2,1,0:T(8,128)S(1)} all-to-all(f32[128,24,128]{2,1,0:T(8,128)S(1)} %pad_maximum_fusion.6), channel_id=1, replica_groups=mesh['gx'=16,'gy'=8] {'gx','gy'}, dimensions={0} | all-to-all | bytes 3145728 | tf_op jit(solution)/shard_map/all_to_all | solution.py:95
  209.1 4.8 all-to-all-start.3
  214.1 24.5 %all-to-all-done.3 = f32[128,24,128]{2,1,0:T(8,128)S(1)} async-done(((f32[128,24,128]{2,1,0:T(8,128)}), f32[128,24,128]{2,1,0:T(8,128)S(1)}, u32[]{:S(2)}, u32[]{:S(2)}) %all-to-all-start.3) | async-done | bytes 1572896 | tf_op jit(solution)/shard_map/all_to_all | solution.py:95
  241.3 3.3 copy.212
  246.6 11.4 %fusion.8 = f32[343,256]{1,0:T(8,128)S(1)} fusion(f32[6144,343]{1,0:T(8,128)} %bitcast.307, f32[6144,64]{0,1:T(8,128)S(1)} %get-tuple-element.182, f32[6144,64]{0,1:T(8,128)S(1)} %get-tuple-element.183, f32[6144,64]{0,1:T(8,128)S(1)} %get-tuple-element.184, f32[6144,64]{0,1:T(8,128)S(1)} %get-tuple-element.181), kind=kOutput, calls=%fused_computation.8 | convolution fusion | flops 3241672704 | bytes 15072256 | tf_op jit(solution)/shard_map/dot_general | solution.py:133
  260.9 5.7 %collective-permute-done.9 = f32[12,12,64]{2,1,0:T(8,128)S(1)} collective-permute-done((f32[12,12,64]{2,1,0:T(8,128)S(1)}, f32[12,12,64]{2,1,0:T(8,128)S(1)}, u32[]{:S(2)}, u32[]{:S(2)}) %collective-permute-start.9) | collective-permute-done | bytes 36896 | tf_op jit(solution)/shard_map/ppermute | solution.py:23
  273.3 3.1 collective-permute-done.14
  278.0 7.9 %fusion.181 = f32[6144,256]{0,1:T(8,128)S(1)} fusion(f32[6144,343]{1,0:T(8,128)} %bitcast.308, f32[343,256]{1,0:T(8,128)S(1)} %reshape.524), kind=kOutput, calls=%fused_computation.330 | convolution fusion | flops 3236954112 | bytes 15072256 | tf_op jit(solution)/shard_map/dot_general | solution.py:121
  291.3 32.7 %all_to_all.41 = f32[128,24,128]{2,1,0:T(8,128)S(1)} all-to-all(f32[128,24,128]{2,1,0:T(8,128)S(1)} %pad_maximum_fusion.8), channel_id=1, replica_groups=mesh['gx'=16,'gy'=8] {'gx','gy'}, dimensions={0} | all-to-all | bytes 3145728 | tf_op jit(solution)/shard_map/all_to_all | solution.py:95
  331.9 4.8 all-to-all-start.5
  340.0 21.3 %all-to-all-done.5 = f32[128,24,128]{2,1,0:T(8,128)S(1)} async-done(((f32[128,24,128]{2,1,0:T(8,128)}), f32[128,24,128]{2,1,0:T(8,128)S(1)}, u32[]{:S(2)}, u32[]{:S(2)}) %all-to-all-start.5) | async-done | bytes 1572896 | tf_op jit(solution)/shard_map/all_to_all | solution.py:95
  367.9 11.4 %fusion.16 = f32[343,256]{1,0:T(8,128)S(1)} fusion(f32[6144,343]{1,0:T(8,128)} %bitcast.309, f32[6144,64]{0,1:T(8,128)S(1)} %get-tuple-element.174, f32[6144,64]{0,1:T(8,128)S(1)} %get-tuple-element.175, f32[6144,64]{0,1:T(8,128)S(1)} %get-tuple-element.176, f32[6144,64]{0,1:T(8,128)S(1)} %get-tuple-element.173), kind=kOutput, calls=%fused_computation.16 | convolution fusion | flops 3241672704 | bytes 15072256 | tf_op jit(solution)/shard_map/dot_general | solution.py:133
  382.2 5.7 %collective-permute-done.15 = f32[12,12,64]{2,1,0:T(8,128)S(1)} collective-permute-done((f32[12,12,64]{2,1,0:T(8,128)S(1)}, f32[12,12,64]{2,1,0:T(8,128)S(1)}, u32[]{:S(2)}, u32[]{:S(2)}) %collective-permute-start.15) | collective-permute-done | bytes 36896 | tf_op jit(solution)/shard_map/ppermute | solution.py:23
  399.3 7.9 %fusion.182 = f32[6144,256]{0,1:T(8,128)S(1)} fusion(f32[6144,343]{1,0:T(8,128)} %bitcast.310, f32[343,256]{1,0:T(8,128)S(1)} %reshape.531), kind=kOutput, calls=%fused_computation.331 | convolution fusion | flops 3236954112 | bytes 15072256 | tf_op jit(solution)/shard_map/dot_general | solution.py:121
  412.7 32.7 %all_to_all.42 = f32[128,24,128]{2,1,0:T(8,128)S(1)} all-to-all(f32[128,24,128]{2,1,0:T(8,128)S(1)} %pad_maximum_fusion.10), channel_id=1, replica_groups=mesh['gx'=16,'gy'=8] {'gx','gy'}, dimensions={0} | all-to-all | bytes 3145728 | tf_op jit(solution)/shard_map/all_to_all | solution.py:95
  452.5 4.8 all-to-all-start.7
  457.5 24.5 %all-to-all-done.7 = f32[128,24,128]{2,1,0:T(8,128)S(1)} async-done(((f32[128,24,128]{2,1,0:T(8,128)}), f32[128,24,128]{2,1,0:T(8,128)S(1)}, u32[]{:S(2)}, u32[]{:S(2)}) %all-to-all-start.7) | async-done | bytes 1572896 | tf_op jit(solution)/shard_map/all_to_all | solution.py:95
  487.8 11.4 %fusion.24 = f32[343,256]{1,0:T(8,128)S(1)} fusion(f32[6144,343]{1,0:T(8,128)} %bitcast.311, f32[6144,64]{0,1:T(8,128)S(1)} %get-tuple-element.166, f32[6144,64]{0,1:T(8,128)S(1)} %get-tuple-element.167, f32[6144,64]{0,1:T(8,128)S(1)} %get-tuple-element.168, f32[6144,64]{0,1:T(8,128)S(1)} %get-tuple-element.165), kind=kOutput, calls=%fused_computation.24 | convolution fusion | flops 3241672704 | bytes 15072256 | tf_op jit(solution)/shard_map/dot_general | solution.py:133
  502.1 5.7 %collective-permute-done.21 = f32[12,12,64]{2,1,0:T(8,128)S(1)} collective-permute-done((f32[12,12,64]{2,1,0:T(8,128)S(1)}, f32[12,12,64]{2,1,0:T(8,128)S(1)}, u32[]{:S(2)}, u32[]{:S(2)}) %collective-permute-start.21) | collective-permute-done | bytes 36896 | tf_op jit(solution)/shard_map/ppermute | solution.py:23
  (289 shorter events, 129.5 us)
Async XLA Ops:
  0.0 135.4 %copy-start = (f32[343,343]{1,0:T(8,128)S(1)}, f32[343,343]{1,0:T(8,128)}, u32[]{:S(2)}) copy-start(f32[343,343]{1,0:T(8,128)} %param.34) | copy-start | bytes 1411792
  1.2 27.3 %copy-start.3 = (f32[12,6,12,64]{3,2,1,0:T(8,128)}, f32[12,6,12,64]{3,2,1,0:T(8,128)S(1)}, u32[]{:S(2)}) copy-start(f32[12,6,12,64]{3,2,1,0:T(8,128)S(1)} %reshape.507) | copy-start | bytes 663556
  1.2 35.3 %collective-permute-start = (f32[12,1,12,64]{3,2,1,0:T(8,128)S(1)}, f32[12,1,12,64]{3,2,1,0:T(8,128)S(1)}, u32[]{:S(2)}, u32[]{:S(2)}) collective-permute-start(f32[12,1,12,64]{3,2,1,0:T(8,128)S(1)} %slice.920), channel_id=1, source_target_pairs={{0,7},{1,0},{2,1},{3,2},{4,3},{5,4},{6,5},{7,6},{8,15},{9,8},{10,9... | collective-permute-start | bytes 110600 | tf_op jit(solution)/shard_map/ppermute | solution.py:23
  5.3 31.2 %collective-permute-start.2 = (f32[1,1,12,64]{3,2,1,0:T(8,128)S(1)}, f32[1,1,12,64]{3,2,1,0:T(8,128)S(1)}, u32[]{:S(2)}, u32[]{:S(2)}) collective-permute-start(f32[1,1,12,64]{3,2,1,0:T(8,128)S(1)} %slice.922), channel_id=1, source_target_pairs={{0,127},{1,120},{2,121},{3,122},{4,123},{5,124},{6,125},{7,126},{8... | collective-permute-start | bytes 9224 | tf_op jit(solution)/shard_map/ppermute | solution.py:34
  11.0 25.5 %collective-permute-start.1 = (f32[1,6,12,64]{3,2,1,0:T(8,128)S(1)}, f32[1,6,12,64]{3,2,1,0:T(8,128)S(1)}, u32[]{:S(2)}, u32[]{:S(2)}) collective-permute-start(f32[1,6,12,64]{3,2,1,0:T(8,128)S(1)} %slice.776), channel_id=1, source_target_pairs={{0,120},{8,0},{16,8},{24,16},{32,24},{40,32},{48,40},{56,48},{64,5... | collective-permute-start | bytes 55304 | tf_op jit(solution)/shard_map/ppermute | solution.py:23
  14.4 109.0 %copy-start.12 = (f32[6144,1]{0,1:T(1,128)}, f32[6144,1]{0,1:T(1,128)S(1)}, u32[]{:S(2)}) copy-start(f32[6144,1]{0,1:T(1,128)S(1)} %get-tuple-element.229) | copy-start | bytes 73732
  51.8 29.9 %all-to-all-start = ((f32[128,24,128]{2,1,0:T(8,128)}), f32[128,24,128]{2,1,0:T(8,128)S(1)}, u32[]{:S(2)}, u32[]{:S(2)}) async-start(f32[128,24,128]{2,1,0:T(8,128)} %pad_maximum_fusion.4), calls=%async_computation | async-start | bytes 3145728 | tf_op jit(solution)/shard_map/all_to_all | solution.py:95
  88.6 29.6 %all-to-all-start.1 = ((f32[128,24,128]{2,1,0:T(8,128)}), f32[128,24,128]{2,1,0:T(8,128)S(1)}, u32[]{:S(2)}, u32[]{:S(2)}) async-start(f32[128,24,128]{2,1,0:T(8,128)} %copy.191), calls=%async_computation.1 | async-start | bytes 3145728 | tf_op jit(solution)/shard_map/all_to_all | solution.py:95
  137.1 6.9 %collective-permute-start.3 = (f32[12,12,64]{2,1,0:T(8,128)S(1)}, f32[12,12,64]{2,1,0:T(8,128)S(1)}, u32[]{:S(2)}, u32[]{:S(2)}) collective-permute-start(f32[12,12,64]{2,1,0:T(8,128)S(1)} %add_bitcast_fusion.3), channel_id=1, source_target_pairs={{0,1},{1,2},{2,3},{3,4},{4,5},{5,6},{6,7},{7,0},{8,9},{9,10},{10,1... | collective-permute-start | bytes 110600 | tf_op jit(solution)/shard_map/ppermute | solution.py:23
  137.2 7.2 %collective-permute-start.4 = (f32[6,12,64]{2,1,0:T(8,128)S(1)}, f32[6,12,64]{2,1,0:T(8,128)S(1)}, u32[]{:S(2)}, u32[]{:S(2)}) collective-permute-start(f32[6,12,64]{2,1,0:T(8,128)S(1)} %add_bitcast_fusion.7), channel_id=1, source_target_pairs={{0,8},{8,16},{16,24},{24,32},{32,40},{40,48},{48,56},{56,64},{64,7... | collective-permute-start | bytes 55304 | tf_op jit(solution)/shard_map/ppermute | solution.py:23
  137.3 9.9 %collective-permute-start.5 = (f32[12,64]{1,0:T(8,128)S(1)}, f32[12,64]{1,0:T(8,128)S(1)}, u32[]{:S(2)}, u32[]{:S(2)}) collective-permute-start(f32[12,64]{1,0:T(8,128)S(1)} %add_bitcast_fusion.11), channel_id=1, source_target_pairs={{0,9},{1,10},{2,11},{3,12},{4,13},{5,14},{6,15},{7,8},{8,17},{9,18... | collective-permute-start | bytes 9224 | tf_op jit(solution)/shard_map/ppermute | solution.py:34
  147.5 6.5 %collective-permute-start.6 = (f32[12,1,12,64]{3,2,1,0:T(8,128)S(1)}, f32[12,1,12,64]{3,2,1,0:T(8,128)S(1)}, u32[]{:S(2)}, u32[]{:S(2)}) collective-permute-start(f32[12,1,12,64]{3,2,1,0:T(8,128)S(1)} %slice.950), channel_id=1, source_target_pairs={{0,7},{1,0},{2,1},{3,2},{4,3},{5,4},{6,5},{7,6},{8,15},{9,8},{10,9... | collective-permute-start | bytes 110600 | tf_op jit(solution)/shard_map/ppermute | solution.py:23
  149.8 4.2 collective-permute-start.7
  150.9 3.1 collective-permute-start.8
  209.1 29.4 %all-to-all-start.3 = ((f32[128,24,128]{2,1,0:T(8,128)}), f32[128,24,128]{2,1,0:T(8,128)S(1)}, u32[]{:S(2)}, u32[]{:S(2)}) async-start(f32[128,24,128]{2,1,0:T(8,128)} %copy.210), calls=%async_computation.3 | async-start | bytes 3145728 | tf_op jit(solution)/shard_map/all_to_all | solution.py:95
  259.7 6.9 %collective-permute-start.9 = (f32[12,12,64]{2,1,0:T(8,128)S(1)}, f32[12,12,64]{2,1,0:T(8,128)S(1)}, u32[]{:S(2)}, u32[]{:S(2)}) collective-permute-start(f32[12,12,64]{2,1,0:T(8,128)S(1)} %add_bitcast_fusion.2), channel_id=1, source_target_pairs={{0,1},{1,2},{2,3},{3,4},{4,5},{5,6},{6,7},{7,0},{8,9},{9,10},{10,1... | collective-permute-start | bytes 110600 | tf_op jit(solution)/shard_map/ppermute | solution.py:23
  259.8 7.2 %collective-permute-start.10 = (f32[6,12,64]{2,1,0:T(8,128)S(1)}, f32[6,12,64]{2,1,0:T(8,128)S(1)}, u32[]{:S(2)}, u32[]{:S(2)}) collective-permute-start(f32[6,12,64]{2,1,0:T(8,128)S(1)} %add_bitcast_fusion.6), channel_id=1, source_target_pairs={{0,8},{8,16},{16,24},{24,32},{32,40},{40,48},{48,56},{56,64},{64,7... | collective-permute-start | bytes 55304 | tf_op jit(solution)/shard_map/ppermute | solution.py:23
  259.9 9.9 %collective-permute-start.11 = (f32[12,64]{1,0:T(8,128)S(1)}, f32[12,64]{1,0:T(8,128)S(1)}, u32[]{:S(2)}, u32[]{:S(2)}) collective-permute-start(f32[12,64]{1,0:T(8,128)S(1)} %add_bitcast_fusion.10), channel_id=1, source_target_pairs={{0,9},{1,10},{2,11},{3,12},{4,13},{5,14},{6,15},{7,8},{8,17},{9,18... | collective-permute-start | bytes 9224 | tf_op jit(solution)/shard_map/ppermute | solution.py:34
  270.1 6.3 %collective-permute-start.12 = (f32[12,1,12,64]{3,2,1,0:T(8,128)S(1)}, f32[12,1,12,64]{3,2,1,0:T(8,128)S(1)}, u32[]{:S(2)}, u32[]{:S(2)}) collective-permute-start(f32[12,1,12,64]{3,2,1,0:T(8,128)S(1)} %slice.974), channel_id=1, source_target_pairs={{0,7},{1,0},{2,1},{3,2},{4,3},{5,4},{6,5},{7,6},{8,15},{9,8},{10,9... | collective-permute-start | bytes 110600 | tf_op jit(solution)/shard_map/ppermute | solution.py:23
  272.2 4.2 collective-permute-start.13
  273.3 3.1 collective-permute-start.14
  331.9 29.4 %all-to-all-start.5 = ((f32[128,24,128]{2,1,0:T(8,128)}), f32[128,24,128]{2,1,0:T(8,128)S(1)}, u32[]{:S(2)}, u32[]{:S(2)}) async-start(f32[128,24,128]{2,1,0:T(8,128)} %copy.229), calls=%async_computation.5 | async-start | bytes 3145728 | tf_op jit(solution)/shard_map/all_to_all | solution.py:95
  381.0 6.9 %collective-permute-start.15 = (f32[12,12,64]{2,1,0:T(8,128)S(1)}, f32[12,12,64]{2,1,0:T(8,128)S(1)}, u32[]{:S(2)}, u32[]{:S(2)}) collective-permute-start(f32[12,12,64]{2,1,0:T(8,128)S(1)} %add_bitcast_fusion.1), channel_id=1, source_target_pairs={{0,1},{1,2},{2,3},{3,4},{4,5},{5,6},{6,7},{7,0},{8,9},{9,10},{10,1... | collective-permute-start | bytes 110600 | tf_op jit(solution)/shard_map/ppermute | solution.py:23
  381.2 7.2 %collective-permute-start.16 = (f32[6,12,64]{2,1,0:T(8,128)S(1)}, f32[6,12,64]{2,1,0:T(8,128)S(1)}, u32[]{:S(2)}, u32[]{:S(2)}) collective-permute-start(f32[6,12,64]{2,1,0:T(8,128)S(1)} %add_bitcast_fusion.5), channel_id=1, source_target_pairs={{0,8},{8,16},{16,24},{24,32},{32,40},{40,48},{48,56},{56,64},{64,7... | collective-permute-start | bytes 55304 | tf_op jit(solution)/shard_map/ppermute | solution.py:23
  381.2 9.9 %collective-permute-start.17 = (f32[12,64]{1,0:T(8,128)S(1)}, f32[12,64]{1,0:T(8,128)S(1)}, u32[]{:S(2)}, u32[]{:S(2)}) collective-permute-start(f32[12,64]{1,0:T(8,128)S(1)} %add_bitcast_fusion.9), channel_id=1, source_target_pairs={{0,9},{1,10},{2,11},{3,12},{4,13},{5,14},{6,15},{7,8},{8,17},{9,18... | collective-permute-start | bytes 9224 | tf_op jit(solution)/shard_map/ppermute | solution.py:34
  391.4 6.3 %collective-permute-start.18 = (f32[12,1,12,64]{3,2,1,0:T(8,128)S(1)}, f32[12,1,12,64]{3,2,1,0:T(8,128)S(1)}, u32[]{:S(2)}, u32[]{:S(2)}) collective-permute-start(f32[12,1,12,64]{3,2,1,0:T(8,128)S(1)} %slice.998), channel_id=1, source_target_pairs={{0,7},{1,0},{2,1},{3,2},{4,3},{5,4},{6,5},{7,6},{8,15},{9,8},{10,9... | collective-permute-start | bytes 110600 | tf_op jit(solution)/shard_map/ppermute | solution.py:23
  393.6 4.2 collective-permute-start.19
  394.6 3.1 collective-permute-start.20
  452.5 29.4 %all-to-all-start.7 = ((f32[128,24,128]{2,1,0:T(8,128)}), f32[128,24,128]{2,1,0:T(8,128)S(1)}, u32[]{:S(2)}, u32[]{:S(2)}) async-start(f32[128,24,128]{2,1,0:T(8,128)} %copy.248), calls=%async_computation.7 | async-start | bytes 3145728 | tf_op jit(solution)/shard_map/all_to_all | solution.py:95
  500.9 6.9 %collective-permute-start.21 = (f32[12,12,64]{2,1,0:T(8,128)S(1)}, f32[12,12,64]{2,1,0:T(8,128)S(1)}, u32[]{:S(2)}, u32[]{:S(2)}) collective-permute-start(f32[12,12,64]{2,1,0:T(8,128)S(1)} %add_bitcast_fusion), channel_id=1, source_target_pairs={{0,1},{1,2},{2,3},{3,4},{4,5},{5,6},{6,7},{7,0},{8,9},{9,10},{10,1... | collective-permute-start | bytes 110600 | tf_op jit(solution)/shard_map/ppermute | solution.py:23
  501.0 7.2 %collective-permute-start.22 = (f32[6,12,64]{2,1,0:T(8,128)S(1)}, f32[6,12,64]{2,1,0:T(8,128)S(1)}, u32[]{:S(2)}, u32[]{:S(2)}) collective-permute-start(f32[6,12,64]{2,1,0:T(8,128)S(1)} %add_bitcast_fusion.4), channel_id=1, source_target_pairs={{0,8},{8,16},{16,24},{24,32},{32,40},{40,48},{48,56},{56,64},{64,7... | collective-permute-start | bytes 55304 | tf_op jit(solution)/shard_map/ppermute | solution.py:23
  501.1 9.9 %collective-permute-start.23 = (f32[12,64]{1,0:T(8,128)S(1)}, f32[12,64]{1,0:T(8,128)S(1)}, u32[]{:S(2)}, u32[]{:S(2)}) collective-permute-start(f32[12,64]{1,0:T(8,128)S(1)} %add_bitcast_fusion.8), channel_id=1, source_target_pairs={{0,9},{1,10},{2,11},{3,12},{4,13},{5,14},{6,15},{7,8},{8,17},{9,18... | collective-permute-start | bytes 9224 | tf_op jit(solution)/shard_map/ppermute | solution.py:34
  (27 other events, 190.6 us)

commit v9 on v8

--- a/solution.py
+++ b/solution.py
@@ -47,8 +47,7 @@
         closed[x0 : x0 + DEG + 1, y0 : y0 + DEG + 1, z0 : z0 + DEG + 1]
         for x0, y0, z0 in cell_ranges()
     ]
-    stacked = jnp.stack(blocks, axis=3)
-    return stacked.reshape((DEG + 1) ** 3, len(blocks) * stacked.shape[-1])
+    return jnp.concatenate(blocks, axis=-1).reshape((DEG + 1) ** 3, -1)
 
 
 def scatter_cells(cell_out, columns):

time: 520 us -> 517 us (level)
    unnamed x76 -> x78, local copies, waits for them, and re-layouts: 19.1 us -> 19 us
where the time goes in v9:
time: 517 us; the launch traced here: 509 us
  waiting for transfers between devices  156 us (30%)
  matrix products  98.1 us (19%)
  blocking collectives  97.6 us (19%)
  local copies, waits for them, and re-layouts  83.9 us (16%)
  starting transfers between devices  49.5 us (10%)
  other arithmetic  15.9 us (3%)
  between operations  8.31 us (2%)
    all_to_all x5, waiting for transfers between devices, exchange(): lax.all_to_all(values, ('gx', 'gy'), split_axis=0, concat_axis=0, tiled=T...  111 us
    all_to_all x3, blocking collectives, exchange(): lax.all_to_all(values, ('gx', 'gy'), split_axis=0, concat_axis=0, tiled=T...  97.6 us
    dot_general x4, matrix products, apply_operator(): jnp.dot(tile_t, spread_in, precision=DENSE)  45.5 us
    dot_general x4, matrix products, apply_operator(): every_cell = jnp.dot(tile_all, cell_in, precision=DENSE)  31.6 us
    all_to_all x5, starting transfers between devices, exchange(): lax.all_to_all(values, ('gx', 'gy'), split_axis=0, concat_axis=0, tiled=T...  24.6 us
    ppermute x16, waiting for transfers between devices, shifted(): return lax.ppermute(value, axis, pairs)  24.5 us
    ppermute x8, waiting for transfers between devices, diagonal(): return lax.ppermute(value, ('gx', 'gy'), pairs)  20.6 us
    unnamed x78, local copies, waits for them, and re-layouts  19 us
  transfers between devices with their start and end apart: 29, of which 20 were waited for; matrix products, arithmetic and copies ran while one was open for 6% of the time, Pallas kernels for 0%

profile of v9, /device:TPU:0, one launch (start us, length us, event | category | flops | bytes accessed | tf_op | source)
XLA Modules:
  0.0 509.5 jit_solution(4893214978202495000)
XLA Ops:
  1.2 4.1 collective-permute-start
  5.3 4.6 collective-permute-start.2
  14.4 14.0 %copy.273 = f32[1,256,18,343]{3,2,1,0:T(8,128)} copy(f32[1,256,18,343]{1,0,3,2:T(1,128)} %param.36) | data formatting | bytes 12644352
  28.5 8.0 %pad.118.clone = f32[256,24,343]{2,1,0:T(8,128)} pad(f32[256,18,343]{2,1,0:T(8,128)} %bitcast.280, f32[]{:T(128)} %constant.278.clone.1), padding=0_0x0_6x0_0 | pad | bytes 14751748 | tf_op jit(solution)/shard_map/jit(_pad)/pad | solution.py:86
  37.0 8.0 %fusion.190 = f32[6144,256]{0,1:T(8,128)S(1)} fusion(f32[6144,343]{1,0:T(8,128)} %bitcast.272, f32[343,256]{1,0:T(8,128)S(1)} %reshape.508), kind=kOutput, calls=%fused_computation.346 | convolution fusion | flops 3236954112 | bytes 15072256 | tf_op jit(solution)/shard_map/dot_general | solution.py:120
  51.6 5.2 %all-to-all-start = ((f32[128,24,128]{2,1,0:T(8,128)}), f32[128,24,128]{2,1,0:T(8,128)S(1)}, u32[]{:S(2)}, u32[]{:S(2)}) async-start(f32[128,24,128]{2,1,0:T(8,128)} %pad_maximum_fusion.4), calls=%async_computation | async-start | bytes 3145728 | tf_op jit(solution)/shard_map/all_to_all | solution.py:94
  60.1 21.3 %all-to-all-done = f32[128,24,128]{2,1,0:T(8,128)S(1)} async-done(((f32[128,24,128]{2,1,0:T(8,128)}), f32[128,24,128]{2,1,0:T(8,128)S(1)}, u32[]{:S(2)}, u32[]{:S(2)}) %all-to-all-start) | async-done | bytes 1572896 | tf_op jit(solution)/shard_map/all_to_all | solution.py:94
  89.4 4.9 all-to-all-start.1
  99.6 19.4 %all-to-all-done.1 = f32[128,24,128]{2,1,0:T(8,128)S(1)} async-done(((f32[128,24,128]{2,1,0:T(8,128)}), f32[128,24,128]{2,1,0:T(8,128)S(1)}, u32[]{:S(2)}, u32[]{:S(2)}) %all-to-all-start.1) | async-done | bytes 1572896 | tf_op jit(solution)/shard_map/all_to_all | solution.py:94
  125.5 11.4 %fusion = f32[343,256]{1,0:T(8,128)S(1)} fusion(f32[6144,343]{1,0:T(8,128)} %bitcast.273, f32[6144,64]{0,1:T(8,128)S(1)} %get-tuple-element.190, f32[6144,64]{0,1:T(8,128)S(1)} %get-tuple-element.191, f32[6144,64]{0,1:T(8,128)S(1)} %get-tuple-element.192, f32[6144,64]{0,1:T(8,128)S(1)} %get-tuple-element.189), kind=kOutput, calls=%fused_computation | convolution fusion | flops 3241672704 | bytes 15072256 | tf_op jit(solution)/shard_map/dot_general | solution.py:132
  139.8 5.7 %collective-permute-done.3 = f32[12,12,64]{2,1,0:T(8,128)S(1)} collective-permute-done((f32[12,12,64]{2,1,0:T(8,128)S(1)}, f32[12,12,64]{2,1,0:T(8,128)S(1)}, u32[]{:S(2)}, u32[]{:S(2)}) %collective-permute-start.3) | collective-permute-done | bytes 36896 | tf_op jit(solution)/shard_map/ppermute | solution.py:23
  152.3 3.1 collective-permute-done.8
  155.8 7.9 %fusion.191 = f32[6144,256]{0,1:T(8,128)S(1)} fusion(f32[6144,343]{1,0:T(8,128)} %bitcast.274, f32[343,256]{1,0:T(8,128)S(1)} %reshape.517), kind=kOutput, calls=%fused_computation.347 | convolution fusion | flops 3236954112 | bytes 15072256 | tf_op jit(solution)/shard_map/dot_general | solution.py:120
  169.1 32.7 %all_to_all.40 = f32[128,24,128]{2,1,0:T(8,128)S(1)} all-to-all(f32[128,24,128]{2,1,0:T(8,128)S(1)} %pad_maximum_fusion.6), channel_id=1, replica_groups=mesh['gx'=16,'gy'=8] {'gx','gy'}, dimensions={0} | all-to-all | bytes 3145728 | tf_op jit(solution)/shard_map/all_to_all | solution.py:94
  209.0 4.8 all-to-all-start.3
  214.0 24.5 %all-to-all-done.3 = f32[128,24,128]{2,1,0:T(8,128)S(1)} async-done(((f32[128,24,128]{2,1,0:T(8,128)}), f32[128,24,128]{2,1,0:T(8,128)S(1)}, u32[]{:S(2)}, u32[]{:S(2)}) %all-to-all-start.3) | async-done | bytes 1572896 | tf_op jit(solution)/shard_map/all_to_all | solution.py:94
  244.2 11.4 %fusion.8 = f32[343,256]{1,0:T(8,128)S(1)} fusion(f32[6144,343]{1,0:T(8,128)} %bitcast.275, f32[6144,64]{0,1:T(8,128)S(1)} %get-tuple-element.182, f32[6144,64]{0,1:T(8,128)S(1)} %get-tuple-element.183, f32[6144,64]{0,1:T(8,128)S(1)} %get-tuple-element.184, f32[6144,64]{0,1:T(8,128)S(1)} %get-tuple-element.181), kind=kOutput, calls=%fused_computation.8 | convolution fusion | flops 3241672704 | bytes 15072256 | tf_op jit(solution)/shard_map/dot_general | solution.py:132
  258.5 5.7 %collective-permute-done.9 = f32[12,12,64]{2,1,0:T(8,128)S(1)} collective-permute-done((f32[12,12,64]{2,1,0:T(8,128)S(1)}, f32[12,12,64]{2,1,0:T(8,128)S(1)}, u32[]{:S(2)}, u32[]{:S(2)}) %collective-permute-start.9) | collective-permute-done | bytes 36896 | tf_op jit(solution)/shard_map/ppermute | solution.py:23
  271.1 3.1 collective-permute-done.14
  275.4 7.9 %fusion.192 = f32[6144,256]{0,1:T(8,128)S(1)} fusion(f32[6144,343]{1,0:T(8,128)} %bitcast.276, f32[343,256]{1,0:T(8,128)S(1)} %reshape.524), kind=kOutput, calls=%fused_computation.348 | convolution fusion | flops 3236954112 | bytes 15072256 | tf_op jit(solution)/shard_map/dot_general | solution.py:120
  288.7 32.2 %all_to_all.41 = f32[128,24,128]{2,1,0:T(8,128)S(1)} all-to-all(f32[128,24,128]{2,1,0:T(8,128)S(1)} %pad_maximum_fusion.8), channel_id=1, replica_groups=mesh['gx'=16,'gy'=8] {'gx','gy'}, dimensions={0} | all-to-all | bytes 3145728 | tf_op jit(solution)/shard_map/all_to_all | solution.py:94
  328.9 4.8 all-to-all-start.5
  336.9 21.5 %all-to-all-done.5 = f32[128,24,128]{2,1,0:T(8,128)S(1)} async-done(((f32[128,24,128]{2,1,0:T(8,128)}), f32[128,24,128]{2,1,0:T(8,128)S(1)}, u32[]{:S(2)}, u32[]{:S(2)}) %all-to-all-start.5) | async-done | bytes 1572896 | tf_op jit(solution)/shard_map/all_to_all | solution.py:94
  364.9 11.4 %fusion.16 = f32[343,256]{1,0:T(8,128)S(1)} fusion(f32[6144,343]{1,0:T(8,128)} %bitcast.277, f32[6144,64]{0,1:T(8,128)S(1)} %get-tuple-element.174, f32[6144,64]{0,1:T(8,128)S(1)} %get-tuple-element.175, f32[6144,64]{0,1:T(8,128)S(1)} %get-tuple-element.176, f32[6144,64]{0,1:T(8,128)S(1)} %get-tuple-element.173), kind=kOutput, calls=%fused_computation.16 | convolution fusion | flops 3241672704 | bytes 15072256 | tf_op jit(solution)/shard_map/dot_general | solution.py:132
  379.2 5.6 %collective-permute-done.15 = f32[12,12,64]{2,1,0:T(8,128)S(1)} collective-permute-done((f32[12,12,64]{2,1,0:T(8,128)S(1)}, f32[12,12,64]{2,1,0:T(8,128)S(1)}, u32[]{:S(2)}, u32[]{:S(2)}) %collective-permute-start.15) | collective-permute-done | bytes 36896 | tf_op jit(solution)/shard_map/ppermute | solution.py:23
  391.6 3.1 collective-permute-done.20
  395.9 7.9 %fusion.193 = f32[6144,256]{0,1:T(8,128)S(1)} fusion(f32[6144,343]{1,0:T(8,128)} %bitcast.278, f32[343,256]{1,0:T(8,128)S(1)} %reshape.531), kind=kOutput, calls=%fused_computation.349 | convolution fusion | flops 3236954112 | bytes 15072256 | tf_op jit(solution)/shard_map/dot_general | solution.py:120
  409.2 32.7 %all_to_all.42 = f32[128,24,128]{2,1,0:T(8,128)S(1)} all-to-all(f32[128,24,128]{2,1,0:T(8,128)S(1)} %pad_maximum_fusion.10), channel_id=1, replica_groups=mesh['gx'=16,'gy'=8] {'gx','gy'}, dimensions={0} | all-to-all | bytes 3145728 | tf_op jit(solution)/shard_map/all_to_all | solution.py:94
  449.6 4.8 all-to-all-start.7
  454.5 24.5 %all-to-all-done.7 = f32[128,24,128]{2,1,0:T(8,128)S(1)} async-done(((f32[128,24,128]{2,1,0:T(8,128)}), f32[128,24,128]{2,1,0:T(8,128)S(1)}, u32[]{:S(2)}, u32[]{:S(2)}) %all-to-all-start.7) | async-done | bytes 1572896 | tf_op jit(solution)/shard_map/all_to_all | solution.py:94
  484.8 11.4 %fusion.24 = f32[343,256]{1,0:T(8,128)S(1)} fusion(f32[6144,343]{1,0:T(8,128)} %bitcast.279, f32[6144,64]{0,1:T(8,128)S(1)} %get-tuple-element.166, f32[6144,64]{0,1:T(8,128)S(1)} %get-tuple-element.167, f32[6144,64]{0,1:T(8,128)S(1)} %get-tuple-element.168, f32[6144,64]{0,1:T(8,128)S(1)} %get-tuple-element.165), kind=kOutput, calls=%fused_computation.24 | convolution fusion | flops 3241672704 | bytes 15072256 | tf_op jit(solution)/shard_map/dot_general | solution.py:132
  499.1 5.7 %collective-permute-done.21 = f32[12,12,64]{2,1,0:T(8,128)S(1)} collective-permute-done((f32[12,12,64]{2,1,0:T(8,128)S(1)}, f32[12,12,64]{2,1,0:T(8,128)S(1)}, u32[]{:S(2)}, u32[]{:S(2)}) %collective-permute-start.21) | collective-permute-done | bytes 36896 | tf_op jit(solution)/shard_map/ppermute | solution.py:23
  (281 shorter events, 127.9 us)
Async XLA Ops:
  0.0 136.9 %copy-start = (f32[343,343]{1,0:T(8,128)S(1)}, f32[343,343]{1,0:T(8,128)}, u32[]{:S(2)}) copy-start(f32[343,343]{1,0:T(8,128)} %param.34) | copy-start | bytes 1411792
  1.2 147.6 %copy-start.1 = (f32[12,6,12,64]{3,2,1,0:T(8,128)}, f32[12,6,12,64]{3,2,1,0:T(8,128)S(1)}, u32[]{:S(2)}) copy-start(f32[12,6,12,64]{3,2,1,0:T(8,128)S(1)} %reshape.507) | copy-start | bytes 663556
  1.2 35.2 %collective-permute-start = (f32[12,1,12,64]{3,2,1,0:T(8,128)S(1)}, f32[12,1,12,64]{3,2,1,0:T(8,128)S(1)}, u32[]{:S(2)}, u32[]{:S(2)}) collective-permute-start(f32[12,1,12,64]{3,2,1,0:T(8,128)S(1)} %slice.920), channel_id=1, source_target_pairs={{0,7},{1,0},{2,1},{3,2},{4,3},{5,4},{6,5},{7,6},{8,15},{9,8},{10,9... | collective-permute-start | bytes 110600 | tf_op jit(solution)/shard_map/ppermute | solution.py:23
  5.3 31.2 %collective-permute-start.2 = (f32[1,1,12,64]{3,2,1,0:T(8,128)S(1)}, f32[1,1,12,64]{3,2,1,0:T(8,128)S(1)}, u32[]{:S(2)}, u32[]{:S(2)}) collective-permute-start(f32[1,1,12,64]{3,2,1,0:T(8,128)S(1)} %slice.922), channel_id=1, source_target_pairs={{0,127},{1,120},{2,121},{3,122},{4,123},{5,124},{6,125},{7,126},{8... | collective-permute-start | bytes 9224 | tf_op jit(solution)/shard_map/ppermute | solution.py:34
  11.0 25.5 %collective-permute-start.1 = (f32[1,6,12,64]{3,2,1,0:T(8,128)S(1)}, f32[1,6,12,64]{3,2,1,0:T(8,128)S(1)}, u32[]{:S(2)}, u32[]{:S(2)}) collective-permute-start(f32[1,6,12,64]{3,2,1,0:T(8,128)S(1)} %slice.776), channel_id=1, source_target_pairs={{0,120},{8,0},{16,8},{24,16},{32,24},{40,32},{48,40},{56,48},{64,5... | collective-permute-start | bytes 55304 | tf_op jit(solution)/shard_map/ppermute | solution.py:23
  14.4 30.6 %copy-start.13 = (f32[6144,1]{0,1:T(1,128)}, f32[6144,1]{0,1:T(1,128)S(1)}, u32[]{:S(2)}) copy-start(f32[6144,1]{0,1:T(1,128)S(1)} %get-tuple-element.216) | copy-start | bytes 73732
  51.6 29.9 %all-to-all-start = ((f32[128,24,128]{2,1,0:T(8,128)}), f32[128,24,128]{2,1,0:T(8,128)S(1)}, u32[]{:S(2)}, u32[]{:S(2)}) async-start(f32[128,24,128]{2,1,0:T(8,128)} %pad_maximum_fusion.4), calls=%async_computation | async-start | bytes 3145728 | tf_op jit(solution)/shard_map/all_to_all | solution.py:94
  89.4 29.6 %all-to-all-start.1 = ((f32[128,24,128]{2,1,0:T(8,128)}), f32[128,24,128]{2,1,0:T(8,128)S(1)}, u32[]{:S(2)}, u32[]{:S(2)}) async-start(f32[128,24,128]{2,1,0:T(8,128)} %copy.182), calls=%async_computation.1 | async-start | bytes 3145728 | tf_op jit(solution)/shard_map/all_to_all | solution.py:94
  138.6 6.9 %collective-permute-start.3 = (f32[12,12,64]{2,1,0:T(8,128)S(1)}, f32[12,12,64]{2,1,0:T(8,128)S(1)}, u32[]{:S(2)}, u32[]{:S(2)}) collective-permute-start(f32[12,12,64]{2,1,0:T(8,128)S(1)} %add_bitcast_fusion.3), channel_id=1, source_target_pairs={{0,1},{1,2},{2,3},{3,4},{4,5},{5,6},{6,7},{7,0},{8,9},{9,10},{10,1... | collective-permute-start | bytes 110600 | tf_op jit(solution)/shard_map/ppermute | solution.py:23
  138.8 7.2 %collective-permute-start.4 = (f32[6,12,64]{2,1,0:T(8,128)S(1)}, f32[6,12,64]{2,1,0:T(8,128)S(1)}, u32[]{:S(2)}, u32[]{:S(2)}) collective-permute-start(f32[6,12,64]{2,1,0:T(8,128)S(1)} %add_bitcast_fusion.7), channel_id=1, source_target_pairs={{0,8},{8,16},{16,24},{24,32},{32,40},{40,48},{48,56},{56,64},{64,7... | collective-permute-start | bytes 55304 | tf_op jit(solution)/shard_map/ppermute | solution.py:23
  138.8 9.9 %collective-permute-start.5 = (f32[12,64]{1,0:T(8,128)S(1)}, f32[12,64]{1,0:T(8,128)S(1)}, u32[]{:S(2)}, u32[]{:S(2)}) collective-permute-start(f32[12,64]{1,0:T(8,128)S(1)} %add_bitcast_fusion.11), channel_id=1, source_target_pairs={{0,9},{1,10},{2,11},{3,12},{4,13},{5,14},{6,15},{7,8},{8,17},{9,18... | collective-permute-start | bytes 9224 | tf_op jit(solution)/shard_map/ppermute | solution.py:34
  149.0 6.3 %collective-permute-start.6 = (f32[12,1,12,64]{3,2,1,0:T(8,128)S(1)}, f32[12,1,12,64]{3,2,1,0:T(8,128)S(1)}, u32[]{:S(2)}, u32[]{:S(2)}) collective-permute-start(f32[12,1,12,64]{3,2,1,0:T(8,128)S(1)} %slice.950), channel_id=1, source_target_pairs={{0,7},{1,0},{2,1},{3,2},{4,3},{5,4},{6,5},{7,6},{8,15},{9,8},{10,9... | collective-permute-start | bytes 110600 | tf_op jit(solution)/shard_map/ppermute | solution.py:23
  151.2 4.2 collective-permute-start.7
  152.3 3.1 collective-permute-start.8
  209.0 29.4 %all-to-all-start.3 = ((f32[128,24,128]{2,1,0:T(8,128)}), f32[128,24,128]{2,1,0:T(8,128)S(1)}, u32[]{:S(2)}, u32[]{:S(2)}) async-start(f32[128,24,128]{2,1,0:T(8,128)} %copy.200), calls=%async_computation.3 | async-start | bytes 3145728 | tf_op jit(solution)/shard_map/all_to_all | solution.py:94
  257.3 6.9 %collective-permute-start.9 = (f32[12,12,64]{2,1,0:T(8,128)S(1)}, f32[12,12,64]{2,1,0:T(8,128)S(1)}, u32[]{:S(2)}, u32[]{:S(2)}) collective-permute-start(f32[12,12,64]{2,1,0:T(8,128)S(1)} %add_bitcast_fusion.2), channel_id=1, source_target_pairs={{0,1},{1,2},{2,3},{3,4},{4,5},{5,6},{6,7},{7,0},{8,9},{9,10},{10,1... | collective-permute-start | bytes 110600 | tf_op jit(solution)/shard_map/ppermute | solution.py:23
  257.4 7.2 %collective-permute-start.10 = (f32[6,12,64]{2,1,0:T(8,128)S(1)}, f32[6,12,64]{2,1,0:T(8,128)S(1)}, u32[]{:S(2)}, u32[]{:S(2)}) collective-permute-start(f32[6,12,64]{2,1,0:T(8,128)S(1)} %add_bitcast_fusion.6), channel_id=1, source_target_pairs={{0,8},{8,16},{16,24},{24,32},{32,40},{40,48},{48,56},{56,64},{64,7... | collective-permute-start | bytes 55304 | tf_op jit(solution)/shard_map/ppermute | solution.py:23
  257.5 9.9 %collective-permute-start.11 = (f32[12,64]{1,0:T(8,128)S(1)}, f32[12,64]{1,0:T(8,128)S(1)}, u32[]{:S(2)}, u32[]{:S(2)}) collective-permute-start(f32[12,64]{1,0:T(8,128)S(1)} %add_bitcast_fusion.10), channel_id=1, source_target_pairs={{0,9},{1,10},{2,11},{3,12},{4,13},{5,14},{6,15},{7,8},{8,17},{9,18... | collective-permute-start | bytes 9224 | tf_op jit(solution)/shard_map/ppermute | solution.py:34
  267.7 6.5 %collective-permute-start.12 = (f32[12,1,12,64]{3,2,1,0:T(8,128)S(1)}, f32[12,1,12,64]{3,2,1,0:T(8,128)S(1)}, u32[]{:S(2)}, u32[]{:S(2)}) collective-permute-start(f32[12,1,12,64]{3,2,1,0:T(8,128)S(1)} %slice.974), channel_id=1, source_target_pairs={{0,7},{1,0},{2,1},{3,2},{4,3},{5,4},{6,5},{7,6},{8,15},{9,8},{10,9... | collective-permute-start | bytes 110600 | tf_op jit(solution)/shard_map/ppermute | solution.py:23
  270.0 4.2 collective-permute-start.13
  271.1 3.1 collective-permute-start.14
  328.9 29.4 %all-to-all-start.5 = ((f32[128,24,128]{2,1,0:T(8,128)}), f32[128,24,128]{2,1,0:T(8,128)S(1)}, u32[]{:S(2)}, u32[]{:S(2)}) async-start(f32[128,24,128]{2,1,0:T(8,128)} %copy.218), calls=%async_computation.5 | async-start | bytes 3145728 | tf_op jit(solution)/shard_map/all_to_all | solution.py:94
  378.0 6.9 %collective-permute-start.15 = (f32[12,12,64]{2,1,0:T(8,128)S(1)}, f32[12,12,64]{2,1,0:T(8,128)S(1)}, u32[]{:S(2)}, u32[]{:S(2)}) collective-permute-start(f32[12,12,64]{2,1,0:T(8,128)S(1)} %add_bitcast_fusion.1), channel_id=1, source_target_pairs={{0,1},{1,2},{2,3},{3,4},{4,5},{5,6},{6,7},{7,0},{8,9},{9,10},{10,1... | collective-permute-start | bytes 110600 | tf_op jit(solution)/shard_map/ppermute | solution.py:23
  378.2 7.2 %collective-permute-start.16 = (f32[6,12,64]{2,1,0:T(8,128)S(1)}, f32[6,12,64]{2,1,0:T(8,128)S(1)}, u32[]{:S(2)}, u32[]{:S(2)}) collective-permute-start(f32[6,12,64]{2,1,0:T(8,128)S(1)} %add_bitcast_fusion.5), channel_id=1, source_target_pairs={{0,8},{8,16},{16,24},{24,32},{32,40},{40,48},{48,56},{56,64},{64,7... | collective-permute-start | bytes 55304 | tf_op jit(solution)/shard_map/ppermute | solution.py:23
  378.3 10.1 %collective-permute-start.17 = (f32[12,64]{1,0:T(8,128)S(1)}, f32[12,64]{1,0:T(8,128)S(1)}, u32[]{:S(2)}, u32[]{:S(2)}) collective-permute-start(f32[12,64]{1,0:T(8,128)S(1)} %add_bitcast_fusion.9), channel_id=1, source_target_pairs={{0,9},{1,10},{2,11},{3,12},{4,13},{5,14},{6,15},{7,8},{8,17},{9,18... | collective-permute-start | bytes 9224 | tf_op jit(solution)/shard_map/ppermute | solution.py:34
  388.6 6.1 %collective-permute-start.18 = (f32[12,1,12,64]{3,2,1,0:T(8,128)S(1)}, f32[12,1,12,64]{3,2,1,0:T(8,128)S(1)}, u32[]{:S(2)}, u32[]{:S(2)}) collective-permute-start(f32[12,1,12,64]{3,2,1,0:T(8,128)S(1)} %slice.998), channel_id=1, source_target_pairs={{0,7},{1,0},{2,1},{3,2},{4,3},{5,4},{6,5},{7,6},{8,15},{9,8},{10,9... | collective-permute-start | bytes 110600 | tf_op jit(solution)/shard_map/ppermute | solution.py:23
  390.6 4.1 collective-permute-start.19
  391.6 3.1 collective-permute-start.20
  449.6 29.4 %all-to-all-start.7 = ((f32[128,24,128]{2,1,0:T(8,128)}), f32[128,24,128]{2,1,0:T(8,128)S(1)}, u32[]{:S(2)}, u32[]{:S(2)}) async-start(f32[128,24,128]{2,1,0:T(8,128)} %copy.236), calls=%async_computation.7 | async-start | bytes 3145728 | tf_op jit(solution)/shard_map/all_to_all | solution.py:94
  497.9 6.9 %collective-permute-start.21 = (f32[12,12,64]{2,1,0:T(8,128)S(1)}, f32[12,12,64]{2,1,0:T(8,128)S(1)}, u32[]{:S(2)}, u32[]{:S(2)}) collective-permute-start(f32[12,12,64]{2,1,0:T(8,128)S(1)} %add_bitcast_fusion), channel_id=1, source_target_pairs={{0,1},{1,2},{2,3},{3,4},{4,5},{5,6},{6,7},{7,0},{8,9},{9,10},{10,1... | collective-permute-start | bytes 110600 | tf_op jit(solution)/shard_map/ppermute | solution.py:23
  498.1 7.2 %collective-permute-start.22 = (f32[6,12,64]{2,1,0:T(8,128)S(1)}, f32[6,12,64]{2,1,0:T(8,128)S(1)}, u32[]{:S(2)}, u32[]{:S(2)}) collective-permute-start(f32[6,12,64]{2,1,0:T(8,128)S(1)} %add_bitcast_fusion.4), channel_id=1, source_target_pairs={{0,8},{8,16},{16,24},{24,32},{32,40},{40,48},{48,56},{56,64},{64,7... | collective-permute-start | bytes 55304 | tf_op jit(solution)/shard_map/ppermute | solution.py:23
  498.2 9.9 %collective-permute-start.23 = (f32[12,64]{1,0:T(8,128)S(1)}, f32[12,64]{1,0:T(8,128)S(1)}, u32[]{:S(2)}, u32[]{:S(2)}) collective-permute-start(f32[12,64]{1,0:T(8,128)S(1)} %add_bitcast_fusion.8), channel_id=1, source_target_pairs={{0,9},{1,10},{2,11},{3,12},{4,13},{5,14},{6,15},{7,8},{8,17},{9,18... | collective-permute-start | bytes 9224 | tf_op jit(solution)/shard_map/ppermute | solution.py:34
  (28 other events, 170.6 us)

commit v10 on v9

--- a/solution.py
+++ b/solution.py
@@ -51,12 +51,10 @@
 
 
 def scatter_cells(cell_out, columns):
-    cells = cell_out.shape[1] // columns
-    blocks = cell_out.reshape(DEG + 1, DEG + 1, DEG + 1, cells, columns)
     nx, ny = CX * DEG + 1, CY * DEG + 1
     total = None
     for index, (x0, y0, z0) in enumerate(cell_ranges()):
-        block = blocks[:, :, :, index]
+        block = cell_out[:, index * columns : (index + 1) * columns].reshape(DEG + 1, DEG + 1, DEG + 1, columns)
         spans = ((x0, nx - x0 - DEG - 1), (y0, ny - y0 - DEG - 1))
         if z0 + DEG < ZN:
             pieces = [jnp.pad(block, spans + ((z0, ZN - z0 - DEG - 1), (0, 0)))]

time: 517 us -> 514 us (level)
    unnamed x78 -> x66, local copies, waits for them, and re-layouts: 19 us -> 18.7 us
where the time goes in v10:
time: 514 us; the launch traced here: 506 us
  waiting for transfers between devices  156 us (30%)
  matrix products  98.1 us (19%)
  blocking collectives  95.9 us (19%)
  local copies, waits for them, and re-layouts  81.5 us (16%)
  starting transfers between devices  49.7 us (10%)
  other arithmetic  15.9 us (3%)
  between operations  8.54 us (2%)
    all_to_all x5, waiting for transfers between devices, exchange(): lax.all_to_all(values, ('gx', 'gy'), split_axis=0, concat_axis=0, tiled=T...  111 us
    all_to_all x3, blocking collectives, exchange(): lax.all_to_all(values, ('gx', 'gy'), split_axis=0, concat_axis=0, tiled=T...  95.9 us
    dot_general x4, matrix products, apply_operator(): jnp.dot(tile_t, spread_in, precision=DENSE)  45.5 us
    dot_general x4, matrix products, apply_operator(): every_cell = jnp.dot(tile_all, cell_in, precision=DENSE)  31.6 us
    all_to_all x5, starting transfers between devices, exchange(): lax.all_to_all(values, ('gx', 'gy'), split_axis=0, concat_axis=0, tiled=T...  24.7 us
    ppermute x16, waiting for transfers between devices, shifted(): return lax.ppermute(value, axis, pairs)  24.5 us
    ppermute x8, waiting for transfers between devices, diagonal(): return lax.ppermute(value, ('gx', 'gy'), pairs)  20.4 us
    unnamed x66, local copies, waits for them, and re-layouts  18.7 us
  transfers between devices with their start and end apart: 29, of which 20 were waited for; matrix products, arithmetic and copies ran while one was open for 6% of the time, Pallas kernels for 0%

profile of v10, /device:TPU:0, one launch (start us, length us, event | category | flops | bytes accessed | tf_op | source)
XLA Modules:
  0.0 505.7 jit_solution(17657014815089951264)
XLA Ops:
  1.2 4.1 collective-permute-start
  5.3 4.6 collective-permute-start.2
  14.4 14.0 %copy.194 = f32[1,256,18,343]{3,2,1,0:T(8,128)} copy(f32[1,256,18,343]{1,0,3,2:T(1,128)} %param.36) | data formatting | bytes 12644352
  28.4 8.0 %pad.118.clone = f32[256,24,343]{2,1,0:T(8,128)} pad(f32[256,18,343]{2,1,0:T(8,128)} %bitcast.236, f32[]{:T(128)} %constant.278.clone.1), padding=0_0x0_6x0_0 | pad | bytes 14751748 | tf_op jit(solution)/shard_map/jit(_pad)/pad | solution.py:84
  37.0 8.0 %fusion.190 = f32[6144,256]{0,1:T(8,128)S(1)} fusion(f32[6144,343]{1,0:T(8,128)} %bitcast.228, f32[343,256]{1,0:T(8,128)S(1)} %reshape.544), kind=kOutput, calls=%fused_computation.330 | convolution fusion | flops 3236954112 | bytes 15072256 | tf_op jit(solution)/shard_map/dot_general | solution.py:118
  51.6 5.0 all-to-all-start
  59.8 21.3 %all-to-all-done = f32[128,24,128]{2,1,0:T(8,128)S(1)} async-done(((f32[128,24,128]{2,1,0:T(8,128)}), f32[128,24,128]{2,1,0:T(8,128)S(1)}, u32[]{:S(2)}, u32[]{:S(2)}) %all-to-all-start) | async-done | bytes 1572896 | tf_op jit(solution)/shard_map/all_to_all | solution.py:92
  89.1 5.2 %all-to-all-start.1 = ((f32[128,24,128]{2,1,0:T(8,128)}), f32[128,24,128]{2,1,0:T(8,128)S(1)}, u32[]{:S(2)}, u32[]{:S(2)}) async-start(f32[128,24,128]{2,1,0:T(8,128)} %copy.135), calls=%async_computation.1 | async-start | bytes 3145728 | tf_op jit(solution)/shard_map/all_to_all | solution.py:92
  99.5 19.4 %all-to-all-done.1 = f32[128,24,128]{2,1,0:T(8,128)S(1)} async-done(((f32[128,24,128]{2,1,0:T(8,128)}), f32[128,24,128]{2,1,0:T(8,128)S(1)}, u32[]{:S(2)}, u32[]{:S(2)}) %all-to-all-start.1) | async-done | bytes 1572896 | tf_op jit(solution)/shard_map/all_to_all | solution.py:92
  125.5 11.4 %fusion = f32[343,256]{1,0:T(8,128)S(1)} fusion(f32[6144,343]{1,0:T(8,128)} %bitcast.229, f32[6144,64]{0,1:T(8,128)S(1)} %get-tuple-element.190, f32[6144,64]{0,1:T(8,128)S(1)} %get-tuple-element.191, f32[6144,64]{0,1:T(8,128)S(1)} %get-tuple-element.192, f32[6144,64]{0,1:T(8,128)S(1)} %get-tuple-element.189), kind=kOutput, calls=%fused_computation | convolution fusion | flops 3241672704 | bytes 15072256 | tf_op jit(solution)/shard_map/dot_general | solution.py:130
  139.2 5.7 %collective-permute-done.3 = f32[12,12,64]{2,1,0:T(8,128)S(1)} collective-permute-done((f32[12,12,64]{2,1,0:T(8,128)S(1)}, f32[12,12,64]{2,1,0:T(8,128)S(1)}, u32[]{:S(2)}, u32[]{:S(2)}) %collective-permute-start.3) | collective-permute-done | bytes 36896 | tf_op jit(solution)/shard_map/ppermute | solution.py:23
  151.6 3.1 collective-permute-done.8
  155.1 7.9 %fusion.191 = f32[6144,256]{0,1:T(8,128)S(1)} fusion(f32[6144,343]{1,0:T(8,128)} %bitcast.230, f32[343,256]{1,0:T(8,128)S(1)} %reshape.556), kind=kOutput, calls=%fused_computation.331 | convolution fusion | flops 3236954112 | bytes 15072256 | tf_op jit(solution)/shard_map/dot_general | solution.py:118
  168.5 32.1 %all_to_all.40 = f32[128,24,128]{2,1,0:T(8,128)S(1)} all-to-all(f32[128,24,128]{2,1,0:T(8,128)S(1)} %pad_maximum_fusion.6), channel_id=1, replica_groups=mesh['gx'=16,'gy'=8] {'gx','gy'}, dimensions={0} | all-to-all | bytes 3145728 | tf_op jit(solution)/shard_map/all_to_all | solution.py:92
  207.8 4.9 all-to-all-start.3
  212.8 24.5 %all-to-all-done.3 = f32[128,24,128]{2,1,0:T(8,128)S(1)} async-done(((f32[128,24,128]{2,1,0:T(8,128)}), f32[128,24,128]{2,1,0:T(8,128)S(1)}, u32[]{:S(2)}, u32[]{:S(2)}) %all-to-all-start.3) | async-done | bytes 1572896 | tf_op jit(solution)/shard_map/all_to_all | solution.py:92
  243.1 11.4 %fusion.8 = f32[343,256]{1,0:T(8,128)S(1)} fusion(f32[6144,343]{1,0:T(8,128)} %bitcast.231, f32[6144,64]{0,1:T(8,128)S(1)} %get-tuple-element.182, f32[6144,64]{0,1:T(8,128)S(1)} %get-tuple-element.183, f32[6144,64]{0,1:T(8,128)S(1)} %get-tuple-element.184, f32[6144,64]{0,1:T(8,128)S(1)} %get-tuple-element.181), kind=kOutput, calls=%fused_computation.8 | convolution fusion | flops 3241672704 | bytes 15072256 | tf_op jit(solution)/shard_map/dot_general | solution.py:130
  256.7 5.7 %collective-permute-done.9 = f32[12,12,64]{2,1,0:T(8,128)S(1)} collective-permute-done((f32[12,12,64]{2,1,0:T(8,128)S(1)}, f32[12,12,64]{2,1,0:T(8,128)S(1)}, u32[]{:S(2)}, u32[]{:S(2)}) %collective-permute-start.9) | collective-permute-done | bytes 36896 | tf_op jit(solution)/shard_map/ppermute | solution.py:23
  269.4 3.1 collective-permute-done.14
  273.7 7.9 %fusion.192 = f32[6144,256]{0,1:T(8,128)S(1)} fusion(f32[6144,343]{1,0:T(8,128)} %bitcast.232, f32[343,256]{1,0:T(8,128)S(1)} %reshape.566), kind=kOutput, calls=%fused_computation.332 | convolution fusion | flops 3236954112 | bytes 15072256 | tf_op jit(solution)/shard_map/dot_general | solution.py:118
  287.0 31.8 %all_to_all.41 = f32[128,24,128]{2,1,0:T(8,128)S(1)} all-to-all(f32[128,24,128]{2,1,0:T(8,128)S(1)} %pad_maximum_fusion.8), channel_id=1, replica_groups=mesh['gx'=16,'gy'=8] {'gx','gy'}, dimensions={0} | all-to-all | bytes 3145728 | tf_op jit(solution)/shard_map/all_to_all | solution.py:92
  326.8 4.8 all-to-all-start.5
  334.7 21.5 %all-to-all-done.5 = f32[128,24,128]{2,1,0:T(8,128)S(1)} async-done(((f32[128,24,128]{2,1,0:T(8,128)}), f32[128,24,128]{2,1,0:T(8,128)S(1)}, u32[]{:S(2)}, u32[]{:S(2)}) %all-to-all-start.5) | async-done | bytes 1572896 | tf_op jit(solution)/shard_map/all_to_all | solution.py:92
  362.8 11.4 %fusion.16 = f32[343,256]{1,0:T(8,128)S(1)} fusion(f32[6144,343]{1,0:T(8,128)} %bitcast.233, f32[6144,64]{0,1:T(8,128)S(1)} %get-tuple-element.174, f32[6144,64]{0,1:T(8,128)S(1)} %get-tuple-element.175, f32[6144,64]{0,1:T(8,128)S(1)} %get-tuple-element.176, f32[6144,64]{0,1:T(8,128)S(1)} %get-tuple-element.173), kind=kOutput, calls=%fused_computation.16 | convolution fusion | flops 3241672704 | bytes 15072256 | tf_op jit(solution)/shard_map/dot_general | solution.py:130
  376.4 5.7 %collective-permute-done.15 = f32[12,12,64]{2,1,0:T(8,128)S(1)} collective-permute-done((f32[12,12,64]{2,1,0:T(8,128)S(1)}, f32[12,12,64]{2,1,0:T(8,128)S(1)}, u32[]{:S(2)}, u32[]{:S(2)}) %collective-permute-start.15) | collective-permute-done | bytes 36896 | tf_op jit(solution)/shard_map/ppermute | solution.py:23
  388.9 3.1 collective-permute-done.20
  393.1 7.9 %fusion.193 = f32[6144,256]{0,1:T(8,128)S(1)} fusion(f32[6144,343]{1,0:T(8,128)} %bitcast.234, f32[343,256]{1,0:T(8,128)S(1)} %reshape.576), kind=kOutput, calls=%fused_computation.333 | convolution fusion | flops 3236954112 | bytes 15072256 | tf_op jit(solution)/shard_map/dot_general | solution.py:118
  406.5 32.0 %all_to_all.42 = f32[128,24,128]{2,1,0:T(8,128)S(1)} all-to-all(f32[128,24,128]{2,1,0:T(8,128)S(1)} %pad_maximum_fusion.10), channel_id=1, replica_groups=mesh['gx'=16,'gy'=8] {'gx','gy'}, dimensions={0} | all-to-all | bytes 3145728 | tf_op jit(solution)/shard_map/all_to_all | solution.py:92
  446.1 4.9 all-to-all-start.7
  451.2 24.5 %all-to-all-done.7 = f32[128,24,128]{2,1,0:T(8,128)S(1)} async-done(((f32[128,24,128]{2,1,0:T(8,128)}), f32[128,24,128]{2,1,0:T(8,128)S(1)}, u32[]{:S(2)}, u32[]{:S(2)}) %all-to-all-start.7) | async-done | bytes 1572896 | tf_op jit(solution)/shard_map/all_to_all | solution.py:92
  481.5 11.4 %fusion.24 = f32[343,256]{1,0:T(8,128)S(1)} fusion(f32[6144,343]{1,0:T(8,128)} %bitcast.235, f32[6144,64]{0,1:T(8,128)S(1)} %get-tuple-element.166, f32[6144,64]{0,1:T(8,128)S(1)} %get-tuple-element.167, f32[6144,64]{0,1:T(8,128)S(1)} %get-tuple-element.168, f32[6144,64]{0,1:T(8,128)S(1)} %get-tuple-element.165), kind=kOutput, calls=%fused_computation.24 | convolution fusion | flops 3241672704 | bytes 15072256 | tf_op jit(solution)/shard_map/dot_general | solution.py:130
  495.2 5.7 %collective-permute-done.21 = f32[12,12,64]{2,1,0:T(8,128)S(1)} collective-permute-done((f32[12,12,64]{2,1,0:T(8,128)S(1)}, f32[12,12,64]{2,1,0:T(8,128)S(1)}, u32[]{:S(2)}, u32[]{:S(2)}) %collective-permute-start.21) | collective-permute-done | bytes 36896 | tf_op jit(solution)/shard_map/ppermute | solution.py:23
  (279 shorter events, 125.5 us)
Async XLA Ops:
  0.0 136.9 %copy-start = (f32[343,343]{1,0:T(8,128)S(1)}, f32[343,343]{1,0:T(8,128)}, u32[]{:S(2)}) copy-start(f32[343,343]{1,0:T(8,128)} %param.34) | copy-start | bytes 1411792
  1.2 147.0 %copy-start.1 = (f32[12,6,12,64]{3,2,1,0:T(8,128)}, f32[12,6,12,64]{3,2,1,0:T(8,128)S(1)}, u32[]{:S(2)}) copy-start(f32[12,6,12,64]{3,2,1,0:T(8,128)S(1)} %reshape.543) | copy-start | bytes 663556
  1.2 35.2 %collective-permute-start = (f32[12,1,12,64]{3,2,1,0:T(8,128)S(1)}, f32[12,1,12,64]{3,2,1,0:T(8,128)S(1)}, u32[]{:S(2)}, u32[]{:S(2)}) collective-permute-start(f32[12,1,12,64]{3,2,1,0:T(8,128)S(1)} %slice.920), channel_id=1, source_target_pairs={{0,7},{1,0},{2,1},{3,2},{4,3},{5,4},{6,5},{7,6},{8,15},{9,8},{10,9... | collective-permute-start | bytes 110600 | tf_op jit(solution)/shard_map/ppermute | solution.py:23
  5.3 31.1 %collective-permute-start.2 = (f32[1,1,12,64]{3,2,1,0:T(8,128)S(1)}, f32[1,1,12,64]{3,2,1,0:T(8,128)S(1)}, u32[]{:S(2)}, u32[]{:S(2)}) collective-permute-start(f32[1,1,12,64]{3,2,1,0:T(8,128)S(1)} %slice.922), channel_id=1, source_target_pairs={{0,127},{1,120},{2,121},{3,122},{4,123},{5,124},{6,125},{7,126},{8... | collective-permute-start | bytes 9224 | tf_op jit(solution)/shard_map/ppermute | solution.py:34
  11.0 25.5 %collective-permute-start.1 = (f32[1,6,12,64]{3,2,1,0:T(8,128)S(1)}, f32[1,6,12,64]{3,2,1,0:T(8,128)S(1)}, u32[]{:S(2)}, u32[]{:S(2)}) collective-permute-start(f32[1,6,12,64]{3,2,1,0:T(8,128)S(1)} %slice.776), channel_id=1, source_target_pairs={{0,120},{8,0},{16,8},{24,16},{32,24},{40,32},{48,40},{56,48},{64,5... | collective-permute-start | bytes 55304 | tf_op jit(solution)/shard_map/ppermute | solution.py:23
  14.4 30.6 %copy-start.13 = (f32[6144,1]{0,1:T(1,128)}, f32[6144,1]{0,1:T(1,128)S(1)}, u32[]{:S(2)}) copy-start(f32[6144,1]{0,1:T(1,128)S(1)} %get-tuple-element.216) | copy-start | bytes 73732
  51.6 29.6 %all-to-all-start = ((f32[128,24,128]{2,1,0:T(8,128)}), f32[128,24,128]{2,1,0:T(8,128)S(1)}, u32[]{:S(2)}, u32[]{:S(2)}) async-start(f32[128,24,128]{2,1,0:T(8,128)} %pad_maximum_fusion.4), calls=%async_computation | async-start | bytes 3145728 | tf_op jit(solution)/shard_map/all_to_all | solution.py:92
  89.1 29.8 %all-to-all-start.1 = ((f32[128,24,128]{2,1,0:T(8,128)}), f32[128,24,128]{2,1,0:T(8,128)S(1)}, u32[]{:S(2)}, u32[]{:S(2)}) async-start(f32[128,24,128]{2,1,0:T(8,128)} %copy.135), calls=%async_computation.1 | async-start | bytes 3145728 | tf_op jit(solution)/shard_map/all_to_all | solution.py:92
  138.0 6.9 %collective-permute-start.3 = (f32[12,12,64]{2,1,0:T(8,128)S(1)}, f32[12,12,64]{2,1,0:T(8,128)S(1)}, u32[]{:S(2)}, u32[]{:S(2)}) collective-permute-start(f32[12,12,64]{2,1,0:T(8,128)S(1)} %add_bitcast_fusion.3), channel_id=1, source_target_pairs={{0,1},{1,2},{2,3},{3,4},{4,5},{5,6},{6,7},{7,0},{8,9},{9,10},{10,1... | collective-permute-start | bytes 110600 | tf_op jit(solution)/shard_map/ppermute | solution.py:23
  138.1 7.2 %collective-permute-start.4 = (f32[6,12,64]{2,1,0:T(8,128)S(1)}, f32[6,12,64]{2,1,0:T(8,128)S(1)}, u32[]{:S(2)}, u32[]{:S(2)}) collective-permute-start(f32[6,12,64]{2,1,0:T(8,128)S(1)} %add_bitcast_fusion.7), channel_id=1, source_target_pairs={{0,8},{8,16},{16,24},{24,32},{32,40},{40,48},{48,56},{56,64},{64,7... | collective-permute-start | bytes 55304 | tf_op jit(solution)/shard_map/ppermute | solution.py:23
  138.2 9.9 %collective-permute-start.5 = (f32[12,64]{1,0:T(8,128)S(1)}, f32[12,64]{1,0:T(8,128)S(1)}, u32[]{:S(2)}, u32[]{:S(2)}) collective-permute-start(f32[12,64]{1,0:T(8,128)S(1)} %add_bitcast_fusion.11), channel_id=1, source_target_pairs={{0,9},{1,10},{2,11},{3,12},{4,13},{5,14},{6,15},{7,8},{8,17},{9,18... | collective-permute-start | bytes 9224 | tf_op jit(solution)/shard_map/ppermute | solution.py:34
  148.4 6.2 %collective-permute-start.6 = (f32[12,1,12,64]{3,2,1,0:T(8,128)S(1)}, f32[12,1,12,64]{3,2,1,0:T(8,128)S(1)}, u32[]{:S(2)}, u32[]{:S(2)}) collective-permute-start(f32[12,1,12,64]{3,2,1,0:T(8,128)S(1)} %slice.950), channel_id=1, source_target_pairs={{0,7},{1,0},{2,1},{3,2},{4,3},{5,4},{6,5},{7,6},{8,15},{9,8},{10,9... | collective-permute-start | bytes 110600 | tf_op jit(solution)/shard_map/ppermute | solution.py:23
  150.3 4.3 collective-permute-start.7
  151.4 3.2 collective-permute-start.8
  207.8 29.5 %all-to-all-start.3 = ((f32[128,24,128]{2,1,0:T(8,128)}), f32[128,24,128]{2,1,0:T(8,128)S(1)}, u32[]{:S(2)}, u32[]{:S(2)}) async-start(f32[128,24,128]{2,1,0:T(8,128)} %copy.149), calls=%async_computation.3 | async-start | bytes 3145728 | tf_op jit(solution)/shard_map/all_to_all | solution.py:92
  255.5 6.9 %collective-permute-start.9 = (f32[12,12,64]{2,1,0:T(8,128)S(1)}, f32[12,12,64]{2,1,0:T(8,128)S(1)}, u32[]{:S(2)}, u32[]{:S(2)}) collective-permute-start(f32[12,12,64]{2,1,0:T(8,128)S(1)} %add_bitcast_fusion.2), channel_id=1, source_target_pairs={{0,1},{1,2},{2,3},{3,4},{4,5},{5,6},{6,7},{7,0},{8,9},{9,10},{10,1... | collective-permute-start | bytes 110600 | tf_op jit(solution)/shard_map/ppermute | solution.py:23
  255.6 7.2 %collective-permute-start.10 = (f32[6,12,64]{2,1,0:T(8,128)S(1)}, f32[6,12,64]{2,1,0:T(8,128)S(1)}, u32[]{:S(2)}, u32[]{:S(2)}) collective-permute-start(f32[6,12,64]{2,1,0:T(8,128)S(1)} %add_bitcast_fusion.6), channel_id=1, source_target_pairs={{0,8},{8,16},{16,24},{24,32},{32,40},{40,48},{48,56},{56,64},{64,7... | collective-permute-start | bytes 55304 | tf_op jit(solution)/shard_map/ppermute | solution.py:23
  255.7 9.9 %collective-permute-start.11 = (f32[12,64]{1,0:T(8,128)S(1)}, f32[12,64]{1,0:T(8,128)S(1)}, u32[]{:S(2)}, u32[]{:S(2)}) collective-permute-start(f32[12,64]{1,0:T(8,128)S(1)} %add_bitcast_fusion.10), channel_id=1, source_target_pairs={{0,9},{1,10},{2,11},{3,12},{4,13},{5,14},{6,15},{7,8},{8,17},{9,18... | collective-permute-start | bytes 9224 | tf_op jit(solution)/shard_map/ppermute | solution.py:34
  265.9 6.5 %collective-permute-start.12 = (f32[12,1,12,64]{3,2,1,0:T(8,128)S(1)}, f32[12,1,12,64]{3,2,1,0:T(8,128)S(1)}, u32[]{:S(2)}, u32[]{:S(2)}) collective-permute-start(f32[12,1,12,64]{3,2,1,0:T(8,128)S(1)} %slice.974), channel_id=1, source_target_pairs={{0,7},{1,0},{2,1},{3,2},{4,3},{5,4},{6,5},{7,6},{8,15},{9,8},{10,9... | collective-permute-start | bytes 110600 | tf_op jit(solution)/shard_map/ppermute | solution.py:23
  267.8 4.6 collective-permute-start.13
  268.9 3.5 collective-permute-start.14
  326.8 29.4 %all-to-all-start.5 = ((f32[128,24,128]{2,1,0:T(8,128)}), f32[128,24,128]{2,1,0:T(8,128)S(1)}, u32[]{:S(2)}, u32[]{:S(2)}) async-start(f32[128,24,128]{2,1,0:T(8,128)} %copy.163), calls=%async_computation.5 | async-start | bytes 3145728 | tf_op jit(solution)/shard_map/all_to_all | solution.py:92
  375.2 6.9 %collective-permute-start.15 = (f32[12,12,64]{2,1,0:T(8,128)S(1)}, f32[12,12,64]{2,1,0:T(8,128)S(1)}, u32[]{:S(2)}, u32[]{:S(2)}) collective-permute-start(f32[12,12,64]{2,1,0:T(8,128)S(1)} %add_bitcast_fusion.1), channel_id=1, source_target_pairs={{0,1},{1,2},{2,3},{3,4},{4,5},{5,6},{6,7},{7,0},{8,9},{9,10},{10,1... | collective-permute-start | bytes 110600 | tf_op jit(solution)/shard_map/ppermute | solution.py:23
  375.4 7.2 %collective-permute-start.16 = (f32[6,12,64]{2,1,0:T(8,128)S(1)}, f32[6,12,64]{2,1,0:T(8,128)S(1)}, u32[]{:S(2)}, u32[]{:S(2)}) collective-permute-start(f32[6,12,64]{2,1,0:T(8,128)S(1)} %add_bitcast_fusion.5), channel_id=1, source_target_pairs={{0,8},{8,16},{16,24},{24,32},{32,40},{40,48},{48,56},{56,64},{64,7... | collective-permute-start | bytes 55304 | tf_op jit(solution)/shard_map/ppermute | solution.py:23
  375.5 9.9 %collective-permute-start.17 = (f32[12,64]{1,0:T(8,128)S(1)}, f32[12,64]{1,0:T(8,128)S(1)}, u32[]{:S(2)}, u32[]{:S(2)}) collective-permute-start(f32[12,64]{1,0:T(8,128)S(1)} %add_bitcast_fusion.9), channel_id=1, source_target_pairs={{0,9},{1,10},{2,11},{3,12},{4,13},{5,14},{6,15},{7,8},{8,17},{9,18... | collective-permute-start | bytes 9224 | tf_op jit(solution)/shard_map/ppermute | solution.py:34
  385.7 6.3 %collective-permute-start.18 = (f32[12,1,12,64]{3,2,1,0:T(8,128)S(1)}, f32[12,1,12,64]{3,2,1,0:T(8,128)S(1)}, u32[]{:S(2)}, u32[]{:S(2)}) collective-permute-start(f32[12,1,12,64]{3,2,1,0:T(8,128)S(1)} %slice.998), channel_id=1, source_target_pairs={{0,7},{1,0},{2,1},{3,2},{4,3},{5,4},{6,5},{7,6},{8,15},{9,8},{10,9... | collective-permute-start | bytes 110600 | tf_op jit(solution)/shard_map/ppermute | solution.py:23
  387.6 4.4 collective-permute-start.19
  388.7 3.3 collective-permute-start.20
  446.1 29.5 %all-to-all-start.7 = ((f32[128,24,128]{2,1,0:T(8,128)}), f32[128,24,128]{2,1,0:T(8,128)S(1)}, u32[]{:S(2)}, u32[]{:S(2)}) async-start(f32[128,24,128]{2,1,0:T(8,128)} %copy.177), calls=%async_computation.7 | async-start | bytes 3145728 | tf_op jit(solution)/shard_map/all_to_all | solution.py:92
  494.0 6.9 %collective-permute-start.21 = (f32[12,12,64]{2,1,0:T(8,128)S(1)}, f32[12,12,64]{2,1,0:T(8,128)S(1)}, u32[]{:S(2)}, u32[]{:S(2)}) collective-permute-start(f32[12,12,64]{2,1,0:T(8,128)S(1)} %add_bitcast_fusion), channel_id=1, source_target_pairs={{0,1},{1,2},{2,3},{3,4},{4,5},{5,6},{6,7},{7,0},{8,9},{9,10},{10,1... | collective-permute-start | bytes 110600 | tf_op jit(solution)/shard_map/ppermute | solution.py:23
  494.1 7.2 %collective-permute-start.22 = (f32[6,12,64]{2,1,0:T(8,128)S(1)}, f32[6,12,64]{2,1,0:T(8,128)S(1)}, u32[]{:S(2)}, u32[]{:S(2)}) collective-permute-start(f32[6,12,64]{2,1,0:T(8,128)S(1)} %add_bitcast_fusion.4), channel_id=1, source_target_pairs={{0,8},{8,16},{16,24},{24,32},{32,40},{40,48},{48,56},{56,64},{64,7... | collective-permute-start | bytes 55304 | tf_op jit(solution)/shard_map/ppermute | solution.py:23
  494.2 9.9 %collective-permute-start.23 = (f32[12,64]{1,0:T(8,128)S(1)}, f32[12,64]{1,0:T(8,128)S(1)}, u32[]{:S(2)}, u32[]{:S(2)}) collective-permute-start(f32[12,64]{1,0:T(8,128)S(1)} %add_bitcast_fusion.8), channel_id=1, source_target_pairs={{0,9},{1,10},{2,11},{3,12},{4,13},{5,14},{6,15},{7,8},{8,17},{9,18... | collective-permute-start | bytes 9224 | tf_op jit(solution)/shard_map/ppermute | solution.py:34
  (28 other events, 170.6 us)

commit v11 on v10

--- a/solution.py
+++ b/solution.py
@@ -98,10 +98,8 @@
             part = full[:, :, k * W : (k + 1) * W]
             atom_sums = part if atom_sums is None else atom_sums + part
         applied = jnp.einsum("apq,aqw->apw", coupling_pad, atom_sums, precision=PRECISE)
-        return jnp.concatenate(
-            [jnp.einsum("sa,apw->spw", hot_k[k], applied, precision=PRECISE) for k in range(CAP)],
-            axis=-1,
-        )
+        answers = jnp.einsum("ska,apw->spkw", incoming, applied, precision=PRECISE)
+        return answers.reshape(owners, rows, CAP * W)
 
     def apply_operator(current):
         face_x = shifted(current[:1], "gx", -1)

time: 514 us -> 508 us (0.988)
  local copies, waits for them, and re-layouts: 81.5 us -> 72.7 us
  other arithmetic: 15.9 us -> 22.5 us
    another operation x8 -> x4, local copies, waits for them, and re-layouts: 10.1 us -> 1.97 us  [apply_operator(): jnp.stack([returned[:, :, k * W:(k + 1) * W] for k in range(CAP)], axis=1)]
    another operation x4, other arithmetic: 0.83 us -> 7.9 us  [apply_operator(): jnp.stack([returned[:, :, k * W:(k + 1) * W] for k in range(CAP)], axis=1)]
    reshape x0 -> x4, local copies, waits for them, and re-layouts: none -> 6.48 us  [owner_work(): return answers.reshape(owners, rows, CAP * W)]
    concatenate x4 -> x0, local copies, waits for them, and re-layouts: 6.42 us -> none  [owner_work(): jnp.concatenate([jnp.einsum('sa,apw->spw', hot_k[k], applied, precision=P...]
    unnamed x8 -> x0, matrix products: 5.43 us -> none
    unnamed x66 -> x58, local copies, waits for them, and re-layouts: 18.7 us -> 18.3 us
where the time goes in v11:
time: 508 us; the launch traced here: 500 us
  waiting for transfers between devices  155 us (31%)
  matrix products  96 us (19%)
  blocking collectives  96 us (19%)
  local copies, waits for them, and re-layouts  72.7 us (14%)
  starting transfers between devices  49.5 us (10%)
  other arithmetic  22.5 us (4%)
  between operations  8.62 us (2%)
    all_to_all x5, waiting for transfers between devices, exchange(): lax.all_to_all(values, ('gx', 'gy'), split_axis=0, concat_axis=0, tiled=T...  110 us
    all_to_all x3, blocking collectives, exchange(): lax.all_to_all(values, ('gx', 'gy'), split_axis=0, concat_axis=0, tiled=T...  96 us
    dot_general x4, matrix products, apply_operator(): jnp.dot(tile_t, spread_in, precision=DENSE)  45.5 us
    dot_general x4, matrix products, apply_operator(): every_cell = jnp.dot(tile_all, cell_in, precision=DENSE)  31.6 us
    all_to_all x5, starting transfers between devices, exchange(): lax.all_to_all(values, ('gx', 'gy'), split_axis=0, concat_axis=0, tiled=T...  24.6 us
    ppermute x16, waiting for transfers between devices, shifted(): return lax.ppermute(value, axis, pairs)  24.5 us
    ppermute x8, waiting for transfers between devices, diagonal(): return lax.ppermute(value, ('gx', 'gy'), pairs)  20.4 us
    unnamed x58, local copies, waits for them, and re-layouts  18.3 us
  transfers between devices with their start and end apart: 29, of which 20 were waited for; matrix products, arithmetic and copies ran while one was open for 6% of the time, Pallas kernels for 0%

profile of v11, /device:TPU:0, one launch (start us, length us, event | category | flops | bytes accessed | tf_op | source)
XLA Modules:
  0.0 500.3 jit_solution(14456117812019248469)
XLA Ops:
  1.2 4.1 collective-permute-start
  5.3 4.6 collective-permute-start.2
  14.4 14.1 %copy.192 = f32[1,256,18,343]{3,2,1,0:T(8,128)} copy(f32[1,256,18,343]{1,0,3,2:T(1,128)} %param.36) | data formatting | bytes 12644352
  28.5 8.0 %pad.118.clone = f32[256,24,343]{2,1,0:T(8,128)} pad(f32[256,18,343]{2,1,0:T(8,128)} %bitcast.227, f32[]{:T(128)} %constant.278.clone.1), padding=0_0x0_6x0_0 | pad | bytes 14751748 | tf_op jit(solution)/shard_map/jit(_pad)/pad | solution.py:84
  37.0 8.0 %fusion.162 = f32[6144,256]{0,1:T(8,128)S(1)} fusion(f32[6144,343]{1,0:T(8,128)} %bitcast.219, f32[343,256]{1,0:T(8,128)S(1)} %reshape.556), kind=kOutput, calls=%fused_computation.304 | convolution fusion | flops 3236954112 | bytes 15072256 | tf_op jit(solution)/shard_map/dot_general | solution.py:116
  51.6 5.0 all-to-all-start
  59.8 21.3 %all-to-all-done = f32[128,24,128]{2,1,0:T(8,128)S(1)} async-done(((f32[128,24,128]{2,1,0:T(8,128)}), f32[128,24,128]{2,1,0:T(8,128)S(1)}, u32[]{:S(2)}, u32[]{:S(2)}) %all-to-all-start) | async-done | bytes 1572896 | tf_op jit(solution)/shard_map/all_to_all | solution.py:92
  87.8 5.0 %all-to-all-start.1 = ((f32[128,24,128]{2,1,0:T(8,128)}), f32[128,24,128]{2,1,0:T(8,128)S(1)}, u32[]{:S(2)}, u32[]{:S(2)}) async-start(f32[128,24,128]{2,1,0:T(8,128)} %copy.124), calls=%async_computation.1 | async-start | bytes 3145728 | tf_op jit(solution)/shard_map/all_to_all | solution.py:92
  99.1 18.4 %all-to-all-done.1 = f32[128,24,128]{2,1,0:T(8,128)S(1)} async-done(((f32[128,24,128]{2,1,0:T(8,128)}), f32[128,24,128]{2,1,0:T(8,128)S(1)}, u32[]{:S(2)}, u32[]{:S(2)}) %all-to-all-start.1) | async-done | bytes 1572896 | tf_op jit(solution)/shard_map/all_to_all | solution.py:92
  123.8 11.4 %fusion = f32[343,256]{1,0:T(8,128)S(1)} fusion(f32[6144,343]{1,0:T(8,128)} %bitcast.220, f32[6144,64]{0,1:T(8,128)S(1)} %get-tuple-element.190, f32[6144,64]{0,1:T(8,128)S(1)} %get-tuple-element.191, f32[6144,64]{0,1:T(8,128)S(1)} %get-tuple-element.192, f32[6144,64]{0,1:T(8,128)S(1)} %get-tuple-element.189), kind=kOutput, calls=%fused_computation | convolution fusion | flops 3241672704 | bytes 15072256 | tf_op jit(solution)/shard_map/dot_general | solution.py:128
  137.5 5.7 %collective-permute-done.3 = f32[12,12,64]{2,1,0:T(8,128)S(1)} collective-permute-done((f32[12,12,64]{2,1,0:T(8,128)S(1)}, f32[12,12,64]{2,1,0:T(8,128)S(1)}, u32[]{:S(2)}, u32[]{:S(2)}) %collective-permute-start.3) | collective-permute-done | bytes 36896 | tf_op jit(solution)/shard_map/ppermute | solution.py:23
  149.9 3.1 collective-permute-done.8
  153.4 7.9 %fusion.163 = f32[6144,256]{0,1:T(8,128)S(1)} fusion(f32[6144,343]{1,0:T(8,128)} %bitcast.221, f32[343,256]{1,0:T(8,128)S(1)} %reshape.569), kind=kOutput, calls=%fused_computation.305 | convolution fusion | flops 3236954112 | bytes 15072256 | tf_op jit(solution)/shard_map/dot_general | solution.py:116
  166.7 32.1 %all_to_all.40 = f32[128,24,128]{2,1,0:T(8,128)S(1)} all-to-all(f32[128,24,128]{2,1,0:T(8,128)S(1)} %pad_maximum_fusion.5), channel_id=1, replica_groups=mesh['gx'=16,'gy'=8] {'gx','gy'}, dimensions={0} | all-to-all | bytes 3145728 | tf_op jit(solution)/shard_map/all_to_all | solution.py:92
  205.5 4.9 all-to-all-start.3
  210.5 24.5 %all-to-all-done.3 = f32[128,24,128]{2,1,0:T(8,128)S(1)} async-done(((f32[128,24,128]{2,1,0:T(8,128)}), f32[128,24,128]{2,1,0:T(8,128)S(1)}, u32[]{:S(2)}, u32[]{:S(2)}) %all-to-all-start.3) | async-done | bytes 1572896 | tf_op jit(solution)/shard_map/all_to_all | solution.py:92
  240.5 11.3 %fusion.8 = f32[343,256]{1,0:T(8,128)S(1)} fusion(f32[6144,343]{1,0:T(8,128)} %bitcast.222, f32[6144,64]{0,1:T(8,128)S(1)} %get-tuple-element.182, f32[6144,64]{0,1:T(8,128)S(1)} %get-tuple-element.183, f32[6144,64]{0,1:T(8,128)S(1)} %get-tuple-element.184, f32[6144,64]{0,1:T(8,128)S(1)} %get-tuple-element.181), kind=kOutput, calls=%fused_computation.8 | convolution fusion | flops 3241672704 | bytes 15072256 | tf_op jit(solution)/shard_map/dot_general | solution.py:128
  254.1 5.7 %collective-permute-done.9 = f32[12,12,64]{2,1,0:T(8,128)S(1)} collective-permute-done((f32[12,12,64]{2,1,0:T(8,128)S(1)}, f32[12,12,64]{2,1,0:T(8,128)S(1)}, u32[]{:S(2)}, u32[]{:S(2)}) %collective-permute-start.9) | collective-permute-done | bytes 36896 | tf_op jit(solution)/shard_map/ppermute | solution.py:23
  266.8 3.1 collective-permute-done.14
  271.0 7.9 %fusion.164 = f32[6144,256]{0,1:T(8,128)S(1)} fusion(f32[6144,343]{1,0:T(8,128)} %bitcast.223, f32[343,256]{1,0:T(8,128)S(1)} %reshape.580), kind=kOutput, calls=%fused_computation.306 | convolution fusion | flops 3236954112 | bytes 15072256 | tf_op jit(solution)/shard_map/dot_general | solution.py:116
  284.3 31.9 %all_to_all.41 = f32[128,24,128]{2,1,0:T(8,128)S(1)} all-to-all(f32[128,24,128]{2,1,0:T(8,128)S(1)} %pad_maximum_fusion.6), channel_id=1, replica_groups=mesh['gx'=16,'gy'=8] {'gx','gy'}, dimensions={0} | all-to-all | bytes 3145728 | tf_op jit(solution)/shard_map/all_to_all | solution.py:92
  322.8 4.8 all-to-all-start.5
  330.9 21.3 %all-to-all-done.5 = f32[128,24,128]{2,1,0:T(8,128)S(1)} async-done(((f32[128,24,128]{2,1,0:T(8,128)}), f32[128,24,128]{2,1,0:T(8,128)S(1)}, u32[]{:S(2)}, u32[]{:S(2)}) %all-to-all-start.5) | async-done | bytes 1572896 | tf_op jit(solution)/shard_map/all_to_all | solution.py:92
  358.6 11.4 %fusion.16 = f32[343,256]{1,0:T(8,128)S(1)} fusion(f32[6144,343]{1,0:T(8,128)} %bitcast.224, f32[6144,64]{0,1:T(8,128)S(1)} %get-tuple-element.174, f32[6144,64]{0,1:T(8,128)S(1)} %get-tuple-element.175, f32[6144,64]{0,1:T(8,128)S(1)} %get-tuple-element.176, f32[6144,64]{0,1:T(8,128)S(1)} %get-tuple-element.173), kind=kOutput, calls=%fused_computation.16 | convolution fusion | flops 3241672704 | bytes 15072256 | tf_op jit(solution)/shard_map/dot_general | solution.py:128
  372.2 5.7 %collective-permute-done.15 = f32[12,12,64]{2,1,0:T(8,128)S(1)} collective-permute-done((f32[12,12,64]{2,1,0:T(8,128)S(1)}, f32[12,12,64]{2,1,0:T(8,128)S(1)}, u32[]{:S(2)}, u32[]{:S(2)}) %collective-permute-start.15) | collective-permute-done | bytes 36896 | tf_op jit(solution)/shard_map/ppermute | solution.py:23
  384.7 3.1 collective-permute-done.20
  388.9 7.9 %fusion.165 = f32[6144,256]{0,1:T(8,128)S(1)} fusion(f32[6144,343]{1,0:T(8,128)} %bitcast.225, f32[343,256]{1,0:T(8,128)S(1)} %reshape.591), kind=kOutput, calls=%fused_computation.307 | convolution fusion | flops 3236954112 | bytes 15072256 | tf_op jit(solution)/shard_map/dot_general | solution.py:116
  402.2 32.0 %all_to_all.42 = f32[128,24,128]{2,1,0:T(8,128)S(1)} all-to-all(f32[128,24,128]{2,1,0:T(8,128)S(1)} %pad_maximum_fusion.7), channel_id=1, replica_groups=mesh['gx'=16,'gy'=8] {'gx','gy'}, dimensions={0} | all-to-all | bytes 3145728 | tf_op jit(solution)/shard_map/all_to_all | solution.py:92
  440.9 4.9 all-to-all-start.7
  446.0 24.5 %all-to-all-done.7 = f32[128,24,128]{2,1,0:T(8,128)S(1)} async-done(((f32[128,24,128]{2,1,0:T(8,128)}), f32[128,24,128]{2,1,0:T(8,128)S(1)}, u32[]{:S(2)}, u32[]{:S(2)}) %all-to-all-start.7) | async-done | bytes 1572896 | tf_op jit(solution)/shard_map/all_to_all | solution.py:92
  476.0 11.4 %fusion.24 = f32[343,256]{1,0:T(8,128)S(1)} fusion(f32[6144,343]{1,0:T(8,128)} %bitcast.226, f32[6144,64]{0,1:T(8,128)S(1)} %get-tuple-element.166, f32[6144,64]{0,1:T(8,128)S(1)} %get-tuple-element.167, f32[6144,64]{0,1:T(8,128)S(1)} %get-tuple-element.168, f32[6144,64]{0,1:T(8,128)S(1)} %get-tuple-element.165), kind=kOutput, calls=%fused_computation.24 | convolution fusion | flops 3241672704 | bytes 15072256 | tf_op jit(solution)/shard_map/dot_general | solution.py:128
  489.7 5.7 %collective-permute-done.21 = f32[12,12,64]{2,1,0:T(8,128)S(1)} collective-permute-done((f32[12,12,64]{2,1,0:T(8,128)S(1)}, f32[12,12,64]{2,1,0:T(8,128)S(1)}, u32[]{:S(2)}, u32[]{:S(2)}) %collective-permute-start.21) | collective-permute-done | bytes 36896 | tf_op jit(solution)/shard_map/ppermute | solution.py:23
  (255 shorter events, 121.2 us)
Async XLA Ops:
  0.0 135.2 %copy-start = (f32[343,343]{1,0:T(8,128)S(1)}, f32[343,343]{1,0:T(8,128)}, u32[]{:S(2)}) copy-start(f32[343,343]{1,0:T(8,128)} %param.34) | copy-start | bytes 1411792
  1.2 145.2 %copy-start.1 = (f32[12,6,12,64]{3,2,1,0:T(8,128)}, f32[12,6,12,64]{3,2,1,0:T(8,128)S(1)}, u32[]{:S(2)}) copy-start(f32[12,6,12,64]{3,2,1,0:T(8,128)S(1)} %reshape.555) | copy-start | bytes 663556
  1.2 35.2 %collective-permute-start = (f32[12,1,12,64]{3,2,1,0:T(8,128)S(1)}, f32[12,1,12,64]{3,2,1,0:T(8,128)S(1)}, u32[]{:S(2)}, u32[]{:S(2)}) collective-permute-start(f32[12,1,12,64]{3,2,1,0:T(8,128)S(1)} %slice.920), channel_id=1, source_target_pairs={{0,7},{1,0},{2,1},{3,2},{4,3},{5,4},{6,5},{7,6},{8,15},{9,8},{10,9... | collective-permute-start | bytes 110600 | tf_op jit(solution)/shard_map/ppermute | solution.py:23
  5.3 31.1 %collective-permute-start.2 = (f32[1,1,12,64]{3,2,1,0:T(8,128)S(1)}, f32[1,1,12,64]{3,2,1,0:T(8,128)S(1)}, u32[]{:S(2)}, u32[]{:S(2)}) collective-permute-start(f32[1,1,12,64]{3,2,1,0:T(8,128)S(1)} %slice.922), channel_id=1, source_target_pairs={{0,127},{1,120},{2,121},{3,122},{4,123},{5,124},{6,125},{7,126},{8... | collective-permute-start | bytes 9224 | tf_op jit(solution)/shard_map/ppermute | solution.py:34
  11.0 25.5 %collective-permute-start.1 = (f32[1,6,12,64]{3,2,1,0:T(8,128)S(1)}, f32[1,6,12,64]{3,2,1,0:T(8,128)S(1)}, u32[]{:S(2)}, u32[]{:S(2)}) collective-permute-start(f32[1,6,12,64]{3,2,1,0:T(8,128)S(1)} %slice.776), channel_id=1, source_target_pairs={{0,120},{8,0},{16,8},{24,16},{32,24},{40,32},{48,40},{56,48},{64,5... | collective-permute-start | bytes 55304 | tf_op jit(solution)/shard_map/ppermute | solution.py:23
  14.4 30.6 %copy-start.13 = (f32[6144,1]{0,1:T(1,128)}, f32[6144,1]{0,1:T(1,128)S(1)}, u32[]{:S(2)}) copy-start(f32[6144,1]{0,1:T(1,128)S(1)} %get-tuple-element.216) | copy-start | bytes 73732
  51.6 29.6 %all-to-all-start = ((f32[128,24,128]{2,1,0:T(8,128)}), f32[128,24,128]{2,1,0:T(8,128)S(1)}, u32[]{:S(2)}, u32[]{:S(2)}) async-start(f32[128,24,128]{2,1,0:T(8,128)} %pad_maximum_fusion.4), calls=%async_computation | async-start | bytes 3145728 | tf_op jit(solution)/shard_map/all_to_all | solution.py:92
  87.8 29.7 %all-to-all-start.1 = ((f32[128,24,128]{2,1,0:T(8,128)}), f32[128,24,128]{2,1,0:T(8,128)S(1)}, u32[]{:S(2)}, u32[]{:S(2)}) async-start(f32[128,24,128]{2,1,0:T(8,128)} %copy.124), calls=%async_computation.1 | async-start | bytes 3145728 | tf_op jit(solution)/shard_map/all_to_all | solution.py:92
  136.3 6.9 %collective-permute-start.3 = (f32[12,12,64]{2,1,0:T(8,128)S(1)}, f32[12,12,64]{2,1,0:T(8,128)S(1)}, u32[]{:S(2)}, u32[]{:S(2)}) collective-permute-start(f32[12,12,64]{2,1,0:T(8,128)S(1)} %add_bitcast_fusion.3), channel_id=1, source_target_pairs={{0,1},{1,2},{2,3},{3,4},{4,5},{5,6},{6,7},{7,0},{8,9},{9,10},{10,1... | collective-permute-start | bytes 110600 | tf_op jit(solution)/shard_map/ppermute | solution.py:23
  136.4 7.2 %collective-permute-start.4 = (f32[6,12,64]{2,1,0:T(8,128)S(1)}, f32[6,12,64]{2,1,0:T(8,128)S(1)}, u32[]{:S(2)}, u32[]{:S(2)}) collective-permute-start(f32[6,12,64]{2,1,0:T(8,128)S(1)} %add_bitcast_fusion.7), channel_id=1, source_target_pairs={{0,8},{8,16},{16,24},{24,32},{32,40},{40,48},{48,56},{56,64},{64,7... | collective-permute-start | bytes 55304 | tf_op jit(solution)/shard_map/ppermute | solution.py:23
  136.5 9.9 %collective-permute-start.5 = (f32[12,64]{1,0:T(8,128)S(1)}, f32[12,64]{1,0:T(8,128)S(1)}, u32[]{:S(2)}, u32[]{:S(2)}) collective-permute-start(f32[12,64]{1,0:T(8,128)S(1)} %add_bitcast_fusion.11), channel_id=1, source_target_pairs={{0,9},{1,10},{2,11},{3,12},{4,13},{5,14},{6,15},{7,8},{8,17},{9,18... | collective-permute-start | bytes 9224 | tf_op jit(solution)/shard_map/ppermute | solution.py:34
  146.7 6.2 %collective-permute-start.6 = (f32[12,1,12,64]{3,2,1,0:T(8,128)S(1)}, f32[12,1,12,64]{3,2,1,0:T(8,128)S(1)}, u32[]{:S(2)}, u32[]{:S(2)}) collective-permute-start(f32[12,1,12,64]{3,2,1,0:T(8,128)S(1)} %slice.950), channel_id=1, source_target_pairs={{0,7},{1,0},{2,1},{3,2},{4,3},{5,4},{6,5},{7,6},{8,15},{9,8},{10,9... | collective-permute-start | bytes 110600 | tf_op jit(solution)/shard_map/ppermute | solution.py:23
  148.6 4.3 collective-permute-start.7
  149.7 3.2 collective-permute-start.8
  205.5 29.5 %all-to-all-start.3 = ((f32[128,24,128]{2,1,0:T(8,128)}), f32[128,24,128]{2,1,0:T(8,128)S(1)}, u32[]{:S(2)}, u32[]{:S(2)}) async-start(f32[128,24,128]{2,1,0:T(8,128)} %copy.137), calls=%async_computation.3 | async-start | bytes 3145728 | tf_op jit(solution)/shard_map/all_to_all | solution.py:92
  252.9 6.9 %collective-permute-start.9 = (f32[12,12,64]{2,1,0:T(8,128)S(1)}, f32[12,12,64]{2,1,0:T(8,128)S(1)}, u32[]{:S(2)}, u32[]{:S(2)}) collective-permute-start(f32[12,12,64]{2,1,0:T(8,128)S(1)} %add_bitcast_fusion.2), channel_id=1, source_target_pairs={{0,1},{1,2},{2,3},{3,4},{4,5},{5,6},{6,7},{7,0},{8,9},{9,10},{10,1... | collective-permute-start | bytes 110600 | tf_op jit(solution)/shard_map/ppermute | solution.py:23
  253.1 7.2 %collective-permute-start.10 = (f32[6,12,64]{2,1,0:T(8,128)S(1)}, f32[6,12,64]{2,1,0:T(8,128)S(1)}, u32[]{:S(2)}, u32[]{:S(2)}) collective-permute-start(f32[6,12,64]{2,1,0:T(8,128)S(1)} %add_bitcast_fusion.6), channel_id=1, source_target_pairs={{0,8},{8,16},{16,24},{24,32},{32,40},{40,48},{48,56},{56,64},{64,7... | collective-permute-start | bytes 55304 | tf_op jit(solution)/shard_map/ppermute | solution.py:23
  253.2 9.9 %collective-permute-start.11 = (f32[12,64]{1,0:T(8,128)S(1)}, f32[12,64]{1,0:T(8,128)S(1)}, u32[]{:S(2)}, u32[]{:S(2)}) collective-permute-start(f32[12,64]{1,0:T(8,128)S(1)} %add_bitcast_fusion.10), channel_id=1, source_target_pairs={{0,9},{1,10},{2,11},{3,12},{4,13},{5,14},{6,15},{7,8},{8,17},{9,18... | collective-permute-start | bytes 9224 | tf_op jit(solution)/shard_map/ppermute | solution.py:34
  263.4 6.5 %collective-permute-start.12 = (f32[12,1,12,64]{3,2,1,0:T(8,128)S(1)}, f32[12,1,12,64]{3,2,1,0:T(8,128)S(1)}, u32[]{:S(2)}, u32[]{:S(2)}) collective-permute-start(f32[12,1,12,64]{3,2,1,0:T(8,128)S(1)} %slice.974), channel_id=1, source_target_pairs={{0,7},{1,0},{2,1},{3,2},{4,3},{5,4},{6,5},{7,6},{8,15},{9,8},{10,9... | collective-permute-start | bytes 110600 | tf_op jit(solution)/shard_map/ppermute | solution.py:23
  265.3 4.6 collective-permute-start.13
  266.4 3.5 collective-permute-start.14
  322.8 29.4 %all-to-all-start.5 = ((f32[128,24,128]{2,1,0:T(8,128)}), f32[128,24,128]{2,1,0:T(8,128)S(1)}, u32[]{:S(2)}, u32[]{:S(2)}) async-start(f32[128,24,128]{2,1,0:T(8,128)} %copy.150), calls=%async_computation.5 | async-start | bytes 3145728 | tf_op jit(solution)/shard_map/all_to_all | solution.py:92
  371.0 6.9 %collective-permute-start.15 = (f32[12,12,64]{2,1,0:T(8,128)S(1)}, f32[12,12,64]{2,1,0:T(8,128)S(1)}, u32[]{:S(2)}, u32[]{:S(2)}) collective-permute-start(f32[12,12,64]{2,1,0:T(8,128)S(1)} %add_bitcast_fusion.1), channel_id=1, source_target_pairs={{0,1},{1,2},{2,3},{3,4},{4,5},{5,6},{6,7},{7,0},{8,9},{9,10},{10,1... | collective-permute-start | bytes 110600 | tf_op jit(solution)/shard_map/ppermute | solution.py:23
  371.2 7.2 %collective-permute-start.16 = (f32[6,12,64]{2,1,0:T(8,128)S(1)}, f32[6,12,64]{2,1,0:T(8,128)S(1)}, u32[]{:S(2)}, u32[]{:S(2)}) collective-permute-start(f32[6,12,64]{2,1,0:T(8,128)S(1)} %add_bitcast_fusion.5), channel_id=1, source_target_pairs={{0,8},{8,16},{16,24},{24,32},{32,40},{40,48},{48,56},{56,64},{64,7... | collective-permute-start | bytes 55304 | tf_op jit(solution)/shard_map/ppermute | solution.py:23
  371.3 9.9 %collective-permute-start.17 = (f32[12,64]{1,0:T(8,128)S(1)}, f32[12,64]{1,0:T(8,128)S(1)}, u32[]{:S(2)}, u32[]{:S(2)}) collective-permute-start(f32[12,64]{1,0:T(8,128)S(1)} %add_bitcast_fusion.9), channel_id=1, source_target_pairs={{0,9},{1,10},{2,11},{3,12},{4,13},{5,14},{6,15},{7,8},{8,17},{9,18... | collective-permute-start | bytes 9224 | tf_op jit(solution)/shard_map/ppermute | solution.py:34
  381.5 6.3 %collective-permute-start.18 = (f32[12,1,12,64]{3,2,1,0:T(8,128)S(1)}, f32[12,1,12,64]{3,2,1,0:T(8,128)S(1)}, u32[]{:S(2)}, u32[]{:S(2)}) collective-permute-start(f32[12,1,12,64]{3,2,1,0:T(8,128)S(1)} %slice.998), channel_id=1, source_target_pairs={{0,7},{1,0},{2,1},{3,2},{4,3},{5,4},{6,5},{7,6},{8,15},{9,8},{10,9... | collective-permute-start | bytes 110600 | tf_op jit(solution)/shard_map/ppermute | solution.py:23
  383.4 4.4 collective-permute-start.19
  384.5 3.3 collective-permute-start.20
  440.9 29.5 %all-to-all-start.7 = ((f32[128,24,128]{2,1,0:T(8,128)}), f32[128,24,128]{2,1,0:T(8,128)S(1)}, u32[]{:S(2)}, u32[]{:S(2)}) async-start(f32[128,24,128]{2,1,0:T(8,128)} %copy.163), calls=%async_computation.7 | async-start | bytes 3145728 | tf_op jit(solution)/shard_map/all_to_all | solution.py:92
  488.5 6.9 %collective-permute-start.21 = (f32[12,12,64]{2,1,0:T(8,128)S(1)}, f32[12,12,64]{2,1,0:T(8,128)S(1)}, u32[]{:S(2)}, u32[]{:S(2)}) collective-permute-start(f32[12,12,64]{2,1,0:T(8,128)S(1)} %add_bitcast_fusion), channel_id=1, source_target_pairs={{0,1},{1,2},{2,3},{3,4},{4,5},{5,6},{6,7},{7,0},{8,9},{9,10},{10,1... | collective-permute-start | bytes 110600 | tf_op jit(solution)/shard_map/ppermute | solution.py:23
  488.6 7.2 %collective-permute-start.22 = (f32[6,12,64]{2,1,0:T(8,128)S(1)}, f32[6,12,64]{2,1,0:T(8,128)S(1)}, u32[]{:S(2)}, u32[]{:S(2)}) collective-permute-start(f32[6,12,64]{2,1,0:T(8,128)S(1)} %add_bitcast_fusion.4), channel_id=1, source_target_pairs={{0,8},{8,16},{16,24},{24,32},{32,40},{40,48},{48,56},{56,64},{64,7... | collective-permute-start | bytes 55304 | tf_op jit(solution)/shard_map/ppermute | solution.py:23
  488.7 9.9 %collective-permute-start.23 = (f32[12,64]{1,0:T(8,128)S(1)}, f32[12,64]{1,0:T(8,128)S(1)}, u32[]{:S(2)}, u32[]{:S(2)}) collective-permute-start(f32[12,64]{1,0:T(8,128)S(1)} %add_bitcast_fusion.8), channel_id=1, source_target_pairs={{0,9},{1,10},{2,11},{3,12},{4,13},{5,14},{6,15},{7,8},{8,17},{9,18... | collective-permute-start | bytes 9224 | tf_op jit(solution)/shard_map/ppermute | solution.py:34
  (24 other events, 162.1 us)
